TPU v7x, 32 devices: a whole 2x2x4 slice. The times are simulated.
32 devices in a mesh: grp: 4 (over y, x), dev: 8 (over z, core).
Axes of the slice: x: 2, y: 2, z: 4, core: 2. Of those that a mesh axis runs over, the one named last changes fastest.
Arguments:
- panel_nodes: float32 [3, 262144], P(None, ('grp', 'dev')), may hold values from -1.6 to 1.6, as said below
- density: float32 [262144], P(('grp', 'dev')), may hold values from -6 to 6
- crevice_routes: int32 [16384, 2], P(('grp', 'dev')), may hold values from 0 to 31, all different within a row; in each aligned block of 512 rows (0 to 511, 512 to 1023, ...) at most 64 rows name the same one
- crevice_centre: int32 [16384, 2], P(('grp', 'dev')), may hold values from 0 to 511
- centres: float32 [3, 16384], P(None, ('grp', 'dev')), may hold values from -0.3 to 0.3, as said below
- targets: float32 [3, 262144], P(None, ('grp', 'dev')), may hold values from -0.8 to 0.8, as said below
- centre_home: int32 [16384, 1], P(('grp', 'dev')), may hold values from 0 to 31; in each aligned block of 512 rows (0 to 511, 512 to 1023, ...) at most 32 rows name the same one
- upsample: float32 [64, 16], replicated, may hold values from 0 to 1, as said below
- fine_weights: float32 [64], replicated, may hold values from 0.005 to 0.05
Outputs:
- returned: float32 [524288], P(('grp', 'dev'))
Inputs may be any that keep to these rules, and one draw needn't show every extreme that they name: `crevice_routes`: each device's 512 panels name at most 64 (panel, route) pairs for any one owner device, and some owner reaches 64 in every draw; the 2 owners of one panel differ. `centre_home`: among the 512 centres of one device at most 32 have the same home, and that bound is reached in every draw; entries of returned with no centre are zero. `panel_nodes`: every point in the convex hull of one panel's nodes lies at distance 0.9 or more from the anchor; every panel node lies within 1.6 of the anchor. `centres`: every centre lies within 0.3 of the anchor. `targets`: each target node lies at distance 0.3 to 0.5 from its centre. `upsample`: entries are positive and each row sums to one.
All inputs are finite; a program needn't handle non-finite values.
Results may differ from a plain program's by a relative error of at most 0.0003.
Values sent between devices are 32-bit elements; how exact they have to be, the bound alone decides.
No kernel may reach another device: no remote copies, remote signals or barrier semaphores. Data moves between devices by JAX's collectives and lax.ppermute only.
A program may use at most 64 MiB of HBM per device.

v0:
```python
import math

import jax
import jax.numpy as jnp
from jax import lax
from jax.sharding import PartitionSpec as P

ORDER = 8


def route_rank(destination, count):
    onehot = (destination[:, None] == jnp.arange(count, dtype=jnp.int32)[None, :]).astype(jnp.int32)
    before = jnp.cumsum(onehot, axis=0) - onehot
    return jnp.sum(before * onehot, axis=1)


def refine(coarse_all, upsample, fine_weights):
    upper = jnp.einsum("sck,nk->scn", coarse_all, upsample, precision=lax.Precision.HIGHEST)
    strength = upper[:, 3, :] * fine_weights[None, :]
    return jnp.concatenate([upper[:, :3, :], strength[:, None, :]], axis=1)


def expansion_terms(sources, centre_pos, target_pos):
    src_vec = sources[:, :3, :] - centre_pos[:, :, None]
    tgt_vec = target_pos - centre_pos[:, :, None]
    src_dist = jnp.sqrt(jnp.sum(src_vec * src_vec, axis=1))
    tgt_dist = jnp.sqrt(jnp.sum(tgt_vec * tgt_vec, axis=1))
    inner = jnp.sum(src_vec[:, :, :, None] * tgt_vec[:, :, None, :], axis=1)
    cosine = inner / (src_dist[:, :, None] * tgt_dist[:, None, :])
    ratio = tgt_dist[:, None, :] / src_dist[:, :, None]
    p_prev = jnp.ones_like(cosine)
    p_now = cosine
    power = ratio
    total = 1.0 + ratio * cosine
    for level in range(1, ORDER):
        p_next = ((2 * level + 1) * cosine * p_now - level * p_prev) / (level + 1)
        power = power * ratio
        total = total + power * p_next
        p_prev, p_now = (p_now, p_next)
    kernel = total / src_dist[:, :, None]
    return jnp.sum(sources[:, 3, :, None] * kernel, axis=1)


def per_device(
    panel_nodes,
    density,
    crevice_routes,
    crevice_centre,
    centres,
    targets,
    centre_home,
    upsample,
    fine_weights,
):
    devices = lax.axis_size(("grp", "dev"))
    panels = crevice_routes.shape[0]
    fanout = crevice_routes.shape[1]
    centre_count = centres.shape[1]
    capacity = max(2, 2 * panels * fanout // devices)
    capacity_back = max(2, 2 * centre_count // devices)
    nodes = upsample.shape[1]
    coarse_all = jnp.concatenate(
        [
            panel_nodes.reshape(3, panels, nodes).transpose(1, 0, 2),
            density.reshape(panels, 1, nodes),
        ],
        axis=1,
    )
    payload = refine(coarse_all, upsample, fine_weights)
    per_row = payload.shape[2]
    payload = payload.reshape(panels, 4 * per_row)
    destination = crevice_routes.reshape(-1)
    slot_index = destination * capacity + route_rank(destination, devices)
    filler = jnp.concatenate(
        [jnp.full((3 * per_row,), 2.0, jnp.float32), jnp.zeros((per_row,), jnp.float32)]
    )
    slots = devices * capacity
    outgoing = (
        jnp.broadcast_to(filler[None, :], (slots, 4 * per_row))
        .at[slot_index]
        .set(jnp.repeat(payload, fanout, axis=0))
    )
    centre_slot = (
        jnp.full((slots,), float(centre_count), jnp.float32)
        .at[slot_index]
        .set(crevice_centre.reshape(-1).astype(jnp.float32))
    )
    incoming, incoming_ids = (
        lax.all_to_all(outgoing, ("grp", "dev"), split_axis=0, concat_axis=0, tiled=True),
        lax.all_to_all(centre_slot, ("grp", "dev"), split_axis=0, concat_axis=0, tiled=True),
    )
    incoming = incoming.reshape(slots, 4, per_row)
    centre_ids = incoming_ids.astype(jnp.int32)
    target_all = targets.reshape(3, centre_count, nodes)
    block = math.gcd(slots, 512)

    def one_block(pieces):
        sources, ids = pieces
        safe_ids = jnp.minimum(ids, centre_count - 1)
        centre_pos = centres[:, safe_ids].T
        target_pos = target_all[:, safe_ids, :].transpose(1, 0, 2)
        return expansion_terms(sources, centre_pos, target_pos)

    terms = lax.map(
        one_block,
        (
            incoming.reshape(slots // block, block, 4, incoming.shape[2]),
            centre_ids.reshape(slots // block, block),
        ),
    )
    potential = jax.ops.segment_sum(
        terms.reshape(slots, nodes), centre_ids, num_segments=centre_count + 1
    )[:centre_count]
    home = centre_home.reshape(-1)
    back_index = home * capacity_back + route_rank(home, devices)
    sending = jnp.zeros((devices * capacity_back, nodes), jnp.float32).at[back_index].set(potential)
    returned = lax.all_to_all(sending, ("grp", "dev"), split_axis=0, concat_axis=0, tiled=True)
    return returned.reshape(-1)


def solution(mesh):
    placed = (
        P(None, ("grp", "dev")),
        P(("grp", "dev")),
        P(("grp", "dev"), None),
        P(("grp", "dev"), None),
        P(None, ("grp", "dev")),
        P(None, ("grp", "dev")),
        P(("grp", "dev"), None),
        P(),
        P(),
    )
    return jax.shard_map(
        per_device, mesh=mesh, in_specs=placed, out_specs=P(("grp", "dev")), check_vma=False
    )
```

profile of v0, /device:TPU:0, one launch (start us, length us, event | category | flops | bytes accessed | tf_op | source)
XLA Modules:
  0.0 181.8 jit_solution(15754825237860678966)
XLA Ops:
  0.0 0.7 broadcast_multiply_fusion
  0.7 0.8 copy.145
  1.6 0.2 eq.62
  2.1 0.2 mul.328
  2.3 9.0 %reduce-window.16 = s32[32,8,128]{2,1,0:T(8,128)S(1)} reduce-window(s32[32,8,128]{2,1,0:T(8,128)S(1)} %fusion.32, s32[]{:T(128)} %copy.186), window={size=1x1x128 pad=0_0x0_0x127_0}, to_apply=%region_3.4 | reduce-window | flops 4161536 | bytes 262148 | tf_op jit(solution)/shard_map/reduce-window.2
  11.9 0.2 reshape.180
  12.2 4.3 %scatter_custom_fusion = f32[2048]{0:T(1024)S(1)} fusion(s32[1024]{0:T(1024)S(1)} %bitcast.84, f32[1024]{0:T(1024)S(1)} %reshape.180, f32[]{:T(128)} %constant.169.clone.1), kind=kCustom, calls=%fused_computation.71 | custom fusion | bytes 8196 | tf_op jit(solution)/shard_map/scatter | solution.py:86
  16.5 0.7 all_to_all.18
  17.2 7.3 %all-to-all-start = ((f32[32,64,1]{1,2,0:T(1,128)}), f32[32,64,1]{1,2,0:T(1,128)S(1)}, u32[]{:S(2)}, u32[]{:S(2)}) async-start(f32[32,64,1]{1,2,0:T(1,128)} %all_to_all.18), calls=%async_computation | async-start | bytes 32768 | tf_op jit(solution)/shard_map/all_to_all | solution.py:90
  24.7 0.3 reshape.153
  25.0 0.2 copy.150
  25.3 0.6 fusion.28
  26.1 0.2 copy.152
  26.3 0.4 broadcast_in_dim.23
  26.7 0.7 reshape.188
  27.4 1.5 broadcast_in_dim.22
  28.9 7.7 %scatter_fusion = f32[2048,256]{1,0:T(8,128)} fusion(f32[2048,256]{1,0:T(8,128)} %broadcast_in_dim.22, s32[1024]{0:T(1024)S(1)} %bitcast.85, f32[1024,256]{1,0:T(8,128)S(1)} %reshape.188), kind=kCustom, calls=%fused_computation.3 | custom fusion | bytes 3149824 | tf_op jit(solution)/shard_map/scatter | solution.py:81
  36.6 6.0 %all-to-all-start.1 = ((f32[32,64,256]{2,1,0:T(8,128)}), f32[32,64,256]{2,1,0:T(8,128)S(1)}, u32[]{:S(2)}, u32[]{:S(2)}) async-start(f32[32,64,256]{2,1,0:T(8,128)} %bitcast.17), calls=%async_computation.1 | async-start | bytes 4194304 | tf_op jit(solution)/shard_map/all_to_all | solution.py:89
  42.7 1.2 reduce-window.14
  43.8 0.2 slice_reduce_fusion
  44.1 0.3 reshape.157
  44.4 1.5 copy.155
  46.4 46.1 %all-to-all-done.1 = f32[32,64,256]{2,1,0:T(8,128)S(1)} async-done(((f32[32,64,256]{2,1,0:T(8,128)}), f32[32,64,256]{2,1,0:T(8,128)S(1)}, u32[]{:S(2)}, u32[]{:S(2)}) %all-to-all-start.1) | async-done | bytes 2097184 | tf_op jit(solution)/shard_map/all_to_all | solution.py:89
  92.5 3.1 %reshape.210 = f32[4,512,4,64]{3,2,1,0:T(4,128)} reshape(f32[32,64,256]{2,1,0:T(8,128)S(1)} %all-to-all-done.1) | data formatting | bytes 4194304 | tf_op jit(solution)/shard_map/reshape;reshape | solution.py:107
  95.6 4.8 %copy.154 = f32[4,512,4,64]{1,3,2,0:T(8,128)} copy(f32[4,512,4,64]{3,2,1,0:T(4,128)} %reshape.210) | data formatting | bytes 4194304 | tf_op jit(solution)/shard_map/while | solution.py:104
  100.4 53.7 %while.12 = (s32[]{:T(128)}, f32[4,512,16]{1,2,0:T(8,128)S(1)}, f32[4,512,4,64]{1,3,2,0:T(8,128)}, s32[4,512]{1,0:T(4,128)S(1)}, f32[3,512,16]{2,0,1:T(4,128)}, /*index=5*/f32[3,512]{0,1:T(8,128)S(1)}, s32[]{:T(128)}) while((s32[]{:T(128)}, f32[4,512,16]{1,2,0:T(8,128)S(1)}, f32[4,512,4,64]{1,3,2,0:T(8,128)}, s32[4,512]{1,0:T(4,128)S(1)}, ...), condition=%wide.region_13.14_spmd, body=%wide.region_8.13_spmd.sunk | while | flops 35974144 | bytes 8374369 | solution.py:104
  100.4 2.7 %gather_fusion = f32[512,3,16]{2,1,0:T(4,128)S(1)} fusion(f32[3,512,16]{2,0,1:T(4,128)} %get-tuple-element.221, s32[1024]{0:T(1024)S(1)} %pad_clamp_fusion.2), kind=kCustom, calls=%fused_computation.clone.1 | custom fusion | bytes 198656 | tf_op jit(solution)/shard_map/while/body/eval_jaxpr/gather | solution.py:101
  103.2 1.0 gather_fusion.1
  104.2 2.8 %multiply_reduce_fusion.8 = (f32[512,16]{1,0:T(8,128)S(1)}, f32[512,3,16]{2,1,0:T(4,128)S(1)}) fusion(f32[512,3,16]{2,1,0:T(4,128)S(1)} %gather_fusion, f32[512,3]{1,0:T(8,128)S(1)} %gather_fusion.1), kind=kLoop, calls=%fused_computation.31.clone.1 | loop fusion | flops 65536 | bytes 235520 | tf_op jit(solution)/shard_map/while/body/eval_jaxpr/reduce_sum | solution.py:27
  107.0 0.3 copy.175
  107.4 1.1 dynamic-slice_bitcast_fusion.2
  108.6 0.6 multiply_reduce_fusion.10
  109.3 4.4 %multiply_reduce_fusion.11 = f32[512,16]{0,1:T(8,128)S(1)} fusion(f32[512,64,16]{0,2,1:T(8,128)S(1)} %multiply_reduce_fusion.10, f32[512,64]{0,1:T(8,128)S(1)} %sqrt.22, f32[512,16]{0,1:T(8,128)S(1)} %sqrt.23, f32[512,64]{0,1:T(8,128)S(1)} %slice_bitcast_fusion.2), kind=kLoop, calls=%fused_computation.30.clone.1 | loop fusion | flops 33021952 | bytes 2424832 | tf_op jit(solution)/shard_map/while/body/eval_jaxpr/reduce_sum | solution.py:41
  113.9 2.7 %gather_fusion = f32[512,3,16]{2,1,0:T(4,128)S(1)} fusion(f32[3,512,16]{2,0,1:T(4,128)} %get-tuple-element.221, s32[1024]{0:T(1024)S(1)} %pad_clamp_fusion.2), kind=kCustom, calls=%fused_computation.clone.1 | custom fusion | bytes 198656 | tf_op jit(solution)/shard_map/while/body/eval_jaxpr/gather | solution.py:101
  116.6 1.0 gather_fusion.1
  117.6 2.8 %multiply_reduce_fusion.8 = (f32[512,16]{1,0:T(8,128)S(1)}, f32[512,3,16]{2,1,0:T(4,128)S(1)}) fusion(f32[512,3,16]{2,1,0:T(4,128)S(1)} %gather_fusion, f32[512,3]{1,0:T(8,128)S(1)} %gather_fusion.1), kind=kLoop, calls=%fused_computation.31.clone.1 | loop fusion | flops 65536 | bytes 235520 | tf_op jit(solution)/shard_map/while/body/eval_jaxpr/reduce_sum | solution.py:27
  120.5 0.3 copy.175
  120.8 1.1 dynamic-slice_bitcast_fusion.2
  122.0 0.6 multiply_reduce_fusion.10
  122.8 4.4 %multiply_reduce_fusion.11 = f32[512,16]{0,1:T(8,128)S(1)} fusion(f32[512,64,16]{0,2,1:T(8,128)S(1)} %multiply_reduce_fusion.10, f32[512,64]{0,1:T(8,128)S(1)} %sqrt.22, f32[512,16]{0,1:T(8,128)S(1)} %sqrt.23, f32[512,64]{0,1:T(8,128)S(1)} %slice_bitcast_fusion.2), kind=kLoop, calls=%fused_computation.30.clone.1 | loop fusion | flops 33021952 | bytes 2424832 | tf_op jit(solution)/shard_map/while/body/eval_jaxpr/reduce_sum | solution.py:41
  127.3 2.7 %gather_fusion = f32[512,3,16]{2,1,0:T(4,128)S(1)} fusion(f32[3,512,16]{2,0,1:T(4,128)} %get-tuple-element.221, s32[1024]{0:T(1024)S(1)} %pad_clamp_fusion.2), kind=kCustom, calls=%fused_computation.clone.1 | custom fusion | bytes 198656 | tf_op jit(solution)/shard_map/while/body/eval_jaxpr/gather | solution.py:101
  130.0 1.0 gather_fusion.1
  131.1 2.8 %multiply_reduce_fusion.8 = (f32[512,16]{1,0:T(8,128)S(1)}, f32[512,3,16]{2,1,0:T(4,128)S(1)}) fusion(f32[512,3,16]{2,1,0:T(4,128)S(1)} %gather_fusion, f32[512,3]{1,0:T(8,128)S(1)} %gather_fusion.1), kind=kLoop, calls=%fused_computation.31.clone.1 | loop fusion | flops 65536 | bytes 235520 | tf_op jit(solution)/shard_map/while/body/eval_jaxpr/reduce_sum | solution.py:27
  133.9 0.3 copy.175
  134.3 1.1 dynamic-slice_bitcast_fusion.2
  135.5 0.6 multiply_reduce_fusion.10
  136.2 4.4 %multiply_reduce_fusion.11 = f32[512,16]{0,1:T(8,128)S(1)} fusion(f32[512,64,16]{0,2,1:T(8,128)S(1)} %multiply_reduce_fusion.10, f32[512,64]{0,1:T(8,128)S(1)} %sqrt.22, f32[512,16]{0,1:T(8,128)S(1)} %sqrt.23, f32[512,64]{0,1:T(8,128)S(1)} %slice_bitcast_fusion.2), kind=kLoop, calls=%fused_computation.30.clone.1 | loop fusion | flops 33021952 | bytes 2424832 | tf_op jit(solution)/shard_map/while/body/eval_jaxpr/reduce_sum | solution.py:41
  140.7 2.7 %gather_fusion = f32[512,3,16]{2,1,0:T(4,128)S(1)} fusion(f32[3,512,16]{2,0,1:T(4,128)} %get-tuple-element.221, s32[1024]{0:T(1024)S(1)} %pad_clamp_fusion.2), kind=kCustom, calls=%fused_computation.clone.1 | custom fusion | bytes 198656 | tf_op jit(solution)/shard_map/while/body/eval_jaxpr/gather | solution.py:101
  143.5 1.0 gather_fusion.1
  144.5 2.8 %multiply_reduce_fusion.8 = (f32[512,16]{1,0:T(8,128)S(1)}, f32[512,3,16]{2,1,0:T(4,128)S(1)}) fusion(f32[512,3,16]{2,1,0:T(4,128)S(1)} %gather_fusion, f32[512,3]{1,0:T(8,128)S(1)} %gather_fusion.1), kind=kLoop, calls=%fused_computation.31.clone.1 | loop fusion | flops 65536 | bytes 235520 | tf_op jit(solution)/shard_map/while/body/eval_jaxpr/reduce_sum | solution.py:27
  147.3 0.3 copy.175
  147.7 1.1 dynamic-slice_bitcast_fusion.2
  148.9 0.6 multiply_reduce_fusion.10
  149.7 4.4 %multiply_reduce_fusion.11 = f32[512,16]{0,1:T(8,128)S(1)} fusion(f32[512,64,16]{0,2,1:T(8,128)S(1)} %multiply_reduce_fusion.10, f32[512,64]{0,1:T(8,128)S(1)} %sqrt.22, f32[512,16]{0,1:T(8,128)S(1)} %sqrt.23, f32[512,64]{0,1:T(8,128)S(1)} %slice_bitcast_fusion.2), kind=kLoop, calls=%fused_computation.30.clone.1 | loop fusion | flops 33021952 | bytes 2424832 | tf_op jit(solution)/shard_map/while/body/eval_jaxpr/reduce_sum | solution.py:41
  154.1 0.3 copy.164
  154.5 12.7 %scatter_custom_fusion.2 = f32[513,16]{1,0:T(8,128)S(1)} fusion(s32[2048]{0:T(1024)S(1)} %reshape.194, f32[2048,16]{1,0:T(8,128)S(1)} %bitcast.77, f32[]{:T(128)} %constant.165.clone.1), kind=kCustom, calls=%fused_computation.44 | custom fusion | flops 32768 | bytes 32836 | tf_op jit(solution)/shard_map/scatter-add | solution.py:111
  167.2 1.9 %scatter_custom_fusion.3 = f32[1024,16]{1,0:T(8,128)S(1)} fusion(s32[512]{0:T(512)S(1)} %bitcast.89, f32[513,16]{1,0:T(8,128)S(1)} %scatter_custom_fusion.2, f32[]{:T(128)} %constant.165.clone.1), kind=kCustom, calls=%fused_computation.41 | custom fusion | bytes 327684 | tf_op jit(solution)/shard_map/scatter | solution.py:116
  169.0 0.2 copy.160
  169.2 0.2 reshape.228
  169.4 9.9 %all_to_all.27 = f32[32,1,512]{2,1,0:T(1,128)S(1)} all-to-all(f32[32,1,512]{2,1,0:T(1,128)S(1)} %reshape.228), channel_id=1, replica_groups=mesh['grp'=4,'dev'=8] {'grp','dev'}, dimensions={0} | all-to-all | bytes 131072 | tf_op jit(solution)/shard_map/all_to_all | solution.py:117
  179.3 0.5 broadcast.282
  179.8 0.8 reduce.8
  180.7 0.2 copy.161
  180.9 0.8 reshape.159
  (85 shorter events, 3.5 us)
Async XLA Ops:
  0.0 25.3 %copy-start = (f32[64,16]{0,1:T(8,128)S(1)}, f32[64,16]{0,1:T(8,128)}, u32[]{:S(2)}) copy-start(f32[64,16]{0,1:T(8,128)} %param.18) | copy-start | bytes 12292
  0.0 11.7 %copy-start.6 = (s32[512,2]{0,1:T(2,128)S(1)}, s32[512,2]{0,1:T(2,128)}, u32[]{:S(2)}) copy-start(s32[512,2]{0,1:T(2,128)} %param.14) | copy-start | bytes 12292
  0.0 24.5 %copy-start.3 = (f32[8192]{0:T(1024)S(1)}, f32[8192]{0:T(1024)}, u32[]{:S(2)}) copy-start(f32[8192]{0:T(1024)} %param.12) | copy-start | bytes 98308
  0.0 24.7 %copy-start.1 = (f32[3,8192]{1,0:T(4,128)S(1)}, f32[3,8192]{1,0:T(4,128)}, u32[]{:S(2)}) copy-start(f32[3,8192]{1,0:T(4,128)} %param.11) | copy-start | bytes 294916
  12.1 13.9 %copy-start.8 = (f32[64]{0:T(128)S(1)}, f32[64]{0:T(128)}, u32[]{:S(2)}) copy-start(f32[64]{0:T(128)} %param.19) | copy-start | bytes 772
  17.2 19.4 %all-to-all-start = ((f32[32,64,1]{1,2,0:T(1,128)}), f32[32,64,1]{1,2,0:T(1,128)S(1)}, u32[]{:S(2)}, u32[]{:S(2)}) async-start(f32[32,64,1]{1,2,0:T(1,128)} %all_to_all.18), calls=%async_computation | async-start | bytes 32768 | tf_op jit(solution)/shard_map/all_to_all | solution.py:90
  26.1 1.3 copy-start.7
  36.6 6.0 %copy-start.4 = (s32[512,1]{0,1:T(1,128)S(1)}, s32[512,1]{0,1:T(1,128)}, u32[]{:S(2)}) copy-start(s32[512,1]{0,1:T(1,128)} %param.17) | copy-start | bytes 6148
  36.6 7.5 %copy-start.2 = (f32[3,8192]{1,0:T(4,128)S(1)}, f32[3,8192]{1,0:T(4,128)}, u32[]{:S(2)}) copy-start(f32[3,8192]{1,0:T(4,128)} %param.16) | copy-start | bytes 294916
  36.6 55.9 %all-to-all-start.1 = ((f32[32,64,256]{2,1,0:T(8,128)}), f32[32,64,256]{2,1,0:T(8,128)S(1)}, u32[]{:S(2)}, u32[]{:S(2)}) async-start(f32[32,64,256]{2,1,0:T(8,128)} %bitcast.17), calls=%async_computation.1 | async-start | bytes 4194304 | tf_op jit(solution)/shard_map/all_to_all | solution.py:89
  42.6 3.3 %copy-start.5 = (f32[3,512]{1,0:T(4,128)S(1)}, f32[3,512]{1,0:T(4,128)}, u32[]{:S(2)}) copy-start(f32[3,512]{1,0:T(4,128)} %param.15) | copy-start | bytes 18436
where the time goes:
time: 183 us; the launch traced here: 182 us
  other arithmetic  56.6 us (31%)
  local copies, waits for them, and re-layouts  54.4 us (30%)
  waiting for transfers between devices  46.1 us (25%)
  starting transfers between devices  13.3 us (7%)
  blocking collectives  9.89 us (5%)
    all_to_all x1, waiting for transfers between devices, per_device(): lax.all_to_all(outgoing, ('grp', 'dev'), split_axis=0, concat_axis=0, til...  46.1 us
    reduce_sum x4, other arithmetic, expansion_terms(): return jnp.sum(sources[:, 3, :, None] * kernel, axis=1)  17.8 us
    scatter-add x1, other arithmetic, per_device(): jax.ops.segment_sum(terms.reshape(slots, nodes), centre_ids, num_segments...  12.7 us
    reduce_sum x4, other arithmetic, expansion_terms(): tgt_dist = jnp.sqrt(jnp.sum(tgt_vec * tgt_vec, axis=1))  11.3 us
    gather x4, local copies, waits for them, and re-layouts, one_block(): target_pos = target_all[:, safe_ids, :].transpose(1, 0, 2)  10.9 us
    another operation x5, other arithmetic  10.3 us
    all_to_all x1, blocking collectives, per_device(): lax.all_to_all(sending, ('grp', 'dev'), split_axis=0, concat_axis=0, tile...  9.89 us
    scatter x1, local copies, waits for them, and re-layouts, per_device(): outgoing = jnp.broadcast_to(filler[None, :], (slots, 4 * per_row)).at[slo...  7.68 us
  transfers between devices with their start and end apart: 2, of which 1 were waited for; matrix products, arithmetic and copies ran while one was open for 9% of the time, Pallas kernels for 0%

commit v1 on v0

v1 whole, which is shorter than its diff:
```python
import jax
import jax.numpy as jnp
from jax import lax
from jax.sharding import PartitionSpec as P

ORDER = 8
HI = lax.Precision.HIGHEST


def route_rank(destination, count):
    rows = destination.shape[0]
    onehot = (destination[:, None] == jnp.arange(count, dtype=jnp.int32)[None, :]).astype(jnp.bfloat16)
    lower = (jnp.arange(rows)[:, None] > jnp.arange(rows)[None, :]).astype(jnp.bfloat16)
    before = jnp.dot(lower, onehot, preferred_element_type=jnp.float32)
    return jnp.sum(before * onehot.astype(jnp.float32), axis=1).astype(jnp.int32)


def expansion_terms(fine, strength, centre_pos, rel_targets):
    src = fine - centre_pos[:, None, :]
    rs2 = jnp.sum(src * src, axis=0)
    rt2 = jnp.sum(rel_targets * rel_targets, axis=0)
    inv_rs2 = 1.0 / rs2
    scale = strength * lax.rsqrt(rs2)
    inner = jnp.sum(src[:, :, None, :] * rel_targets[:, None, :, :], axis=0)
    w = inner * inv_rs2[:, None, :]
    rho2 = rt2[None, :, :] * inv_rs2[:, None, :]
    p_prev = jnp.ones_like(w)
    p_now = w
    total = 1.0 + w
    for level in range(1, ORDER):
        p_next = ((2 * level + 1) / (level + 1)) * w * p_now - (level / (level + 1)) * rho2 * p_prev
        total = total + p_next
        p_prev, p_now = (p_now, p_next)
    return jnp.sum(scale[:, None, :] * total, axis=0)


def per_device(
    panel_nodes,
    density,
    crevice_routes,
    crevice_centre,
    centres,
    targets,
    centre_home,
    upsample,
    fine_weights,
):
    devices = lax.axis_size(("grp", "dev"))
    panels = crevice_routes.shape[0]
    fanout = crevice_routes.shape[1]
    centre_count = centres.shape[1]
    capacity = max(2, 2 * panels * fanout // devices)
    capacity_back = max(2, 2 * centre_count // devices)
    fine_count, nodes = upsample.shape
    pairs = panels * fanout
    slots = devices * capacity

    coarse = jnp.concatenate(
        [panel_nodes.reshape(3, panels, nodes).transpose(0, 2, 1).reshape(3 * nodes, panels),
         density.reshape(panels, nodes).T],
        axis=0,
    )
    coarse_pairs = jnp.repeat(coarse, fanout, axis=1)
    ids_pairs = (crevice_centre.reshape(1, pairs) + 1).astype(jnp.float32)
    payload = jnp.concatenate([coarse_pairs, ids_pairs], axis=0)

    destination = crevice_routes.reshape(-1)
    slot_index = destination * capacity + route_rank(destination, devices)
    place = (slot_index[:, None] == jnp.arange(slots, dtype=jnp.int32)[None, :]).astype(jnp.float32)
    outgoing = jnp.dot(payload, place, precision=HI)

    incoming = lax.all_to_all(outgoing, ("grp", "dev"), split_axis=1, concat_axis=1, tiled=True)

    ids = jnp.round(incoming[4 * nodes]).astype(jnp.int32) - 1
    valid = ids >= 0
    pick = (ids[:, None] == jnp.arange(centre_count, dtype=jnp.int32)[None, :]).astype(jnp.float32)

    centre_pos = centres
    rel = targets.reshape(3, centre_count, nodes) - centre_pos[:, :, None]
    centre_data = jnp.concatenate([centre_pos, rel.transpose(0, 2, 1).reshape(3 * nodes, centre_count)], axis=0)
    gathered = lax.dot_general(centre_data, pick, (((1,), (1,)), ((), ())), precision=HI)
    slot_centre = gathered[:3]
    slot_targets = gathered[3:].reshape(3, nodes, slots)

    coarse_in = incoming[: 4 * nodes].reshape(4, nodes, slots)
    upper = jnp.einsum("jn,cns->cjs", upsample, coarse_in, precision=HI)
    strength = upper[3] * fine_weights[:, None]
    terms = expansion_terms(upper[:3], strength, slot_centre, slot_targets)
    terms = jnp.where(valid[None, :], terms, 0.0)

    potential = jnp.dot(terms, pick, precision=HI)

    home = centre_home.reshape(-1)
    back_index = home * capacity_back + route_rank(home, devices)
    back_place = (
        back_index[None, :] == jnp.arange(devices * capacity_back, dtype=jnp.int32)[:, None]
    ).astype(jnp.float32)
    sending = lax.dot_general(back_place, potential, (((1,), (1,)), ((), ())), precision=HI)
    sending = sending.reshape(devices, capacity_back * nodes)
    returned = lax.all_to_all(sending, ("grp", "dev"), split_axis=0, concat_axis=0, tiled=True)
    return returned.reshape(-1)


def solution(mesh):
    placed = (
        P(None, ("grp", "dev")),
        P(("grp", "dev")),
        P(("grp", "dev"), None),
        P(("grp", "dev"), None),
        P(None, ("grp", "dev")),
        P(None, ("grp", "dev")),
        P(("grp", "dev"), None),
        P(),
        P(),
    )
    return jax.shard_map(
        per_device, mesh=mesh, in_specs=placed, out_specs=P(("grp", "dev")), check_vma=False
    )
```

time: 183 us -> 91.4 us (0.50)
  local copies, waits for them, and re-layouts: 54.4 us -> 6.79 us
  other arithmetic: 56.6 us -> 25.4 us
  waiting for transfers between devices: 46.1 us -> 26.3 us
  matrix products: 0.63 us -> 15.4 us
  starting transfers between devices: 13.3 us -> 7.49 us
    all_to_all x2 -> x1, waiting for transfers between devices: 46.1 us -> 26.3 us  [per_device(): lax.all_to_all(outgoing, ('grp', 'dev'), split_axis=1, concat_axis=1, til...]
    gather x12 -> x0, local copies, waits for them, and re-layouts: 15.6 us -> none  [the longest x4 10.9 us: one_block(): target_pos = target_all[:, safe_ids, :].transpose(1, 0, 2)]
    scatter x3 -> x0, local copies, waits for them, and re-layouts: 13.8 us -> none  [the longest x1 7.68 us: per_device(): outgoing = jnp.broadcast_to(filler[None, :], (slots, 4 * per_row)).at[slo...]
    scatter-add x1 -> x0, other arithmetic: 12.7 us -> none  [per_device(): jax.ops.segment_sum(terms.reshape(slots, nodes), centre_ids, num_segments...]
    another operation x5 -> x0, other arithmetic: 10.3 us -> none
    reduce_sum x18 -> x4, other arithmetic: 31.8 us -> 23.3 us  [the longest x1 14.1 us: expansion_terms(): return jnp.sum(scale[:, None, :] * total, axis=0)]
    all_to_all x0 -> x1, matrix products: none -> 7.97 us  [per_device(): lax.all_to_all(outgoing, ('grp', 'dev'), split_axis=1, concat_axis=1, til...]
    dot_general x1 -> x6, matrix products: 0.63 us -> 7.4 us  [the longest x1 2.24 us: per_device(): lax.dot_general(centre_data, pick, (((1,), (1,)), ((), ())), precision=HI)]
  transfers between devices with their start and end apart: 2 -> 1, of which waited for: 1 -> 1; matrix products, arithmetic and copies ran while one was open for 9% -> 1% of each run, Pallas kernels for 0% -> 0%
where the time goes in v1:
time: 91.4 us; the launch traced here: 91 us
  waiting for transfers between devices  26.3 us (29%)
  other arithmetic  25.4 us (28%)
  matrix products  15.4 us (17%)
  blocking collectives  9.41 us (10%)
  starting transfers between devices  7.49 us (8%)
  local copies, waits for them, and re-layouts  6.79 us (7%)
    all_to_all x1, waiting for transfers between devices, per_device(): lax.all_to_all(outgoing, ('grp', 'dev'), split_axis=1, concat_axis=1, til...  26.3 us
    reduce_sum x1, other arithmetic, expansion_terms(): return jnp.sum(scale[:, None, :] * total, axis=0)  14.1 us
    all_to_all x1, blocking collectives, per_device(): lax.all_to_all(sending, ('grp', 'dev'), split_axis=0, concat_axis=0, tile...  9.41 us
    all_to_all x1, matrix products, per_device(): lax.all_to_all(outgoing, ('grp', 'dev'), split_axis=1, concat_axis=1, til...  7.97 us
    reduce_sum x1, other arithmetic, expansion_terms(): inner = jnp.sum(src[:, :, None, :] * rel_targets[:, None, :, :], axis=0)  7.67 us
    all_to_all x1, starting transfers between devices, per_device(): lax.all_to_all(outgoing, ('grp', 'dev'), split_axis=1, concat_axis=1, til...  7.49 us
    dot_general x1, matrix products, per_device(): lax.dot_general(centre_data, pick, (((1,), (1,)), ((), ())), precision=HI)  2.24 us
    dot_general x1, matrix products, per_device(): upper = jnp.einsum('jn,cns->cjs', upsample, coarse_in, precision=HI)  1.89 us
  transfers between devices with their start and end apart: 1, of which 1 were waited for; matrix products, arithmetic and copies ran while one was open for 1% of the time, Pallas kernels for 0%

profile of v1, /device:TPU:0, one launch (start us, length us, event | category | flops | bytes accessed | tf_op | source)
XLA Modules:
  0.0 91.0 jit_solution(11559862471947307797)
XLA Ops:
  0.0 0.0 copy-start
  0.0 0.0 copy-start.1
  0.0 0.0 copy-start.2
  0.0 0.0 copy-start.3
  0.0 0.7 add_convert_fusion
  0.7 0.1 copy.43
  0.9 0.2 convert_element_type.66
  1.1 0.9 reshape.130
  1.9 0.1 copy.41
  2.0 0.8 copy.45
  2.9 0.2 reshape.132
  3.1 0.5 fusion.26
  3.6 1.2 %reshape.128 = f32[3,512,16]{2,1,0:T(8,128)S(1)} reshape(f32[3,8192]{1,0:T(4,128)} %param.9) | data formatting | bytes 196608 | tf_op jit(solution)/shard_map/reshape | solution.py:59
  4.8 0.2 copy.40
  5.1 0.1 copy.42
  5.2 0.2 broadcast_in_dim.10
  5.4 8.0 %fusion.17 = f32[65,2048]{0,1:T(8,128)} fusion(s32[1024]{0:T(1024)S(1)} %convert_add_fusion, f32[1,1024]{0,1:T(8,128)S(1)} %convert_element_type.66, f32[64,1024]{0,1:T(8,128)S(1)} %bitcast.29), kind=kOutput, calls=%fused_computation.27 | convolution fusion | flops 1637942272 | bytes 802816 | tf_op jit(solution)/shard_map/all_to_all | solution.py:72
  13.4 7.5 %all-to-all-start = ((f32[65,32,64]{0,2,1:T(8,128)}), f32[65,32,64]{0,2,1:T(8,128)S(1)}, u32[]{:S(2)}, u32[]{:S(2)}) async-start(f32[65,32,64]{0,2,1:T(8,128)} %bitcast.5), calls=%async_computation | async-start | bytes 2097152 | tf_op jit(solution)/shard_map/all_to_all | solution.py:72
  20.9 0.0 copy-done.1
  20.9 0.3 reshape.134
  21.2 0.0 copy-done.2
  21.2 0.3 subtract_bitcast_fusion
  21.4 0.2 copy.48
  21.7 0.0 copy-done.3
  21.7 0.3 fusion.27
  22.0 26.3 %all-to-all-done = f32[65,32,64]{0,2,1:T(8,128)S(1)} async-done(((f32[65,32,64]{0,2,1:T(8,128)}), f32[65,32,64]{0,2,1:T(8,128)S(1)}, u32[]{:S(2)}, u32[]{:S(2)}) %all-to-all-start) | async-done | bytes 532512 | tf_op jit(solution)/shard_map/all_to_all | solution.py:72
  48.3 0.9 fusion.30
  49.2 0.1 sub.44
  49.3 2.2 %fusion.19 = f32[51,2048]{1,0:T(8,128)S(1)} fusion(s32[2048]{0:T(1024)S(1)} %sub.44, f32[48,512]{1,0:T(8,128)S(1)} %bitcast.33, f32[3,512]{1,0:T(4,128)S(1)} %copy-done.2), kind=kOutput, calls=%fused_computation.30 | convolution fusion | flops 642803200 | bytes 530432 | tf_op jit(solution)/shard_map/dot_general | solution.py:81
  51.6 0.9 %copy.47 = f32[64,32,64]{2,1,0:T(8,128)S(1)} copy(f32[64,32,64]{0,2,1:T(8,128)S(1)} %bitcast.25) | data formatting | bytes 1048576 | tf_op jit(solution)/shard_map/slice | solution.py:85
  52.5 0.4 reshape.133
  52.9 0.0 copy-done
  52.9 0.0 copy-start.4
  52.9 1.9 %convolution_bitcast_fusion = f32[4,64,2048]{2,1,0:T(8,128)S(1)} fusion(f32[4,16,2048]{2,1,0:T(8,128)S(1)} %reshape.133, f32[64,16]{0,1:T(8,128)S(1)} %copy-done), kind=kOutput, calls=%fused_computation.34 | convolution fusion | flops 100663296 | bytes 2625536 | tf_op jit(solution)/shard_map/jn,cns->cjs/dot_general | solution.py:86
  54.8 1.5 %multiply_reduce_fusion.1 = (f32[64,2048]{1,0:T(8,128)S(1)}, f32[3,64,2048]{2,1,0:T(8,128)}) fusion(f32[3,2048]{1,0:T(4,128)S(1)} %slice.30, f32[4,64,2048]{2,1,0:T(8,128)S(1)} %convolution_bitcast_fusion), kind=kLoop, calls=%fused_computation.40 | loop fusion | flops 1048576 | bytes 3694592 | tf_op jit(solution)/shard_map/reduce_sum | solution.py:20
  56.3 7.7 %multiply_reduce_fusion = f32[64,16,2048]{2,1,0:T(8,128)} fusion(f32[3,16,2048]{2,1,0:T(8,128)S(1)} %bitcast.27, f32[3,64,2048]{2,1,0:T(8,128)} %get-tuple-element.6), kind=kLoop, calls=%fused_computation.7 | loop fusion | flops 10485760 | bytes 10354688 | tf_op jit(solution)/shard_map/reduce_sum | solution.py:24
  64.0 0.0 copy-done.4
  64.0 0.2 fusion.33
  64.1 14.1 %fusion.15 = f32[16,2048]{1,0:T(8,128)S(1)} fusion(f32[64,16,2048]{2,1,0:T(8,128)} %multiply_reduce_fusion, f32[16,2048]{1,0:T(8,128)S(1)} %multiply_reduce_fusion.2, f32[64,2048]{1,0:T(8,128)S(1)} %get-tuple-element.8, f32[64,2048]{1,0:T(8,128)S(1)} %get-tuple-element.7), kind=kLoop, calls=%fused_computation.24 | loop fusion | flops 96436224 | bytes 9699328 | tf_op jit(solution)/shard_map/reduce_sum | solution.py:34
  78.2 1.4 %fusion.18 = f32[16,512]{1,0:T(8,128)S(1)} fusion(s32[2048]{0:T(1024)S(1)} %sub.44, f32[16,2048]{1,0:T(8,128)S(1)} %fusion.15, pred[2048]{0:T(1024)(128)(4,1)S(1)} %broadcast_compare_fusion), kind=kOutput, calls=%fused_computation.29 | convolution fusion | flops 202407936 | bytes 174080 | tf_op jit(solution)/shard_map/dot_general | solution.py:91
  79.7 1.0 %fusion.24 = f32[1024,16]{1,0:T(8,128)S(1)} fusion(f32[16,512]{1,0:T(8,128)S(1)} %fusion.18, s32[512]{0:T(512)S(1)} %convert_add_fusion.1), kind=kOutput, calls=%fused_computation.38 | convolution fusion | flops 101187584 | bytes 100352 | tf_op jit(solution)/shard_map/dot_general | solution.py:98
  80.7 0.2 all_to_all.16
  80.9 9.4 %all_to_all.19 = f32[32,1,512]{2,1,0:T(1,128)S(1)} all-to-all(f32[32,1,512]{2,1,0:T(1,128)S(1)} %all_to_all.16), channel_id=1, replica_groups=mesh['grp'=4,'dev'=8] {'grp','dev'}, dimensions={0} | all-to-all | bytes 131072 | tf_op jit(solution)/shard_map/all_to_all | solution.py:100
  90.3 0.6 copy.54
  (7 shorter events, 0.1 us)
Async XLA Ops:
  0.0 52.9 %copy-start = (f32[64,16]{0,1:T(8,128)S(1)}, f32[64,16]{0,1:T(8,128)}, u32[]{:S(2)}) copy-start(f32[64,16]{0,1:T(8,128)} %param.16) | copy-start | bytes 12292
  0.0 20.9 %copy-start.1 = (f32[3,8192]{1,0:T(4,128)S(1)}, f32[3,8192]{1,0:T(4,128)}, u32[]{:S(2)}) copy-start(f32[3,8192]{1,0:T(4,128)} %param.14) | copy-start | bytes 294916
  0.0 21.1 %copy-start.2 = (f32[3,512]{1,0:T(4,128)S(1)}, f32[3,512]{1,0:T(4,128)}, u32[]{:S(2)}) copy-start(f32[3,512]{1,0:T(4,128)} %param.13) | copy-start | bytes 18436
  0.0 21.7 %copy-start.3 = (s32[512,1]{0,1:T(1,128)S(1)}, s32[512,1]{0,1:T(1,128)}, u32[]{:S(2)}) copy-start(s32[512,1]{0,1:T(1,128)} %param.15) | copy-start | bytes 6148
  13.4 34.9 %all-to-all-start = ((f32[65,32,64]{0,2,1:T(8,128)}), f32[65,32,64]{0,2,1:T(8,128)S(1)}, u32[]{:S(2)}, u32[]{:S(2)}) async-start(f32[65,32,64]{0,2,1:T(8,128)} %bitcast.5), calls=%async_computation | async-start | bytes 2097152 | tf_op jit(solution)/shard_map/all_to_all | solution.py:72
  52.9 11.1 %copy-start.4 = (f32[64]{0:T(128)S(1)}, f32[64]{0:T(128)}, u32[]{:S(2)}) copy-start(f32[64]{0:T(128)} %param.17) | copy-start | bytes 772

commit v2 on v1

v2 whole, which is shorter than its diff:
```python
import jax
import jax.numpy as jnp
from jax import lax
from jax.sharding import PartitionSpec as P

ORDER = 8
HI = lax.Precision.HIGHEST
BF = jnp.bfloat16
F32 = jnp.float32


def route_rank(destination, count):
    rows = destination.shape[0]
    onehot = (destination[:, None] == jnp.arange(count, dtype=jnp.int32)[None, :]).astype(BF)
    lower = (jnp.arange(rows)[:, None] > jnp.arange(rows)[None, :]).astype(BF)
    before = jnp.dot(lower, onehot, preferred_element_type=F32)
    return jnp.sum(before * onehot.astype(F32), axis=1).astype(jnp.int32)


def split3(x, axis):
    hi = lax.reduce_precision(x, exponent_bits=8, mantissa_bits=7)
    rest = x - hi
    mid = lax.reduce_precision(rest, exponent_bits=8, mantissa_bits=7)
    lo = rest - mid
    return jnp.concatenate([hi, mid, lo], axis=axis).astype(BF)


def join3(y, axis):
    a, b, c = jnp.split(y, 3, axis=axis)
    return (a + b) + c


def expansion_terms(fine, strength, centre_pos, rel_targets):
    ax = fine[0] - centre_pos[0][None, :]
    ay = fine[1] - centre_pos[1][None, :]
    az = fine[2] - centre_pos[2][None, :]
    bx, by, bz = rel_targets[0], rel_targets[1], rel_targets[2]
    rs2 = ax * ax + ay * ay + az * az
    rt2 = bx * bx + by * by + bz * bz
    inv_rs2 = 1.0 / rs2
    scale = strength * lax.rsqrt(rs2)
    ax = ax * inv_rs2
    ay = ay * inv_rs2
    az = az * inv_rs2
    w = ax[:, None, :] * bx[None] + ay[:, None, :] * by[None] + az[:, None, :] * bz[None]
    rho2 = rt2[None, :, :] * inv_rs2[:, None, :]
    p_prev = jnp.ones_like(w)
    p_now = w
    total = 1.0 + w
    for level in range(1, ORDER):
        p_next = ((2 * level + 1) / (level + 1)) * w * p_now - (level / (level + 1)) * rho2 * p_prev
        total = total + p_next
        p_prev, p_now = (p_now, p_next)
    return jnp.sum(scale[:, None, :] * total, axis=0)


def per_device(
    panel_nodes,
    density,
    crevice_routes,
    crevice_centre,
    centres,
    targets,
    centre_home,
    upsample,
    fine_weights,
):
    devices = lax.axis_size(("grp", "dev"))
    panels = crevice_routes.shape[0]
    fanout = crevice_routes.shape[1]
    centre_count = centres.shape[1]
    capacity = max(2, 2 * panels * fanout // devices)
    capacity_back = max(2, 2 * centre_count // devices)
    fine_count, nodes = upsample.shape
    pairs = panels * fanout
    slots = devices * capacity
    width = 4 * nodes

    coarse = jnp.concatenate(
        [panel_nodes.reshape(3, panels, nodes).transpose(1, 0, 2).reshape(panels, 3 * nodes),
         density.reshape(panels, nodes)],
        axis=1,
    )
    coarse_pairs = jnp.broadcast_to(coarse[:, None, :], (panels, fanout, width)).reshape(pairs, width)
    ids1 = crevice_centre.reshape(pairs) + 1
    id_parts = jnp.stack([ids1 // 16, ids1 % 16], axis=1).astype(BF)
    rhs = jnp.concatenate([split3(coarse_pairs, 1), id_parts], axis=1)

    destination = crevice_routes.reshape(-1)
    slot_index = destination * capacity + route_rank(destination, devices)
    place = (jnp.arange(slots, dtype=jnp.int32)[:, None] == slot_index[None, :]).astype(BF)
    placed = jnp.dot(place, rhs, preferred_element_type=F32)
    payload = join3(placed[:, : 3 * width], 1)
    slot_ids = 16.0 * placed[:, 3 * width] + placed[:, 3 * width + 1]
    outgoing = jnp.concatenate(
        [payload.reshape(devices, capacity * width), slot_ids.reshape(devices, capacity)], axis=1
    )

    incoming = lax.all_to_all(outgoing, ("grp", "dev"), split_axis=0, concat_axis=0, tiled=True)

    coarse_in = incoming[:, : capacity * width].reshape(slots, width)
    ids = jnp.round(incoming[:, capacity * width :]).astype(jnp.int32).reshape(slots) - 1
    valid = ids >= 0
    pick = (jnp.arange(centre_count, dtype=jnp.int32)[:, None] == ids[None, :]).astype(BF)

    rel = targets.reshape(3, centre_count, nodes) - centres[:, :, None]
    centre_data = jnp.concatenate(
        [centres, rel.transpose(0, 2, 1).reshape(3 * nodes, centre_count)], axis=0
    )
    gathered = join3(jnp.dot(split3(centre_data, 0), pick, preferred_element_type=F32), 0)
    slot_centre = gathered[:3]
    slot_targets = gathered[3:].reshape(3, nodes, slots)

    upper = jnp.einsum(
        "jn,scn->cjs", upsample, coarse_in.reshape(slots, 4, nodes), precision=HI
    )
    strength = upper[3] * fine_weights[:, None]
    terms = expansion_terms(upper[:3], strength, slot_centre, slot_targets)
    terms = jnp.where(valid[None, :], terms, 0.0)

    potential = join3(
        lax.dot_general(split3(terms, 0), pick, (((1,), (1,)), ((), ())), preferred_element_type=F32), 0
    )

    home = centre_home.reshape(-1)
    back_index = home * capacity_back + route_rank(home, devices)
    back_place = (
        jnp.arange(devices * capacity_back, dtype=jnp.int32)[:, None] == back_index[None, :]
    ).astype(BF)
    sending = join3(
        lax.dot_general(back_place, split3(potential, 0), (((1,), (1,)), ((), ())), preferred_element_type=F32), 1
    )
    sending = sending.reshape(devices, capacity_back * nodes)
    returned = lax.all_to_all(sending, ("grp", "dev"), split_axis=0, concat_axis=0, tiled=True)
    return returned.reshape(-1)


def solution(mesh):
    placed = (
        P(None, ("grp", "dev")),
        P(("grp", "dev")),
        P(("grp", "dev"), None),
        P(("grp", "dev"), None),
        P(None, ("grp", "dev")),
        P(None, ("grp", "dev")),
        P(("grp", "dev"), None),
        P(),
        P(),
    )
    return jax.shard_map(
        per_device, mesh=mesh, in_specs=placed, out_specs=P(("grp", "dev")), check_vma=False
    )
```

time: 91.4 us -> 72.7 us (0.80)
  waiting for transfers between devices: 26.3 us -> 15.4 us
  other arithmetic: 25.4 us -> 14.9 us
  local copies, waits for them, and re-layouts: 6.79 us -> 12.5 us
  matrix products: 15.4 us -> 12.2 us
    all_to_all x1, waiting for transfers between devices: 26.3 us -> 15.4 us  [per_device(): lax.all_to_all(outgoing, ('grp', 'dev'), split_axis=0, concat_axis=0, til...]
    reduce_sum x3 -> x0, other arithmetic: 9.19 us -> none  [the longest x1 7.67 us: expansion_terms(): inner = jnp.sum(src[:, :, None, :] * rel_targets[:, None, :, :], axis=0)]
    all_to_all x1 -> x0, matrix products: 7.97 us -> none  [per_device(): lax.all_to_all(outgoing, ('grp', 'dev'), split_axis=1, concat_axis=1, til...]
    dot_general x6 -> x7, matrix products: 7.4 us -> 12.2 us  [the longest x1 7.02 us: per_device(): jnp.einsum('jn,scn->cjs', upsample, coarse_in.reshape(slots, 4, nodes), p...]
    another operation x0 -> x3, local copies, waits for them, and re-layouts: none -> 4.67 us  [the longest x1 4.26 us: per_device(): coarse_in.reshape(slots, 4, nodes)]
    all_to_all x0 -> x1, local copies, waits for them, and re-layouts: none -> 1.36 us  [per_device(): lax.all_to_all(outgoing, ('grp', 'dev'), split_axis=0, concat_axis=0, til...]
    add x0 -> x5, local copies, waits for them, and re-layouts: none -> 0.92 us  [the longest x2 0.52 us: join3(): return a + b + c]
  transfers between devices with their start and end apart: 1 -> 1, of which waited for: 1 -> 1; matrix products, arithmetic and copies ran while one was open for 1% -> 2% of each run, Pallas kernels for 0% -> 0%
where the time goes in v2:
time: 72.7 us; the launch traced here: 72.4 us
  waiting for transfers between devices  15.4 us (21%)
  other arithmetic  14.9 us (20%)
  local copies, waits for them, and re-layouts  12.5 us (17%)
  matrix products  12.2 us (17%)
  blocking collectives  9.41 us (13%)
  starting transfers between devices  7.48 us (10%)
    all_to_all x1, waiting for transfers between devices, per_device(): lax.all_to_all(outgoing, ('grp', 'dev'), split_axis=0, concat_axis=0, til...  15.4 us
    reduce_sum x1, other arithmetic, expansion_terms(): return jnp.sum(scale[:, None, :] * total, axis=0)  13.6 us
    all_to_all x1, blocking collectives, per_device(): lax.all_to_all(sending, ('grp', 'dev'), split_axis=0, concat_axis=0, tile...  9.41 us
    all_to_all x1, starting transfers between devices, per_device(): lax.all_to_all(outgoing, ('grp', 'dev'), split_axis=0, concat_axis=0, til...  7.48 us
    dot_general x1, matrix products, per_device(): jnp.einsum('jn,scn->cjs', upsample, coarse_in.reshape(slots, 4, nodes), p...  7.02 us
    another operation x1, local copies, waits for them, and re-layouts, per_device(): coarse_in.reshape(slots, 4, nodes)  4.26 us
    dot_general x1, matrix products, per_device(): placed = jnp.dot(place, rhs, preferred_element_type=F32)  2.02 us
  transfers between devices with their start and end apart: 1, of which 1 were waited for; matrix products, arithmetic and copies ran while one was open for 2% of the time, Pallas kernels for 0%

profile of v2, /device:TPU:0, one launch (start us, length us, event | category | flops | bytes accessed | tf_op | source)
XLA Modules:
  0.0 72.4 jit_solution(5868244715204381133)
XLA Ops:
  0.0 0.0 copy-start
  0.0 0.0 copy-start.4
  0.0 0.0 copy-start.3
  0.0 0.9 %reshape.438 = f32[512,16]{1,0:T(8,128)S(1)} reshape(f32[8192]{0:T(1024)} %param.10) | data formatting | bytes 65536 | tf_op jit(solution)/shard_map/reshape | solution.py:81
  0.9 0.1 copy.36
  1.0 1.2 %reshape.436 = f32[3,512,16]{2,1,0:T(8,128)S(1)} reshape(f32[3,8192]{1,0:T(4,128)} %param.9) | data formatting | bytes 196608 | tf_op jit(solution)/shard_map/reshape | solution.py:80
  2.2 0.2 copy.35
  2.5 0.1 copy.37
  2.6 0.2 broadcast_in_dim.10
  2.8 0.1 fusion.34
  3.0 0.0 copy-done.4
  3.0 0.1 copy.38
  3.1 0.2 add.182
  3.4 0.2 copy.39
  3.6 0.2 copy.40
  3.8 0.0 copy-done.3
  3.8 0.1 copy.34
  4.0 0.2 reshape.435
  4.1 0.5 fusion.31
  4.7 0.6 concatenate.28
  5.3 2.0 %fusion.17 = f32[2048,194]{0,1:T(8,128)S(1)} fusion(bf16[1024,194]{1,0:T(8,128)(2,1)S(1)} %concatenate.28, s32[1024]{0:T(1024)S(1)} %convert_add_fusion), kind=kOutput, calls=%fused_computation.26 | convolution fusion | flops 815792128 | bytes 1990656 | tf_op jit(solution)/shard_map/dot_general | solution.py:92
  7.3 0.0 copy-start.1
  7.3 0.0 copy-start.2
  7.4 0.1 slice_add_fusion
  7.4 0.1 add.188
  7.5 0.3 copy.41
  7.9 0.0 copy-start.5
  7.9 0.4 reshape.440
  8.3 1.4 %copy.42 = f32[32,1,4160]{2,1,0:T(1,128)} copy(f32[32,1,4160]{2,0,1:T(8,128)S(1)} %maximum_bitcast_fusion) | data formatting | bytes 1064960 | tf_op jit(solution)/shard_map/all_to_all | solution.py:99
  9.6 7.5 %all-to-all-start = ((f32[32,1,4160]{2,1,0:T(1,128)}), f32[32,1,4160]{2,1,0:T(1,128)S(1)}, u32[]{:S(2)}, u32[]{:S(2)}) async-start(f32[32,1,4160]{2,1,0:T(1,128)} %copy.42), calls=%async_computation | async-start | bytes 1081344 | tf_op jit(solution)/shard_map/all_to_all | solution.py:99
  17.1 0.0 copy-done.1
  17.1 0.3 reshape.441
  17.4 0.0 copy-done.2
  17.4 0.3 subtract_bitcast_fusion
  17.7 0.2 copy.44
  18.0 0.0 copy-done.5
  18.0 0.3 fusion.32
  18.3 15.4 %all-to-all-done = f32[32,1,4160]{2,1,0:T(1,128)S(1)} async-done(((f32[32,1,4160]{2,1,0:T(1,128)}), f32[32,1,4160]{2,1,0:T(1,128)S(1)}, u32[]{:S(2)}, u32[]{:S(2)}) %all-to-all-start) | async-done | bytes 532512 | tf_op jit(solution)/shard_map/all_to_all | solution.py:99
  33.7 0.1 sub.147
  33.8 1.0 %fusion.21 = f32[153,2048]{1,0:T(8,128)S(1)} fusion(s32[2048]{0:T(1024)S(1)} %sub.147, bf16[51,512]{1,0:T(8,128)(2,1)S(1)} %get-tuple-element.30, bf16[51,512]{1,0:T(8,128)(2,1)S(1)} %get-tuple-element.29, bf16[51,512]{1,0:T(8,128)(2,1)S(1)} %get-tuple-element.28), kind=kOutput, calls=%fused_computation.31 | convolution fusion | flops 322382848 | bytes 1418240 | tf_op jit(solution)/shard_map/dot_general | solution.py:110
  34.8 0.1 slice_add_fusion.2
  35.0 0.1 fusion.74
  35.0 4.3 %reshape_reshape.3 = f32[2048,4,16]{2,1,0:T(4,128)} reshape(f32[32,4096]{1,0:T(8,128)S(1)} %slice.78) | data formatting | bytes 1048576 | tf_op jit(solution)/shard_map/reshape;reshape | solution.py:115
  39.3 0.0 copy-done
  39.3 0.0 copy-start.6
  39.3 7.0 %fusion.24 = f32[4,64,2048]{2,1,0:T(8,128)S(1)} fusion(f32[2048,4,16]{2,1,0:T(4,128)} %reshape_reshape.3, f32[64,16]{0,1:T(8,128)S(1)} %copy-done), kind=kOutput, calls=%fused_computation.35 | convolution fusion | flops 100663296 | bytes 2625536 | tf_op jit(solution)/shard_map/jn,scn->cjs/dot_general | solution.py:114
  46.3 0.0 copy-done.6
  46.3 0.2 fusion.39
  46.6 0.2 fusion.40
  46.8 13.6 %fusion.15 = f32[16,2048]{1,0:T(8,128)S(1)} fusion(f32[64,2048]{1,0:T(8,128)S(1)} %get-tuple-element.14, f32[16,2048]{1,0:T(8,128)S(1)} %get-tuple-element.19, f32[16,2048]{1,0:T(8,128)S(1)} %get-tuple-element.20, f32[64,2048]{1,0:T(8,128)S(1)} %get-tuple-element.12, f32[16,2048]{1,0:T(8,128)S(1)} %get-tuple-element.21, ...), kind=kLoop, calls=%fused_computation.23 | loop fusion | flops 104824832 | bytes 3276800 | tf_op jit(solution)/shard_map/reduce_sum | solution.py:54
  60.4 0.9 %fusion.20 = f32[48,512]{1,0:T(8,128)S(1)} fusion(s32[2048]{0:T(1024)S(1)} %sub.147, bf16[16,2048]{1,0:T(8,128)(2,1)S(1)} %get-tuple-element.26, bf16[16,2048]{1,0:T(8,128)(2,1)S(1)} %get-tuple-element.27, bf16[16,2048]{1,0:T(8,128)(2,1)S(1)} %get-tuple-element.25), kind=kOutput, calls=%fused_computation.30 | convolution fusion | flops 102301696 | bytes 303104 | tf_op jit(solution)/shard_map/dot_general | solution.py:122
  61.3 0.5 fusion.29
  61.9 0.2 copy.45
  62.1 0.2 all_to_all.19
  62.3 9.4 %all_to_all.22 = f32[32,1,512]{2,1,0:T(1,128)S(1)} all-to-all(f32[32,1,512]{2,1,0:T(1,128)S(1)} %all_to_all.19), channel_id=1, replica_groups=mesh['grp'=4,'dev'=8] {'grp','dev'}, dimensions={0} | all-to-all | bytes 131072 | tf_op jit(solution)/shard_map/all_to_all | solution.py:134
  71.7 0.6 copy.55
  (18 shorter events, 0.4 us)
Async XLA Ops:
  0.0 39.3 %copy-start = (f32[64,16]{0,1:T(8,128)S(1)}, f32[64,16]{0,1:T(8,128)}, u32[]{:S(2)}) copy-start(f32[64,16]{0,1:T(8,128)} %param.16) | copy-start | bytes 12292
  0.0 3.0 %copy-start.4 = (s32[512,2]{0,1:T(2,128)S(1)}, s32[512,2]{0,1:T(2,128)}, u32[]{:S(2)}) copy-start(s32[512,2]{0,1:T(2,128)} %param.12) | copy-start | bytes 12292
  0.0 3.8 %copy-start.3 = (s32[512,2]{0,1:T(2,128)S(1)}, s32[512,2]{0,1:T(2,128)}, u32[]{:S(2)}) copy-start(s32[512,2]{0,1:T(2,128)} %param.11) | copy-start | bytes 12292
  7.3 9.8 %copy-start.1 = (f32[3,8192]{1,0:T(4,128)S(1)}, f32[3,8192]{1,0:T(4,128)}, u32[]{:S(2)}) copy-start(f32[3,8192]{1,0:T(4,128)} %param.14) | copy-start | bytes 294916
  7.3 10.1 %copy-start.2 = (f32[3,512]{1,0:T(4,128)S(1)}, f32[3,512]{1,0:T(4,128)}, u32[]{:S(2)}) copy-start(f32[3,512]{1,0:T(4,128)} %param.13) | copy-start | bytes 18436
  7.9 10.1 %copy-start.5 = (s32[512,1]{0,1:T(1,128)S(1)}, s32[512,1]{0,1:T(1,128)}, u32[]{:S(2)}) copy-start(s32[512,1]{0,1:T(1,128)} %param.15) | copy-start | bytes 6148
  9.6 24.0 %all-to-all-start = ((f32[32,1,4160]{2,1,0:T(1,128)}), f32[32,1,4160]{2,1,0:T(1,128)S(1)}, u32[]{:S(2)}, u32[]{:S(2)}) async-start(f32[32,1,4160]{2,1,0:T(1,128)} %copy.42), calls=%async_computation | async-start | bytes 1081344 | tf_op jit(solution)/shard_map/all_to_all | solution.py:99
  39.3 7.0 %copy-start.6 = (f32[64]{0:T(128)S(1)}, f32[64]{0:T(128)}, u32[]{:S(2)}) copy-start(f32[64]{0:T(128)} %param.17) | copy-start | bytes 772

commit v3 on v2

--- a/solution.py
+++ b/solution.py
@@ -31,9 +31,9 @@
 
 
 def expansion_terms(fine, strength, centre_pos, rel_targets):
-    ax = fine[0] - centre_pos[0][None, :]
-    ay = fine[1] - centre_pos[1][None, :]
-    az = fine[2] - centre_pos[2][None, :]
+    ax = fine[0] - centre_pos[0][None]
+    ay = fine[1] - centre_pos[1][None]
+    az = fine[2] - centre_pos[2][None]
     bx, by, bz = rel_targets[0], rel_targets[1], rel_targets[2]
     rs2 = ax * ax + ay * ay + az * az
     rt2 = bx * bx + by * by + bz * bz
@@ -42,8 +42,8 @@
     ax = ax * inv_rs2
     ay = ay * inv_rs2
     az = az * inv_rs2
-    w = ax[:, None, :] * bx[None] + ay[:, None, :] * by[None] + az[:, None, :] * bz[None]
-    rho2 = rt2[None, :, :] * inv_rs2[:, None, :]
+    w = ax[:, None] * bx[None] + ay[:, None] * by[None] + az[:, None] * bz[None]
+    rho2 = rt2[None] * inv_rs2[:, None]
     p_prev = jnp.ones_like(w)
     p_now = w
     total = 1.0 + w
@@ -51,7 +51,7 @@
         p_next = ((2 * level + 1) / (level + 1)) * w * p_now - (level / (level + 1)) * rho2 * p_prev
         total = total + p_next
         p_prev, p_now = (p_now, p_next)
-    return jnp.sum(scale[:, None, :] * total, axis=0)
+    return jnp.sum(scale[:, None] * total, axis=0)
 
 
 def per_device(
@@ -98,8 +98,9 @@
 
     incoming = lax.all_to_all(outgoing, ("grp", "dev"), split_axis=0, concat_axis=0, tiled=True)
 
-    coarse_in = incoming[:, : capacity * width].reshape(slots, width)
-    ids = jnp.round(incoming[:, capacity * width :]).astype(jnp.int32).reshape(slots) - 1
+    coarse_in = incoming[:, : capacity * width].reshape(slots // 2, 2 * width)
+    ids = jnp.round(incoming[:, capacity * width :]).astype(jnp.int32)
+    ids = ids.reshape(devices, capacity // 2, 2).transpose(2, 0, 1).reshape(slots) - 1
     valid = ids >= 0
     pick = (jnp.arange(centre_count, dtype=jnp.int32)[:, None] == ids[None, :]).astype(BF)
 
@@ -108,14 +109,18 @@
         [centres, rel.transpose(0, 2, 1).reshape(3 * nodes, centre_count)], axis=0
     )
     gathered = join3(jnp.dot(split3(centre_data, 0), pick, preferred_element_type=F32), 0)
-    slot_centre = gathered[:3]
-    slot_targets = gathered[3:].reshape(3, nodes, slots)
+    slot_centre = gathered[:3].reshape(3, 2, slots // 2)
+    slot_targets = gathered[3:].reshape(3, nodes, 2, slots // 2)
 
-    upper = jnp.einsum(
-        "jn,scn->cjs", upsample, coarse_in.reshape(slots, 4, nodes), precision=HI
-    )
-    strength = upper[3] * fine_weights[:, None]
-    terms = expansion_terms(upper[:3], strength, slot_centre, slot_targets)
+    eye_c = jnp.eye(4, dtype=F32)
+    eye_p = jnp.eye(2, dtype=F32)
+    refine_w = (
+        eye_c[:, None, None, None, :, None] * upsample[None, :, None, None, None, :] * eye_p[None, None, :, :, None, None]
+    ).reshape(4 * fine_count * 2, 2 * width)
+    upper = lax.dot_general(refine_w, coarse_in, (((1,), (1,)), ((), ())), precision=HI)
+    upper = upper.reshape(4, fine_count, 2, slots // 2)
+    strength = upper[3] * fine_weights[:, None, None]
+    terms = expansion_terms(upper[:3], strength, slot_centre, slot_targets).reshape(nodes, slots)
     terms = jnp.where(valid[None, :], terms, 0.0)
 
     potential = join3(

time: 72.7 us -> 71 us (0.977)
  matrix products: 12.2 us -> 7.03 us
  other arithmetic: 14.9 us -> 18.4 us
  waiting for transfers between devices: 15.4 us -> 12.7 us
  local copies, waits for them, and re-layouts: 12.5 us -> 15 us
    dot_general x1, matrix products: 7.02 us -> 1.8 us  [per_device(): lax.dot_general(refine_w, coarse_in, (((1,), (1,)), ((), ())), precision=HI)]
    another operation x3 -> x2, local copies, waits for them, and re-layouts: 4.67 us -> 0.41 us  [the longest x1 4.26 us: per_device(): coarse_in.reshape(slots, 4, nodes)]
    all_to_all x1, waiting for transfers between devices: 15.4 us -> 12.7 us  [per_device(): lax.all_to_all(outgoing, ('grp', 'dev'), split_axis=0, concat_axis=0, til...]
    slice x2 -> x5, local copies, waits for them, and re-layouts: 0.05 us -> 2.39 us  [the longest x2 2.05 us: per_device(): coarse_in = incoming[:, :capacity * width].reshape(slots // 2, 2 * width)]
    all_to_all x1 -> x2, local copies, waits for them, and re-layouts: 1.36 us -> 3.12 us  [per_device(): lax.all_to_all(outgoing, ('grp', 'dev'), split_axis=0, concat_axis=0, til...]
    mul x0 -> x6, local copies, waits for them, and re-layouts: none -> 1.68 us  [the longest x1 1.32 us: per_device(): eye_c[:, None, None, None, :, None] * upsample[None, :, None, None, None, :]]
    squeeze x0 -> x4, local copies, waits for them, and re-layouts: none -> 1.22 us  [the longest x1 0.31 us: expansion_terms(): ax = fine[0] - centre_pos[0][None]]
    reshape x2, local copies, waits for them, and re-layouts: 1.01 us -> 0.23 us  [per_device(): density.reshape(panels, nodes)]
  transfers between devices with their start and end apart: 1 -> 1, of which waited for: 1 -> 1; matrix products, arithmetic and copies ran while one was open for 2% -> 5% of each run, Pallas kernels for 0% -> 0%
where the time goes in v3:
time: 71 us; the launch traced here: 70.7 us
  other arithmetic  18.4 us (26%)
  local copies, waits for them, and re-layouts  15 us (21%)
  waiting for transfers between devices  12.7 us (18%)
  blocking collectives  9.41 us (13%)
  starting transfers between devices  7.48 us (11%)
  matrix products  7.03 us (10%)
    reduce_sum x1, other arithmetic, expansion_terms(): return jnp.sum(scale[:, None] * total, axis=0)  13.6 us
    all_to_all x1, waiting for transfers between devices, per_device(): lax.all_to_all(outgoing, ('grp', 'dev'), split_axis=0, concat_axis=0, til...  12.7 us
    all_to_all x1, blocking collectives, per_device(): lax.all_to_all(sending, ('grp', 'dev'), split_axis=0, concat_axis=0, tile...  9.41 us
    all_to_all x1, starting transfers between devices, per_device(): lax.all_to_all(outgoing, ('grp', 'dev'), split_axis=0, concat_axis=0, til...  7.48 us
    all_to_all x2, local copies, waits for them, and re-layouts, per_device(): lax.all_to_all(outgoing, ('grp', 'dev'), split_axis=0, concat_axis=0, til...  3.12 us
    slice x2, local copies, waits for them, and re-layouts, per_device(): coarse_in = incoming[:, :capacity * width].reshape(slots // 2, 2 * width)  2.05 us
    dot_general x1, matrix products, per_device(): placed = jnp.dot(place, rhs, preferred_element_type=F32)  2.02 us
    dot_general x1, matrix products, per_device(): lax.dot_general(refine_w, coarse_in, (((1,), (1,)), ((), ())), precision=HI)  1.8 us
  transfers between devices with their start and end apart: 1, of which 1 were waited for; matrix products, arithmetic and copies ran while one was open for 5% of the time, Pallas kernels for 0%

profile of v3, /device:TPU:0, one launch (start us, length us, event | category | flops | bytes accessed | tf_op | source)
XLA Modules:
  0.0 70.7 jit_solution(4083936191375504698)
XLA Ops:
  0.0 0.7 broadcast_add_fusion
  0.7 0.1 copy.79
  0.9 0.2 add.188
  1.1 0.2 copy.80
  1.3 1.2 %reshape.316 = f32[3,512,16]{2,1,0:T(8,128)S(1)} reshape(f32[3,8192]{1,0:T(4,128)} %param.9) | data formatting | bytes 196608 | tf_op jit(solution)/shard_map/reshape | solution.py:80
  2.5 0.2 copy.76
  2.7 0.1 reshape.318
  2.9 0.1 copy.77
  3.0 0.1 copy.78
  3.1 0.2 broadcast_in_dim.10
  3.3 0.1 fusion.29
  3.5 0.2 copy.81
  3.7 0.1 copy.75
  3.8 0.2 reshape.315
  4.0 0.5 fusion.26
  4.6 0.6 concatenate.28
  5.2 2.0 %fusion.17 = f32[2048,194]{0,1:T(8,128)S(1)} fusion(bf16[1024,194]{1,0:T(8,128)(2,1)S(1)} %concatenate.28, s32[1024]{0:T(1024)S(1)} %convert_add_fusion), kind=kOutput, calls=%fused_computation.26 | convolution fusion | flops 815792128 | bytes 1990656 | tf_op jit(solution)/shard_map/dot_general | solution.py:92
  7.2 0.1 slice_add_fusion
  7.3 0.3 copy.82
  7.7 0.4 reshape.320
  8.0 0.1 add.194
  8.1 1.4 %copy.83 = f32[32,1,4160]{2,1,0:T(1,128)} copy(f32[32,1,4160]{2,0,1:T(8,128)S(1)} %maximum_bitcast_fusion) | data formatting | bytes 1064960 | tf_op jit(solution)/shard_map/all_to_all | solution.py:99
  9.5 7.5 %all-to-all-start = ((f32[32,1,4160]{2,1,0:T(1,128)}), f32[32,1,4160]{2,1,0:T(1,128)S(1)}, u32[]{:S(2)}, u32[]{:S(2)}) async-start(f32[32,1,4160]{2,1,0:T(1,128)} %copy.83), calls=%async_computation | async-start | bytes 1081344 | tf_op jit(solution)/shard_map/all_to_all | solution.py:99
  17.0 0.3 reshape.322
  17.3 0.3 subtract_bitcast_fusion
  17.6 0.2 copy.88
  17.8 0.1 copy.86
  17.9 0.1 broadcast_multiply_fusion.1
  18.1 0.0 copy-start.11
  18.1 0.4 broadcast_multiply_fusion
  18.5 1.3 %mul.396 = f32[512,128]{1,0:T(8,128)S(1)} reshape(f32[4,64,2,2,4,16]{5,4,3,2,1,0:T(4,128)S(1)} %broadcast_multiply_fusion) | data formatting | bytes 524288 | tf_op jit(solution)/shard_map/mul | solution.py:118
  19.9 0.3 fusion.27
  20.2 0.6 convert_add_fusion.1
  20.8 12.7 %all-to-all-done = f32[32,1,4160]{2,1,0:T(1,128)S(1)} async-done(((f32[32,1,4160]{2,1,0:T(1,128)}), f32[32,1,4160]{2,1,0:T(1,128)S(1)}, u32[]{:S(2)}, u32[]{:S(2)}) %all-to-all-start) | async-done | bytes 532512 | tf_op jit(solution)/shard_map/all_to_all | solution.py:99
  33.5 1.8 %copy.84 = f32[32,1,4160]{0,2,1:T(8,128)S(1)} copy(f32[32,1,4160]{2,1,0:T(1,128)S(1)} %all-to-all-done) | data formatting | bytes 1064960 | tf_op jit(solution)/shard_map/all_to_all | solution.py:99
  35.3 1.5 %slice.86 = f32[32,4096]{0,1:T(8,128)} slice(f32[32,4160]{0,1:T(8,128)S(1)} %bitcast.41), slice={[0:32], [0:4096]} | slice | bytes 1048576 | tf_op jit(solution)/shard_map/slice | solution.py:101
  36.8 0.1 copy.85
  36.9 0.1 sub.153
  36.9 1.0 %fusion.19 = f32[153,2048]{1,0:T(8,128)S(1)} fusion(s32[2048]{0:T(1024)S(1)} %sub.153, bf16[51,512]{1,0:T(8,128)(2,1)S(1)} %get-tuple-element.33, bf16[51,512]{1,0:T(8,128)(2,1)S(1)} %get-tuple-element.32, bf16[51,512]{1,0:T(8,128)(2,1)S(1)} %get-tuple-element.31), kind=kOutput, calls=%fused_computation.29 | convolution fusion | flops 322382848 | bytes 1418240 | tf_op jit(solution)/shard_map/dot_general | solution.py:111
  38.0 0.1 slice_add_fusion.2
  38.1 0.1 slice_reduce_fusion.2
  38.2 0.6 broadcast_compare_fusion
  38.8 0.6 copy.87
  39.4 0.1 reshape.321
  39.5 1.8 %fusion.63 = f32[512,1024]{1,0:T(8,128)S(1)} fusion(f32[512,128]{1,0:T(8,128)S(1)} %mul.396, f32[1024,128]{1,0:T(8,128)S(1)} %reshape.321), kind=kOutput, calls=%fused_computation.136 | convolution fusion | flops 805306368 | bytes 2883584 | tf_op jit(solution)/shard_map/dot_general | solution.py:120
  41.3 0.2 fusion.61
  41.6 0.3 squeeze.18
  41.9 0.3 squeeze.19
  42.2 0.3 squeeze.20
  42.5 0.3 squeeze.8
  42.9 0.8 %rsqrt_multiply_fusion = (f32[64,2,1024]{2,1,0:T(2,128)S(1)}, f32[64,2,1024]{2,1,0:T(2,128)S(1)}) fusion(f32[64,2,1024]{2,1,0:T(2,128)S(1)} %squeeze.8, f32[64]{0:T(128)S(1)} %copy-done.13, f32[64,2,1024]{2,1,0:T(2,128)S(1)} %squeeze.20, f32[2,1024]{1,0:T(2,128)S(1)} %sub.164, f32[64,2,1024]{2,1,0:T(2,128)S(1)} %squeeze.19, f32[2,1024]{1,0:T(2,128)S(1)} %sub.161, ...), kind=kLoop, calls=%fused_computation.53 | loop fusion | flops 1310720 | bytes 3170560 | tf_op jit(solution)/shard_map/mul | solution.py:41
  43.6 0.5 subtract_multiply_fusion.2
  44.1 0.1 mul.416
  44.2 0.1 mul.411
  44.4 0.1 mul.406
  44.6 0.2 copy-done.3
  44.8 0.2 subtract_multiply_fusion.1
  45.0 13.6 %fusion.15 = f32[16,2,1024]{2,0,1:T(8,128)S(1)} fusion(f32[64,2,1024]{2,1,0:T(2,128)S(1)} %get-tuple-element.13, f32[16,2,1024]{2,0,1:T(8,128)S(1)} %copy.92, f32[16,2,1024]{2,0,1:T(8,128)S(1)} %get-tuple-element.36, f32[64,2,1024]{2,1,0:T(2,128)S(1)} %bitcast.47, f32[16,2,1024]{2,0,1:T(8,128)S(1)} %get-tuple-element.37, f32[64,2,1024]{2,1,0:T(2,128)S(1)} %bitcast.46, ...), kind=kLoop, calls=%fused_computation.23 | loop fusion | flops 104824832 | bytes 3276800 | tf_op jit(solution)/shard_map/reduce_sum | solution.py:54
  58.8 0.9 %fusion.18 = f32[48,512]{1,0:T(8,128)S(1)} fusion(s32[2048]{0:T(1024)S(1)} %copy-done.7, bf16[16,2048]{1,0:T(8,128)(2,1)S(1)} %get-tuple-element.29, bf16[16,2048]{1,0:T(8,128)(2,1)S(1)} %get-tuple-element.30, bf16[16,2048]{1,0:T(8,128)(2,1)S(1)} %get-tuple-element.28), kind=kOutput, calls=%fused_computation.28 | convolution fusion | flops 102301696 | bytes 303104 | tf_op jit(solution)/shard_map/dot_general | solution.py:127
  59.7 0.5 fusion.24
  60.2 0.2 copy.94
  60.4 0.2 all_to_all.19
  60.6 9.4 %all_to_all.22 = f32[32,1,512]{2,1,0:T(1,128)S(1)} all-to-all(f32[32,1,512]{2,1,0:T(1,128)S(1)} %all_to_all.19), channel_id=1, replica_groups=mesh['grp'=4,'dev'=8] {'grp','dev'}, dimensions={0} | all-to-all | bytes 131072 | tf_op jit(solution)/shard_map/all_to_all | solution.py:139
  70.1 0.6 copy.105
  (51 shorter events, 0.5 us)
Async XLA Ops:
  0.0 2.7 %copy-start.5 = (f32[8192]{0:T(1024)S(1)}, f32[8192]{0:T(1024)}, u32[]{:S(2)}) copy-start(f32[8192]{0:T(1024)} %param.10) | copy-start | bytes 98308
  2.5 1.2 %copy-start.10 = (s32[512,2]{0,1:T(2,128)S(1)}, s32[512,2]{0,1:T(2,128)}, u32[]{:S(2)}) copy-start(s32[512,2]{0,1:T(2,128)} %param.11) | copy-start | bytes 12292
  7.6 9.4 %copy-start.1 = (f32[3,8192]{1,0:T(4,128)S(1)}, f32[3,8192]{1,0:T(4,128)}, u32[]{:S(2)}) copy-start(f32[3,8192]{1,0:T(4,128)} %param.14) | copy-start | bytes 294916
  8.0 9.3 %copy-start.4 = (f32[3,512]{1,0:T(4,128)S(1)}, f32[3,512]{1,0:T(4,128)}, u32[]{:S(2)}) copy-start(f32[3,512]{1,0:T(4,128)} %param.13) | copy-start | bytes 18436
  9.5 8.3 %copy-start.9 = (f32[64,16]{0,1:T(8,128)S(1)}, f32[64,16]{0,1:T(8,128)}, u32[]{:S(2)}) copy-start(f32[64,16]{0,1:T(8,128)} %param.16) | copy-start | bytes 12292
  9.5 24.0 %all-to-all-start = ((f32[32,1,4160]{2,1,0:T(1,128)}), f32[32,1,4160]{2,1,0:T(1,128)S(1)}, u32[]{:S(2)}, u32[]{:S(2)}) async-start(f32[32,1,4160]{2,1,0:T(1,128)} %copy.83), calls=%async_computation | async-start | bytes 1081344 | tf_op jit(solution)/shard_map/all_to_all | solution.py:99
  18.1 1.8 %copy-start.11 = (s32[512,1]{0,1:T(1,128)S(1)}, s32[512,1]{0,1:T(1,128)}, u32[]{:S(2)}) copy-start(s32[512,1]{0,1:T(1,128)} %param.15) | copy-start | bytes 6148
  36.9 1.3 %copy-start.6 = (s32[2048]{0:T(1024)}, s32[2048]{0:T(1024)S(1)}, u32[]{:S(2)}) copy-start(s32[2048]{0:T(1024)S(1)} %sub.153) | copy-start | bytes 24580
  36.9 1.9 %copy-start = (f32[32,4096]{0,1:T(8,128)S(1)}, f32[32,4096]{0,1:T(8,128)}, u32[]{:S(2)}) copy-start(f32[32,4096]{0,1:T(8,128)} %slice.86) | copy-start | bytes 1572868
  38.8 4.0 %copy-start.2 = (f32[2,1024]{1,0:T(2,128)}, f32[2,1024]{1,0:T(2,128)S(1)}, u32[]{:S(2)}) copy-start(f32[2,1024]{1,0:T(2,128)S(1)} %sub.164) | copy-start | bytes 24580
  41.6 1.3 %copy-start.13 = (f32[64]{0:T(128)S(1)}, f32[64]{0:T(128)}, u32[]{:S(2)}) copy-start(f32[64]{0:T(128)} %param.17) | copy-start | bytes 772
  44.1 0.7 copy-start.3
  45.0 13.7 %copy-start.8 = (pred[2048]{0:T(1024)(128)(4,1)S(1)}, pred[2048]{0:T(1024)(128)(4,1)}, u32[]{:S(2)}) copy-start(pred[2048]{0:T(1024)(128)(4,1)} %broadcast_compare_fusion) | copy-start | bytes 6148
  45.0 13.7 %copy-start.7 = (s32[2048]{0:T(1024)S(1)}, s32[2048]{0:T(1024)}, u32[]{:S(2)}) copy-start(s32[2048]{0:T(1024)} %copy-done.6) | copy-start | bytes 24580
  58.7 1.0 %copy-start.12 = (s32[512]{0:T(512)S(1)}, s32[512]{0:T(512)}, u32[]{:S(2)}) copy-start(s32[512]{0:T(512)} %convert_add_fusion.1) | copy-start | bytes 6148

commit v4 on v3

--- a/solution.py
+++ b/solution.py
@@ -30,7 +30,18 @@
     return (a + b) + c
 
 
+def clenshaw_constants(order):
+    c1 = [(2 * l + 1) / (l + 1) for l in range(order + 1)]
+    c2 = [l / (l + 1) for l in range(order + 2)]
+    mu = [1.0] * (order + 1)
+    for l in range(order - 1, -1, -1):
+        mu[l] = c1[l] * mu[l + 1]
+    gamma = [c2[l + 1] / (c1[l] * c1[l + 1]) for l in range(order - 1)]
+    return mu, gamma
+
+
 def expansion_terms(fine, strength, centre_pos, rel_targets):
+    mu, gamma = clenshaw_constants(ORDER)
     ax = fine[0] - centre_pos[0][None]
     ay = fine[1] - centre_pos[1][None]
     az = fine[2] - centre_pos[2][None]
@@ -38,20 +49,18 @@
     rs2 = ax * ax + ay * ay + az * az
     rt2 = bx * bx + by * by + bz * bz
     inv_rs2 = 1.0 / rs2
-    scale = strength * lax.rsqrt(rs2)
+    scale = (strength * mu[0]) * lax.rsqrt(rs2)
     ax = ax * inv_rs2
     ay = ay * inv_rs2
     az = az * inv_rs2
     w = ax[:, None] * bx[None] + ay[:, None] * by[None] + az[:, None] * bz[None]
     rho2 = rt2[None] * inv_rs2[:, None]
-    p_prev = jnp.ones_like(w)
-    p_now = w
-    total = 1.0 + w
-    for level in range(1, ORDER):
-        p_next = ((2 * level + 1) / (level + 1)) * w * p_now - (level / (level + 1)) * rho2 * p_prev
-        total = total + p_next
-        p_prev, p_now = (p_now, p_next)
-    return jnp.sum(scale[:, None] * total, axis=0)
+    t_next = w + (1.0 / mu[ORDER - 1])
+    t_after = jnp.ones_like(w)
+    for level in range(ORDER - 2, -1, -1):
+        t_now = (w * t_next + (1.0 / mu[level])) - gamma[level] * (rho2 * t_after)
+        t_after, t_next = (t_next, t_now)
+    return jnp.sum(scale[:, None] * t_next, axis=0)
 
 
 def per_device(
@@ -84,14 +93,26 @@
     coarse_pairs = jnp.broadcast_to(coarse[:, None, :], (panels, fanout, width)).reshape(pairs, width)
     ids1 = crevice_centre.reshape(pairs) + 1
     id_parts = jnp.stack([ids1 // 16, ids1 % 16], axis=1).astype(BF)
-    rhs = jnp.concatenate([split3(coarse_pairs, 1), id_parts], axis=1)
+    parts = split3(coarse_pairs, 1).reshape(pairs, 3, 1, width)
+    none = jnp.zeros_like(parts)
+    none_id = jnp.zeros_like(id_parts)
+    rhs = jnp.concatenate(
+        [
+            jnp.concatenate([jnp.concatenate([parts, none], 2).reshape(pairs, 6 * width), id_parts, none_id], 1),
+            jnp.concatenate([jnp.concatenate([none, parts], 2).reshape(pairs, 6 * width), none_id, id_parts], 1),
+        ],
+        0,
+    )
 
     destination = crevice_routes.reshape(-1)
     slot_index = destination * capacity + route_rank(destination, devices)
-    place = (jnp.arange(slots, dtype=jnp.int32)[:, None] == slot_index[None, :]).astype(BF)
+    row_slot = 2 * jnp.arange(slots // 2, dtype=jnp.int32)[:, None]
+    place = jnp.concatenate(
+        [(row_slot == slot_index[None, :]), (row_slot + 1 == slot_index[None, :])], axis=1
+    ).astype(BF)
     placed = jnp.dot(place, rhs, preferred_element_type=F32)
-    payload = join3(placed[:, : 3 * width], 1)
-    slot_ids = 16.0 * placed[:, 3 * width] + placed[:, 3 * width + 1]
+    payload = join3(placed[:, : 6 * width], 1)
+    slot_ids = 16.0 * placed[:, 6 * width :: 2] + placed[:, 6 * width + 1 :: 2]
     outgoing = jnp.concatenate(
         [payload.reshape(devices, capacity * width), slot_ids.reshape(devices, capacity)], axis=1
     )

time: 71 us -> 72.6 us (1.023)
  local copies, waits for them, and re-layouts: 15 us -> 16.4 us
  other arithmetic: 18.4 us -> 17.4 us
  matrix products: 7.03 us -> 7.99 us
    reduce_sum x1, other arithmetic: 13.6 us -> 11.8 us  [expansion_terms(): return jnp.sum(scale[:, None] * t_next, axis=0)]
    eq x0 -> x1, other arithmetic: none -> 1.32 us  [per_device(): row_slot == slot_index[None, :]]
    dot_general x1, matrix products: 2.02 us -> 3 us  [per_device(): placed = jnp.dot(place, rhs, preferred_element_type=F32)]
    concatenate x1, local copies, waits for them, and re-layouts: 0.57 us -> 1.36 us  [per_device(): jnp.concatenate([parts, none], 2).reshape(pairs, 6 * width)]
    reshape x2, local copies, waits for them, and re-layouts: 0.23 us -> 0.98 us  [per_device(): density.reshape(panels, nodes)]
where the time goes in v4:
time: 72.6 us; the launch traced here: 72.2 us
  other arithmetic  17.4 us (24%)
  local copies, waits for them, and re-layouts  16.4 us (23%)
  waiting for transfers between devices  12.7 us (17%)
  blocking collectives  9.41 us (13%)
  matrix products  7.99 us (11%)
  starting transfers between devices  7.48 us (10%)
    all_to_all x1, waiting for transfers between devices, per_device(): lax.all_to_all(outgoing, ('grp', 'dev'), split_axis=0, concat_axis=0, til...  12.7 us
    reduce_sum x1, other arithmetic, expansion_terms(): return jnp.sum(scale[:, None] * t_next, axis=0)  11.8 us
    all_to_all x1, blocking collectives, per_device(): lax.all_to_all(sending, ('grp', 'dev'), split_axis=0, concat_axis=0, tile...  9.41 us
    all_to_all x1, starting transfers between devices, per_device(): lax.all_to_all(outgoing, ('grp', 'dev'), split_axis=0, concat_axis=0, til...  7.48 us
    all_to_all x2, local copies, waits for them, and re-layouts, per_device(): lax.all_to_all(outgoing, ('grp', 'dev'), split_axis=0, concat_axis=0, til...  3.11 us
    dot_general x1, matrix products, per_device(): placed = jnp.dot(place, rhs, preferred_element_type=F32)  3 us
    slice x2, local copies, waits for them, and re-layouts, per_device(): coarse_in = incoming[:, :capacity * width].reshape(slots // 2, 2 * width)  2.05 us
    dot_general x1, matrix products, per_device(): lax.dot_general(refine_w, coarse_in, (((1,), (1,)), ((), ())), precision=HI)  1.8 us
  transfers between devices with their start and end apart: 1, of which 1 were waited for; matrix products, arithmetic and copies ran while one was open for 5% of the time, Pallas kernels for 0%

profile of v4, /device:TPU:0, one launch (start us, length us, event | category | flops | bytes accessed | tf_op | source)
XLA Modules:
  0.0 72.2 jit_solution(10903505824808973157)
XLA Ops:
  0.0 1.2 %reshape.404 = f32[3,512,16]{2,1,0:T(8,128)S(1)} reshape(f32[3,8192]{1,0:T(4,128)} %param.9) | data formatting | bytes 196608 | tf_op jit(solution)/shard_map/reshape | solution.py:89
  1.2 0.2 copy.91
  1.4 0.9 %reshape.406 = f32[512,16]{1,0:T(8,128)S(1)} reshape(f32[8192]{0:T(1024)} %param.10) | data formatting | bytes 65536 | tf_op jit(solution)/shard_map/reshape | solution.py:90
  2.3 0.1 copy.92
  2.4 0.1 copy.93
  2.6 0.2 broadcast_in_dim.12
  2.8 0.1 fusion.51
  2.9 0.2 pad_maximum_fusion
  3.1 0.3 copy.112
  3.4 1.4 %fusion.87 = (bf16[1024,3,2,64]{0,3,2,1:T(8,128)(2,1)}, bf16[1024,3,2,64]{0,3,2,1:T(8,128)(2,1)}) fusion(bf16[1024,3,1,64]{0,3,2,1:T(8,128)(2,1)S(1)} %copy.112), kind=kLoop, calls=%fused_computation.163 | loop fusion | bytes 1966080 | tf_op jit(solution)/shard_map/concatenate | solution.py:101
  4.8 0.1 copy.90
  4.9 0.2 reshape.403
  5.1 0.5 fusion.46
  5.7 0.1 copy.95
  5.8 0.2 add.216
  6.1 1.3 %broadcast_compare_fusion.1 = (pred[1024,1024]{1,0:T(32,128)(4,1)S(1)}, pred[1024,1024]{1,0:T(32,128)(4,1)S(1)}) fusion(s32[1024]{0:T(1024)S(1)} %get-tuple-element.40, s32[1024]{0:T(1024)S(1)} %get-tuple-element.41, s32[1024]{0:T(1024)S(1)} %broadcast_add_fusion.1), kind=kLoop, calls=%fused_computation.40 | loop fusion | flops 2097152 | bytes 2109440 | tf_op jit(solution)/shard_map/eq | solution.py:111
  7.4 3.0 %fusion.20 = f32[1024,388]{0,1:T(8,128)S(1)} fusion(pred[1024,1024]{1,0:T(32,128)(4,1)S(1)} %get-tuple-element.39, pred[1024,1024]{1,0:T(32,128)(4,1)S(1)} %get-tuple-element.38, bf16[1024,1]{0,1:T(2,128)(2,1)S(1)} %fusion.77, bf16[1024,1]{0,1:T(2,128)(2,1)S(1)} %get-tuple-element.14, bf16[1024,2]{0,1:T(2,128)(2,1)S(1)} %broadcast_in_dim.13, ...), kind=kOutput, calls=%fused_computation.28 | convolution fusion | flops 1642201088 | bytes 5267456 | tf_op jit(solution)/shard_map/dot_general | solution.py:113
  10.5 0.1 slice_add_fusion
  10.6 0.2 copy.98
  10.8 0.3 reshape.411
  11.1 0.2 copy.97
  11.3 0.1 reshape.410
  11.5 1.3 %copy.99 = f32[32,1,4160]{2,1,0:T(1,128)} copy(f32[32,1,4160]{2,0,1:T(8,128)S(1)} %maximum_bitcast_fusion) | data formatting | bytes 1064960 | tf_op jit(solution)/shard_map/all_to_all | solution.py:120
  12.8 7.5 %all-to-all-start = ((f32[32,1,4160]{2,1,0:T(1,128)}), f32[32,1,4160]{2,1,0:T(1,128)S(1)}, u32[]{:S(2)}, u32[]{:S(2)}) async-start(f32[32,1,4160]{2,1,0:T(1,128)} %copy.99), calls=%async_computation | async-start | bytes 1081344 | tf_op jit(solution)/shard_map/all_to_all | solution.py:120
  20.3 0.3 reshape.413
  20.6 0.3 subtract_bitcast_fusion
  20.9 0.2 copy.104
  21.1 0.1 copy.102
  21.2 0.1 broadcast_multiply_fusion.1
  21.4 0.4 broadcast_multiply_fusion
  21.8 1.3 %mul.380 = f32[512,128]{1,0:T(8,128)S(1)} reshape(f32[4,64,2,2,4,16]{5,4,3,2,1,0:T(4,128)S(1)} %broadcast_multiply_fusion) | data formatting | bytes 524288 | tf_op jit(solution)/shard_map/mul | solution.py:139
  23.2 0.3 fusion.47
  23.5 0.6 convert_add_fusion.1
  24.1 12.7 %all-to-all-done = f32[32,1,4160]{2,1,0:T(1,128)S(1)} async-done(((f32[32,1,4160]{2,1,0:T(1,128)}), f32[32,1,4160]{2,1,0:T(1,128)S(1)}, u32[]{:S(2)}, u32[]{:S(2)}) %all-to-all-start) | async-done | bytes 532512 | tf_op jit(solution)/shard_map/all_to_all | solution.py:120
  36.8 1.8 %copy.100 = f32[32,1,4160]{0,2,1:T(8,128)S(1)} copy(f32[32,1,4160]{2,1,0:T(1,128)S(1)} %all-to-all-done) | data formatting | bytes 1064960 | tf_op jit(solution)/shard_map/all_to_all | solution.py:120
  38.6 1.5 %slice.84 = f32[32,4096]{0,1:T(8,128)} slice(f32[32,4160]{0,1:T(8,128)S(1)} %bitcast.50), slice={[0:32], [0:4096]} | slice | bytes 1048576 | tf_op jit(solution)/shard_map/slice | solution.py:122
  40.1 0.1 copy.101
  40.2 0.1 sub.181
  40.2 1.0 %fusion.25 = f32[153,2048]{1,0:T(8,128)S(1)} fusion(s32[2048]{0:T(1024)S(1)} %sub.181, bf16[51,512]{1,0:T(8,128)(2,1)S(1)} %get-tuple-element.35, bf16[51,512]{1,0:T(8,128)(2,1)S(1)} %get-tuple-element.34, bf16[51,512]{1,0:T(8,128)(2,1)S(1)} %get-tuple-element.33), kind=kOutput, calls=%fused_computation.34 | convolution fusion | flops 322382848 | bytes 1418240 | tf_op jit(solution)/shard_map/dot_general | solution.py:132
  41.3 0.1 slice_add_fusion.2
  41.4 0.1 slice_reduce_fusion.2
  41.5 0.6 broadcast_compare_fusion.2
  42.1 0.6 copy.103
  42.7 0.1 reshape.412
  42.8 1.8 %fusion.88 = f32[512,1024]{1,0:T(8,128)S(1)} fusion(f32[512,128]{1,0:T(8,128)S(1)} %mul.380, f32[1024,128]{1,0:T(8,128)S(1)} %reshape.412), kind=kOutput, calls=%fused_computation.164 | convolution fusion | flops 805306368 | bytes 2883584 | tf_op jit(solution)/shard_map/dot_general | solution.py:141
  44.6 0.2 fusion.85
  44.9 0.3 squeeze.16
  45.2 0.3 squeeze.17
  45.5 0.3 squeeze.18
  45.8 0.3 squeeze.15
  46.2 0.9 %rsqrt_multiply_fusion = (f32[64,2,1024]{2,1,0:T(2,128)S(1)}, f32[64,2,1024]{2,1,0:T(2,128)S(1)}) fusion(f32[64,2,1024]{2,1,0:T(2,128)S(1)} %squeeze.15, f32[64]{0:T(128)S(1)} %copy-done.14, f32[64,2,1024]{2,1,0:T(2,128)S(1)} %squeeze.18, f32[2,1024]{1,0:T(2,128)S(1)} %sub.192, f32[64,2,1024]{2,1,0:T(2,128)S(1)} %squeeze.17, f32[2,1024]{1,0:T(2,128)S(1)} %sub.189, ...), kind=kLoop, calls=%fused_computation.75 | loop fusion | flops 1441792 | bytes 3170560 | tf_op jit(solution)/shard_map/mul | solution.py:52
  47.0 0.5 subtract_multiply_fusion.2
  47.5 0.1 mul.402
  47.6 0.1 mul.397
  47.7 0.1 mul.392
  48.0 0.2 copy-done.4
  48.2 0.2 subtract_multiply_fusion.1
  48.4 11.8 %fusion.18 = f32[16,2,1024]{2,0,1:T(8,128)S(1)} fusion(f32[64,2,1024]{2,1,0:T(2,128)S(1)} %get-tuple-element.13, f32[16,2,1024]{2,0,1:T(8,128)S(1)} %copy.108, f32[16,2,1024]{2,0,1:T(8,128)S(1)} %bitcast.63, f32[64,2,1024]{2,1,0:T(2,128)S(1)} %bitcast.56, f32[16,2,1024]{2,0,1:T(8,128)S(1)} %bitcast.64, f32[64,2,1024]{2,1,0:T(2,128)S(1)} %bitcast.55, ...), kind=kLoop, calls=%fused_computation.26 | loop fusion | flops 90144768 | bytes 3276800 | tf_op jit(solution)/shard_map/reduce_sum | solution.py:63
  60.3 0.9 %fusion.24 = f32[48,512]{1,0:T(8,128)S(1)} fusion(s32[2048]{0:T(1024)S(1)} %copy-done.7, bf16[16,2048]{1,0:T(8,128)(2,1)S(1)} %get-tuple-element.31, bf16[16,2048]{1,0:T(8,128)(2,1)S(1)} %get-tuple-element.32, bf16[16,2048]{1,0:T(8,128)(2,1)S(1)} %get-tuple-element.30), kind=kOutput, calls=%fused_computation.33 | convolution fusion | flops 102301696 | bytes 303104 | tf_op jit(solution)/shard_map/dot_general | solution.py:148
  61.2 0.5 fusion.29
  61.7 0.2 copy.110
  61.9 0.2 all_to_all.19
  62.2 9.4 %all_to_all.22 = f32[32,1,512]{2,1,0:T(1,128)S(1)} all-to-all(f32[32,1,512]{2,1,0:T(1,128)S(1)} %all_to_all.19), channel_id=1, replica_groups=mesh['grp'=4,'dev'=8] {'grp','dev'}, dimensions={0} | all-to-all | bytes 131072 | tf_op jit(solution)/shard_map/all_to_all | solution.py:160
  71.6 0.6 copy.129
  (60 shorter events, 0.6 us)
Async XLA Ops:
  2.9 1.9 %copy-start.10 = (s32[512,2]{0,1:T(2,128)S(1)}, s32[512,2]{0,1:T(2,128)}, u32[]{:S(2)}) copy-start(s32[512,2]{0,1:T(2,128)} %param.11) | copy-start | bytes 12292
  3.4 2.3 %copy-start.11 = (s32[512,2]{0,1:T(2,128)S(1)}, s32[512,2]{0,1:T(2,128)}, u32[]{:S(2)}) copy-start(s32[512,2]{0,1:T(2,128)} %param.12) | copy-start | bytes 12292
  4.9 2.5 %copy-start.1 = (bf16[1024,3,2,64]{0,3,2,1:T(8,128)(2,1)S(1)}, bf16[1024,3,2,64]{0,3,2,1:T(8,128)(2,1)}, u32[]{:S(2)}) copy-start(bf16[1024,3,2,64]{0,3,2,1:T(8,128)(2,1)} %get-tuple-element.28) | copy-start | bytes 2359300
  11.3 9.0 %copy-start.2 = (f32[3,8192]{1,0:T(4,128)S(1)}, f32[3,8192]{1,0:T(4,128)}, u32[]{:S(2)}) copy-start(f32[3,8192]{1,0:T(4,128)} %param.14) | copy-start | bytes 294916
  11.4 9.2 %copy-start.5 = (f32[3,512]{1,0:T(4,128)S(1)}, f32[3,512]{1,0:T(4,128)}, u32[]{:S(2)}) copy-start(f32[3,512]{1,0:T(4,128)} %param.13) | copy-start | bytes 18436
  12.8 8.3 %copy-start.9 = (f32[64,16]{0,1:T(8,128)S(1)}, f32[64,16]{0,1:T(8,128)}, u32[]{:S(2)}) copy-start(f32[64,16]{0,1:T(8,128)} %param.16) | copy-start | bytes 12292
  12.8 24.0 %all-to-all-start = ((f32[32,1,4160]{2,1,0:T(1,128)}), f32[32,1,4160]{2,1,0:T(1,128)S(1)}, u32[]{:S(2)}, u32[]{:S(2)}) async-start(f32[32,1,4160]{2,1,0:T(1,128)} %copy.99), calls=%async_computation | async-start | bytes 1081344 | tf_op jit(solution)/shard_map/all_to_all | solution.py:120
  21.4 1.8 %copy-start.12 = (s32[512,1]{0,1:T(1,128)S(1)}, s32[512,1]{0,1:T(1,128)}, u32[]{:S(2)}) copy-start(s32[512,1]{0,1:T(1,128)} %param.15) | copy-start | bytes 6148
  40.2 1.3 %copy-start.6 = (s32[2048]{0:T(1024)}, s32[2048]{0:T(1024)S(1)}, u32[]{:S(2)}) copy-start(s32[2048]{0:T(1024)S(1)} %sub.181) | copy-start | bytes 24580
  40.2 1.9 %copy-start = (f32[32,4096]{0,1:T(8,128)S(1)}, f32[32,4096]{0,1:T(8,128)}, u32[]{:S(2)}) copy-start(f32[32,4096]{0,1:T(8,128)} %slice.84) | copy-start | bytes 1572868
  42.1 4.0 %copy-start.3 = (f32[2,1024]{1,0:T(2,128)}, f32[2,1024]{1,0:T(2,128)S(1)}, u32[]{:S(2)}) copy-start(f32[2,1024]{1,0:T(2,128)S(1)} %sub.192) | copy-start | bytes 24580
  44.9 1.3 %copy-start.14 = (f32[64]{0:T(128)S(1)}, f32[64]{0:T(128)}, u32[]{:S(2)}) copy-start(f32[64]{0:T(128)} %param.17) | copy-start | bytes 772
  47.5 0.7 copy-start.4
  48.4 11.8 %copy-start.8 = (pred[2048]{0:T(1024)(128)(4,1)S(1)}, pred[2048]{0:T(1024)(128)(4,1)}, u32[]{:S(2)}) copy-start(pred[2048]{0:T(1024)(128)(4,1)} %broadcast_compare_fusion.2) | copy-start | bytes 6148
  48.4 11.9 %copy-start.7 = (s32[2048]{0:T(1024)S(1)}, s32[2048]{0:T(1024)}, u32[]{:S(2)}) copy-start(s32[2048]{0:T(1024)} %copy-done.6) | copy-start | bytes 24580
  60.2 1.0 %copy-start.13 = (s32[512]{0:T(512)S(1)}, s32[512]{0:T(512)}, u32[]{:S(2)}) copy-start(s32[512]{0:T(512)} %convert_add_fusion.1) | copy-start | bytes 6148

commit v5 on v4

--- a/solution.py
+++ b/solution.py
@@ -93,26 +93,14 @@
     coarse_pairs = jnp.broadcast_to(coarse[:, None, :], (panels, fanout, width)).reshape(pairs, width)
     ids1 = crevice_centre.reshape(pairs) + 1
     id_parts = jnp.stack([ids1 // 16, ids1 % 16], axis=1).astype(BF)
-    parts = split3(coarse_pairs, 1).reshape(pairs, 3, 1, width)
-    none = jnp.zeros_like(parts)
-    none_id = jnp.zeros_like(id_parts)
-    rhs = jnp.concatenate(
-        [
-            jnp.concatenate([jnp.concatenate([parts, none], 2).reshape(pairs, 6 * width), id_parts, none_id], 1),
-            jnp.concatenate([jnp.concatenate([none, parts], 2).reshape(pairs, 6 * width), none_id, id_parts], 1),
-        ],
-        0,
-    )
+    rhs = jnp.concatenate([split3(coarse_pairs, 1), id_parts], axis=1)
 
     destination = crevice_routes.reshape(-1)
     slot_index = destination * capacity + route_rank(destination, devices)
-    row_slot = 2 * jnp.arange(slots // 2, dtype=jnp.int32)[:, None]
-    place = jnp.concatenate(
-        [(row_slot == slot_index[None, :]), (row_slot + 1 == slot_index[None, :])], axis=1
-    ).astype(BF)
+    place = (jnp.arange(slots, dtype=jnp.int32)[:, None] == slot_index[None, :]).astype(BF)
     placed = jnp.dot(place, rhs, preferred_element_type=F32)
-    payload = join3(placed[:, : 6 * width], 1)
-    slot_ids = 16.0 * placed[:, 6 * width :: 2] + placed[:, 6 * width + 1 :: 2]
+    payload = join3(placed[:, : 3 * width], 1)
+    slot_ids = 16.0 * placed[:, 3 * width] + placed[:, 3 * width + 1]
     outgoing = jnp.concatenate(
         [payload.reshape(devices, capacity * width), slot_ids.reshape(devices, capacity)], axis=1
     )

time: 72.6 us -> 69.3 us (0.955)
  local copies, waits for them, and re-layouts: 16.4 us -> 15 us
  matrix products: 7.99 us -> 7.03 us
  other arithmetic: 17.4 us -> 16.6 us
    eq x1 -> x0, other arithmetic: 1.32 us -> none  [per_device(): row_slot == slot_index[None, :]]
    dot_general x1, matrix products: 3 us -> 2.02 us  [per_device(): placed = jnp.dot(place, rhs, preferred_element_type=F32)]
    concatenate x1, local copies, waits for them, and re-layouts: 1.36 us -> 0.57 us  [per_device(): rhs = jnp.concatenate([split3(coarse_pairs, 1), id_parts], axis=1)]
    reshape x2, local copies, waits for them, and re-layouts: 0.98 us -> 0.23 us  [per_device(): density.reshape(panels, nodes)]
where the time goes in v5:
time: 69.3 us; the launch traced here: 68.9 us
  other arithmetic  16.6 us (24%)
  local copies, waits for them, and re-layouts  15 us (22%)
  waiting for transfers between devices  12.7 us (18%)
  blocking collectives  9.41 us (14%)
  starting transfers between devices  7.48 us (11%)
  matrix products  7.03 us (10%)
    all_to_all x1, waiting for transfers between devices, per_device(): lax.all_to_all(outgoing, ('grp', 'dev'), split_axis=0, concat_axis=0, til...  12.7 us
    reduce_sum x1, other arithmetic, expansion_terms(): return jnp.sum(scale[:, None] * t_next, axis=0)  11.8 us
    all_to_all x1, blocking collectives, per_device(): lax.all_to_all(sending, ('grp', 'dev'), split_axis=0, concat_axis=0, tile...  9.41 us
    all_to_all x1, starting transfers between devices, per_device(): lax.all_to_all(outgoing, ('grp', 'dev'), split_axis=0, concat_axis=0, til...  7.48 us
    all_to_all x2, local copies, waits for them, and re-layouts, per_device(): lax.all_to_all(outgoing, ('grp', 'dev'), split_axis=0, concat_axis=0, til...  3.12 us
    slice x2, local copies, waits for them, and re-layouts, per_device(): coarse_in = incoming[:, :capacity * width].reshape(slots // 2, 2 * width)  2.05 us
    dot_general x1, matrix products, per_device(): placed = jnp.dot(place, rhs, preferred_element_type=F32)  2.02 us
    dot_general x1, matrix products, per_device(): lax.dot_general(refine_w, coarse_in, (((1,), (1,)), ((), ())), precision=HI)  1.8 us
  transfers between devices with their start and end apart: 1, of which 1 were waited for; matrix products, arithmetic and copies ran while one was open for 5% of the time, Pallas kernels for 0%

profile of v5, /device:TPU:0, one launch (start us, length us, event | category | flops | bytes accessed | tf_op | source)
XLA Modules:
  0.0 68.9 jit_solution(14883609498314302054)
XLA Ops:
  0.0 0.7 %broadcast_add_fusion = s32[512,2]{0,1:T(2,128)S(1)} fusion(s32[512,2]{0,1:T(2,128)} %param.12), kind=kLoop, calls=%fused_computation.130 | loop fusion | flops 1024 | bytes 8192 | tf_op jit(solution)/shard_map/add | solution.py:94
  0.7 0.1 copy.79
  0.9 0.2 add.203
  1.1 0.2 copy.80
  1.3 1.2 %reshape.317 = f32[3,512,16]{2,1,0:T(8,128)S(1)} reshape(f32[3,8192]{1,0:T(4,128)} %param.9) | data formatting | bytes 196608 | tf_op jit(solution)/shard_map/reshape | solution.py:89
  2.5 0.2 copy.76
  2.7 0.1 reshape.319
  2.9 0.1 copy.77
  3.0 0.1 copy.78
  3.1 0.2 broadcast_in_dim.10
  3.3 0.1 fusion.32
  3.5 0.2 copy.81
  3.7 0.1 copy.75
  3.8 0.2 reshape.316
  4.0 0.5 fusion.29
  4.6 0.6 concatenate.28
  5.2 2.0 %fusion.20 = f32[2048,194]{0,1:T(8,128)S(1)} fusion(bf16[1024,194]{1,0:T(8,128)(2,1)S(1)} %concatenate.28, s32[1024]{0:T(1024)S(1)} %convert_add_fusion), kind=kOutput, calls=%fused_computation.29 | convolution fusion | flops 815792128 | bytes 1990656 | tf_op jit(solution)/shard_map/dot_general | solution.py:101
  7.2 0.1 slice_add_fusion
  7.3 0.3 copy.82
  7.7 0.4 reshape.321
  8.0 0.1 add.209
  8.1 1.4 %copy.83 = f32[32,1,4160]{2,1,0:T(1,128)} copy(f32[32,1,4160]{2,0,1:T(8,128)S(1)} %maximum_bitcast_fusion) | data formatting | bytes 1064960 | tf_op jit(solution)/shard_map/all_to_all | solution.py:108
  9.5 7.5 %all-to-all-start = ((f32[32,1,4160]{2,1,0:T(1,128)}), f32[32,1,4160]{2,1,0:T(1,128)S(1)}, u32[]{:S(2)}, u32[]{:S(2)}) async-start(f32[32,1,4160]{2,1,0:T(1,128)} %copy.83), calls=%async_computation | async-start | bytes 1081344 | tf_op jit(solution)/shard_map/all_to_all | solution.py:108
  17.0 0.3 reshape.323
  17.3 0.3 subtract_bitcast_fusion
  17.6 0.2 copy.88
  17.8 0.1 copy.86
  17.9 0.1 broadcast_multiply_fusion.1
  18.1 0.0 copy-start.11
  18.1 0.4 broadcast_multiply_fusion
  18.5 1.3 %mul.364 = f32[512,128]{1,0:T(8,128)S(1)} reshape(f32[4,64,2,2,4,16]{5,4,3,2,1,0:T(4,128)S(1)} %broadcast_multiply_fusion) | data formatting | bytes 524288 | tf_op jit(solution)/shard_map/mul | solution.py:127
  19.9 0.3 fusion.30
  20.2 0.6 convert_add_fusion.1
  20.8 12.7 %all-to-all-done = f32[32,1,4160]{2,1,0:T(1,128)S(1)} async-done(((f32[32,1,4160]{2,1,0:T(1,128)}), f32[32,1,4160]{2,1,0:T(1,128)S(1)}, u32[]{:S(2)}, u32[]{:S(2)}) %all-to-all-start) | async-done | bytes 532512 | tf_op jit(solution)/shard_map/all_to_all | solution.py:108
  33.5 1.8 %copy.84 = f32[32,1,4160]{0,2,1:T(8,128)S(1)} copy(f32[32,1,4160]{2,1,0:T(1,128)S(1)} %all-to-all-done) | data formatting | bytes 1064960 | tf_op jit(solution)/shard_map/all_to_all | solution.py:108
  35.3 1.5 %slice.86 = f32[32,4096]{0,1:T(8,128)} slice(f32[32,4160]{0,1:T(8,128)S(1)} %bitcast.41), slice={[0:32], [0:4096]} | slice | bytes 1048576 | tf_op jit(solution)/shard_map/slice | solution.py:110
  36.8 0.1 copy.85
  36.9 0.1 sub.153
  36.9 1.0 %fusion.22 = f32[153,2048]{1,0:T(8,128)S(1)} fusion(s32[2048]{0:T(1024)S(1)} %sub.153, bf16[51,512]{1,0:T(8,128)(2,1)S(1)} %get-tuple-element.33, bf16[51,512]{1,0:T(8,128)(2,1)S(1)} %get-tuple-element.32, bf16[51,512]{1,0:T(8,128)(2,1)S(1)} %get-tuple-element.31), kind=kOutput, calls=%fused_computation.32 | convolution fusion | flops 322382848 | bytes 1418240 | tf_op jit(solution)/shard_map/dot_general | solution.py:120
  38.0 0.1 slice_add_fusion.2
  38.1 0.1 slice_reduce_fusion.2
  38.2 0.6 broadcast_compare_fusion
  38.8 0.6 copy.87
  39.4 0.1 reshape.322
  39.5 1.8 %fusion.66 = f32[512,1024]{1,0:T(8,128)S(1)} fusion(f32[512,128]{1,0:T(8,128)S(1)} %mul.364, f32[1024,128]{1,0:T(8,128)S(1)} %reshape.322), kind=kOutput, calls=%fused_computation.139 | convolution fusion | flops 805306368 | bytes 2883584 | tf_op jit(solution)/shard_map/dot_general | solution.py:129
  41.3 0.2 fusion.64
  41.6 0.3 squeeze.18
  41.9 0.3 squeeze.19
  42.2 0.3 squeeze.20
  42.5 0.3 squeeze.8
  42.9 0.9 %rsqrt_multiply_fusion = (f32[64,2,1024]{2,1,0:T(2,128)S(1)}, f32[64,2,1024]{2,1,0:T(2,128)S(1)}) fusion(f32[64,2,1024]{2,1,0:T(2,128)S(1)} %squeeze.8, f32[64]{0:T(128)S(1)} %copy-done.13, f32[64,2,1024]{2,1,0:T(2,128)S(1)} %squeeze.20, f32[2,1024]{1,0:T(2,128)S(1)} %sub.164, f32[64,2,1024]{2,1,0:T(2,128)S(1)} %squeeze.19, f32[2,1024]{1,0:T(2,128)S(1)} %sub.161, ...), kind=kLoop, calls=%fused_computation.56 | loop fusion | flops 1441792 | bytes 3170560 | tf_op jit(solution)/shard_map/mul | solution.py:52
  43.7 0.5 subtract_multiply_fusion.2
  44.2 0.1 mul.386
  44.3 0.1 mul.381
  44.4 0.1 mul.376
  44.7 0.2 copy-done.3
  44.9 0.2 subtract_multiply_fusion.1
  45.1 11.8 %fusion.18 = f32[16,2,1024]{2,0,1:T(8,128)S(1)} fusion(f32[64,2,1024]{2,1,0:T(2,128)S(1)} %get-tuple-element.13, f32[16,2,1024]{2,0,1:T(8,128)S(1)} %copy.92, f32[16,2,1024]{2,0,1:T(8,128)S(1)} %get-tuple-element.36, f32[64,2,1024]{2,1,0:T(2,128)S(1)} %bitcast.47, f32[16,2,1024]{2,0,1:T(8,128)S(1)} %get-tuple-element.37, f32[64,2,1024]{2,1,0:T(2,128)S(1)} %bitcast.46, ...), kind=kLoop, calls=%fused_computation.26 | loop fusion | flops 90144768 | bytes 3276800 | tf_op jit(solution)/shard_map/reduce_sum | solution.py:63
  57.0 0.9 %fusion.21 = f32[48,512]{1,0:T(8,128)S(1)} fusion(s32[2048]{0:T(1024)S(1)} %copy-done.7, bf16[16,2048]{1,0:T(8,128)(2,1)S(1)} %get-tuple-element.29, bf16[16,2048]{1,0:T(8,128)(2,1)S(1)} %get-tuple-element.30, bf16[16,2048]{1,0:T(8,128)(2,1)S(1)} %get-tuple-element.28), kind=kOutput, calls=%fused_computation.31 | convolution fusion | flops 102301696 | bytes 303104 | tf_op jit(solution)/shard_map/dot_general | solution.py:136
  57.9 0.5 fusion.27
  58.4 0.2 copy.94
  58.6 0.2 all_to_all.19
  58.9 9.4 %all_to_all.22 = f32[32,1,512]{2,1,0:T(1,128)S(1)} all-to-all(f32[32,1,512]{2,1,0:T(1,128)S(1)} %all_to_all.19), channel_id=1, replica_groups=mesh['grp'=4,'dev'=8] {'grp','dev'}, dimensions={0} | all-to-all | bytes 131072 | tf_op jit(solution)/shard_map/all_to_all | solution.py:148
  68.3 0.6 copy.105
  (51 shorter events, 0.5 us)
Async XLA Ops:
  0.0 2.7 %copy-start.5 = (f32[8192]{0:T(1024)S(1)}, f32[8192]{0:T(1024)}, u32[]{:S(2)}) copy-start(f32[8192]{0:T(1024)} %param.10) | copy-start | bytes 98308
  2.5 1.2 %copy-start.10 = (s32[512,2]{0,1:T(2,128)S(1)}, s32[512,2]{0,1:T(2,128)}, u32[]{:S(2)}) copy-start(s32[512,2]{0,1:T(2,128)} %param.11) | copy-start | bytes 12292
  7.6 9.4 %copy-start.1 = (f32[3,8192]{1,0:T(4,128)S(1)}, f32[3,8192]{1,0:T(4,128)}, u32[]{:S(2)}) copy-start(f32[3,8192]{1,0:T(4,128)} %param.14) | copy-start | bytes 294916
  8.0 9.3 %copy-start.4 = (f32[3,512]{1,0:T(4,128)S(1)}, f32[3,512]{1,0:T(4,128)}, u32[]{:S(2)}) copy-start(f32[3,512]{1,0:T(4,128)} %param.13) | copy-start | bytes 18436
  9.5 8.3 %copy-start.9 = (f32[64,16]{0,1:T(8,128)S(1)}, f32[64,16]{0,1:T(8,128)}, u32[]{:S(2)}) copy-start(f32[64,16]{0,1:T(8,128)} %param.16) | copy-start | bytes 12292
  9.5 24.0 %all-to-all-start = ((f32[32,1,4160]{2,1,0:T(1,128)}), f32[32,1,4160]{2,1,0:T(1,128)S(1)}, u32[]{:S(2)}, u32[]{:S(2)}) async-start(f32[32,1,4160]{2,1,0:T(1,128)} %copy.83), calls=%async_computation | async-start | bytes 1081344 | tf_op jit(solution)/shard_map/all_to_all | solution.py:108
  18.1 1.8 %copy-start.11 = (s32[512,1]{0,1:T(1,128)S(1)}, s32[512,1]{0,1:T(1,128)}, u32[]{:S(2)}) copy-start(s32[512,1]{0,1:T(1,128)} %param.15) | copy-start | bytes 6148
  36.9 1.3 %copy-start.6 = (s32[2048]{0:T(1024)}, s32[2048]{0:T(1024)S(1)}, u32[]{:S(2)}) copy-start(s32[2048]{0:T(1024)S(1)} %sub.153) | copy-start | bytes 24580
  36.9 1.9 %copy-start = (f32[32,4096]{0,1:T(8,128)S(1)}, f32[32,4096]{0,1:T(8,128)}, u32[]{:S(2)}) copy-start(f32[32,4096]{0,1:T(8,128)} %slice.86) | copy-start | bytes 1572868
  38.8 4.0 %copy-start.2 = (f32[2,1024]{1,0:T(2,128)}, f32[2,1024]{1,0:T(2,128)S(1)}, u32[]{:S(2)}) copy-start(f32[2,1024]{1,0:T(2,128)S(1)} %sub.164) | copy-start | bytes 24580
  41.6 1.3 %copy-start.13 = (f32[64]{0:T(128)S(1)}, f32[64]{0:T(128)}, u32[]{:S(2)}) copy-start(f32[64]{0:T(128)} %param.17) | copy-start | bytes 772
  44.2 0.7 %copy-start.3 = (f32[2,1024]{1,0:T(2,128)S(1)}, f32[2,1024]{1,0:T(2,128)}, u32[]{:S(2)}) copy-start(f32[2,1024]{1,0:T(2,128)} %copy-done.2) | copy-start | bytes 24580
  45.1 11.8 %copy-start.8 = (pred[2048]{0:T(1024)(128)(4,1)S(1)}, pred[2048]{0:T(1024)(128)(4,1)}, u32[]{:S(2)}) copy-start(pred[2048]{0:T(1024)(128)(4,1)} %broadcast_compare_fusion) | copy-start | bytes 6148
  45.1 11.9 %copy-start.7 = (s32[2048]{0:T(1024)S(1)}, s32[2048]{0:T(1024)}, u32[]{:S(2)}) copy-start(s32[2048]{0:T(1024)} %copy-done.6) | copy-start | bytes 24580
  56.9 1.0 %copy-start.12 = (s32[512]{0:T(512)S(1)}, s32[512]{0:T(512)}, u32[]{:S(2)}) copy-start(s32[512]{0:T(512)} %convert_add_fusion.1) | copy-start | bytes 6148

commit v6 on v5

--- a/solution.py
+++ b/solution.py
@@ -42,10 +42,10 @@
 
 def expansion_terms(fine, strength, centre_pos, rel_targets):
     mu, gamma = clenshaw_constants(ORDER)
-    ax = fine[0] - centre_pos[0][None]
-    ay = fine[1] - centre_pos[1][None]
-    az = fine[2] - centre_pos[2][None]
-    bx, by, bz = rel_targets[0], rel_targets[1], rel_targets[2]
+    ax = fine[:, 0] - centre_pos[:, 0][:, None]
+    ay = fine[:, 1] - centre_pos[:, 1][:, None]
+    az = fine[:, 2] - centre_pos[:, 2][:, None]
+    bx, by, bz = rel_targets[:, 0], rel_targets[:, 1], rel_targets[:, 2]
     rs2 = ax * ax + ay * ay + az * az
     rt2 = bx * bx + by * by + bz * bz
     inv_rs2 = 1.0 / rs2
@@ -53,14 +53,14 @@
     ax = ax * inv_rs2
     ay = ay * inv_rs2
     az = az * inv_rs2
-    w = ax[:, None] * bx[None] + ay[:, None] * by[None] + az[:, None] * bz[None]
-    rho2 = rt2[None] * inv_rs2[:, None]
+    w = ax[:, :, None] * bx[:, None] + ay[:, :, None] * by[:, None] + az[:, :, None] * bz[:, None]
+    rho2 = rt2[:, None] * inv_rs2[:, :, None]
     t_next = w + (1.0 / mu[ORDER - 1])
     t_after = jnp.ones_like(w)
     for level in range(ORDER - 2, -1, -1):
         t_now = (w * t_next + (1.0 / mu[level])) - gamma[level] * (rho2 * t_after)
         t_after, t_next = (t_next, t_now)
-    return jnp.sum(scale[:, None] * t_next, axis=0)
+    return jnp.sum(scale[:, :, None] * t_next, axis=1)
 
 
 def per_device(
@@ -102,39 +102,51 @@
     payload = join3(placed[:, : 3 * width], 1)
     slot_ids = 16.0 * placed[:, 3 * width] + placed[:, 3 * width + 1]
     outgoing = jnp.concatenate(
-        [payload.reshape(devices, capacity * width), slot_ids.reshape(devices, capacity)], axis=1
+        [
+            payload.reshape(devices, capacity * width),
+            slot_ids.reshape(devices, capacity),
+            jnp.zeros((devices, 2 * width - capacity), F32),
+        ],
+        axis=1,
     )
 
     incoming = lax.all_to_all(outgoing, ("grp", "dev"), split_axis=0, concat_axis=0, tiled=True)
 
-    coarse_in = incoming[:, : capacity * width].reshape(slots // 2, 2 * width)
-    ids = jnp.round(incoming[:, capacity * width :]).astype(jnp.int32)
-    ids = ids.reshape(devices, capacity // 2, 2).transpose(2, 0, 1).reshape(slots) - 1
+    rows = capacity // 2
+    block = incoming.reshape(devices, rows + 1, 2 * width)
+    coarse_in = block[:, :rows, :].reshape(slots // 2, 2 * width)
+    ids = jnp.round(block[:, rows, :capacity]).astype(jnp.int32)
+    ids = ids.reshape(devices, rows, 2).transpose(2, 0, 1).reshape(2, slots // 2) - 1
     valid = ids >= 0
-    pick = (jnp.arange(centre_count, dtype=jnp.int32)[:, None] == ids[None, :]).astype(BF)
+    pick = (jnp.arange(centre_count, dtype=jnp.int32)[None, :, None] == ids[:, None, :]).astype(BF)
 
     rel = targets.reshape(3, centre_count, nodes) - centres[:, :, None]
+    data_rows = 3 + 3 * nodes
+    padded_rows = -(-data_rows // 8) * 8
     centre_data = jnp.concatenate(
-        [centres, rel.transpose(0, 2, 1).reshape(3 * nodes, centre_count)], axis=0
+        [
+            centres,
+            rel.transpose(0, 2, 1).reshape(3 * nodes, centre_count),
+            jnp.zeros((padded_rows - data_rows, centre_count), F32),
+        ],
+        axis=0,
     )
-    gathered = join3(jnp.dot(split3(centre_data, 0), pick, preferred_element_type=F32), 0)
-    slot_centre = gathered[:3].reshape(3, 2, slots // 2)
-    slot_targets = gathered[3:].reshape(3, nodes, 2, slots // 2)
+    gathered = join3(jnp.einsum("fg,pgs->pfs", split3(centre_data, 0), pick, preferred_element_type=F32), 1)
+    slot_centre = gathered[:, :3]
+    slot_targets = gathered[:, 3:data_rows].reshape(2, 3, nodes, slots // 2)
 
     eye_c = jnp.eye(4, dtype=F32)
     eye_p = jnp.eye(2, dtype=F32)
     refine_w = (
-        eye_c[:, None, None, None, :, None] * upsample[None, :, None, None, None, :] * eye_p[None, None, :, :, None, None]
-    ).reshape(4 * fine_count * 2, 2 * width)
+        eye_p[:, None, None, :, None, None] * eye_c[None, :, None, None, :, None] * upsample[None, None, :, None, None, :]
+    ).reshape(2 * 4 * fine_count, 2 * width)
     upper = lax.dot_general(refine_w, coarse_in, (((1,), (1,)), ((), ())), precision=HI)
-    upper = upper.reshape(4, fine_count, 2, slots // 2)
-    strength = upper[3] * fine_weights[:, None, None]
-    terms = expansion_terms(upper[:3], strength, slot_centre, slot_targets).reshape(nodes, slots)
-    terms = jnp.where(valid[None, :], terms, 0.0)
+    upper = upper.reshape(2, 4, fine_count, slots // 2)
+    strength = upper[:, 3] * fine_weights[None, :, None]
+    terms = expansion_terms(upper[:, :3], strength, slot_centre, slot_targets)
+    terms = jnp.where(valid[:, None, :], terms, 0.0)
 
-    potential = join3(
-        lax.dot_general(split3(terms, 0), pick, (((1,), (1,)), ((), ())), preferred_element_type=F32), 0
-    )
+    potential = join3(jnp.einsum("pks,pgs->kg", split3(terms, 1), pick, preferred_element_type=F32), 0)
 
     home = centre_home.reshape(-1)
     back_index = home * capacity_back + route_rank(home, devices)

time: 69.3 us -> 63.1 us (0.911)
  local copies, waits for them, and re-layouts: 15 us -> 8.17 us
  waiting for transfers between devices: 12.7 us -> 14.8 us
  other arithmetic: 16.6 us -> 15.4 us
    slice x5 -> x4, local copies, waits for them, and re-layouts: 2.39 us -> 0.12 us  [the longest x1 0.05 us: per_device(): coarse_in = block[:, :rows, :].reshape(slots // 2, 2 * width)]
    all_to_all x1, waiting for transfers between devices: 12.7 us -> 14.8 us  [per_device(): lax.all_to_all(outgoing, ('grp', 'dev'), split_axis=0, concat_axis=0, til...]
    all_to_all x2 -> x1, local copies, waits for them, and re-layouts: 3.12 us -> 1.35 us  [per_device(): lax.all_to_all(outgoing, ('grp', 'dev'), split_axis=0, concat_axis=0, til...]
    mul x6 -> x4, local copies, waits for them, and re-layouts: 1.68 us -> 0.25 us  [per_device(): eye_p[:, None, None, :, None, None] * eye_c[None, :, None, None, :, None]]
    all_to_all x1, other arithmetic: 0.04 us -> 1.28 us  [per_device(): lax.all_to_all(outgoing, ('grp', 'dev'), split_axis=0, concat_axis=0, til...]
    squeeze x4 -> x0, local copies, waits for them, and re-layouts: 1.22 us -> none  [the longest x1 0.31 us: expansion_terms(): ax = fine[0] - centre_pos[0][None]]
  transfers between devices with their start and end apart: 1 -> 1, of which waited for: 1 -> 1; matrix products, arithmetic and copies ran while one was open for 5% -> 3% of each run, Pallas kernels for 0% -> 0%
where the time goes in v6:
time: 63.1 us; the launch traced here: 62.8 us
  other arithmetic  15.4 us (24%)
  waiting for transfers between devices  14.8 us (23%)
  blocking collectives  9.41 us (15%)
  local copies, waits for them, and re-layouts  8.17 us (13%)
  starting transfers between devices  7.48 us (12%)
  matrix products  6.97 us (11%)
    all_to_all x1, waiting for transfers between devices, per_device(): lax.all_to_all(outgoing, ('grp', 'dev'), split_axis=0, concat_axis=0, til...  14.8 us
    reduce_sum x1, other arithmetic, expansion_terms(): return jnp.sum(scale[:, :, None] * t_next, axis=1)  11.8 us
    all_to_all x1, blocking collectives, per_device(): lax.all_to_all(sending, ('grp', 'dev'), split_axis=0, concat_axis=0, tile...  9.41 us
    all_to_all x1, starting transfers between devices, per_device(): lax.all_to_all(outgoing, ('grp', 'dev'), split_axis=0, concat_axis=0, til...  7.48 us
    dot_general x1, matrix products, per_device(): placed = jnp.dot(place, rhs, preferred_element_type=F32)  2.02 us
    dot_general x1, matrix products, per_device(): lax.dot_general(refine_w, coarse_in, (((1,), (1,)), ((), ())), precision=HI)  1.8 us
    all_to_all x1, local copies, waits for them, and re-layouts, per_device(): lax.all_to_all(outgoing, ('grp', 'dev'), split_axis=0, concat_axis=0, til...  1.35 us
    all_to_all x1, other arithmetic, per_device(): lax.all_to_all(outgoing, ('grp', 'dev'), split_axis=0, concat_axis=0, til...  1.28 us
  transfers between devices with their start and end apart: 1, of which 1 were waited for; matrix products, arithmetic and copies ran while one was open for 3% of the time, Pallas kernels for 0%

profile of v6, /device:TPU:0, one launch (start us, length us, event | category | flops | bytes accessed | tf_op | source)
XLA Modules:
  0.0 62.8 jit_solution(11825516712675792890)
XLA Ops:
  0.0 0.7 %broadcast_add_fusion = s32[512,2]{0,1:T(2,128)S(1)} fusion(s32[512,2]{0,1:T(2,128)} %param.12), kind=kLoop, calls=%fused_computation.141 | loop fusion | flops 1024 | bytes 8192 | tf_op jit(solution)/shard_map/add | solution.py:94
  0.7 0.1 copy.87
  0.9 0.2 add.197
  1.1 0.2 copy.88
  1.3 1.2 %reshape.279 = f32[3,512,16]{2,1,0:T(8,128)S(1)} reshape(f32[3,8192]{1,0:T(4,128)} %param.9) | data formatting | bytes 196608 | tf_op jit(solution)/shard_map/reshape | solution.py:89
  2.5 0.0 copy-start.4
  2.5 0.2 copy.84
  2.7 0.0 copy-done.2
  2.7 0.1 reshape.281
  2.9 0.1 copy.85
  3.0 0.1 copy.86
  3.1 0.2 broadcast_in_dim.14
  3.3 0.1 fusion.34
  3.5 0.2 copy.89
  3.7 0.0 copy-done.4
  3.7 0.1 copy.83
  3.8 0.2 reshape.278
  4.0 0.5 fusion.31
  4.6 0.6 concatenate.28
  5.2 2.0 %fusion.20 = f32[2048,194]{0,1:T(8,128)S(1)} fusion(bf16[1024,194]{1,0:T(8,128)(2,1)S(1)} %concatenate.28, s32[1024]{0:T(1024)S(1)} %convert_add_fusion.1), kind=kOutput, calls=%fused_computation.29 | convolution fusion | flops 815792128 | bytes 1990656 | tf_op jit(solution)/shard_map/dot_general | solution.py:101
  7.2 0.1 slice_add_fusion
  7.3 0.3 copy.90
  7.6 0.0 copy-start
  7.7 0.4 reshape.283
  8.0 0.1 add.203
  8.1 0.1 concatenate.29
  8.2 1.4 %copy.91 = f32[32,1,4224]{2,1,0:T(1,128)} copy(f32[32,1,4224]{2,0,1:T(8,128)S(1)} %bitcast.86) | data formatting | bytes 1081344 | tf_op jit(solution)/shard_map/all_to_all | solution.py:113
  9.5 7.5 %all-to-all-start = ((f32[32,1,4224]{2,1,0:T(1,128)}), f32[32,1,4224]{2,1,0:T(1,128)S(1)}, u32[]{:S(2)}, u32[]{:S(2)}) async-start(f32[32,1,4224]{2,1,0:T(1,128)} %copy.91), calls=%async_computation | async-start | bytes 1081344 | tf_op jit(solution)/shard_map/all_to_all | solution.py:113
  17.0 0.0 copy-done
  17.0 0.0 copy-start.5
  17.0 0.3 reshape.286
  17.3 0.0 copy-done.1
  17.3 0.3 subtract_bitcast_fusion
  17.6 0.2 copy.98
  17.8 0.0 copy-done.3
  17.9 0.1 copy.95
  18.0 0.1 broadcast_multiply_fusion
  18.0 0.1 mul.356
  18.1 0.1 mul.357
  18.2 0.1 pad.11.clone
  18.3 0.0 copy-done.5
  18.3 0.3 fusion.32
  18.6 0.1 reduce-precision_convert_fusion.5
  18.7 14.8 %all-to-all-done = f32[32,1,4224]{2,1,0:T(1,128)S(1)} async-done(((f32[32,1,4224]{2,1,0:T(1,128)}), f32[32,1,4224]{2,1,0:T(1,128)S(1)}, u32[]{:S(2)}, u32[]{:S(2)}) %all-to-all-start) | async-done | bytes 540704 | tf_op jit(solution)/shard_map/all_to_all | solution.py:113
  33.5 1.3 %reduce.1 = f32[32,4224]{1,0:T(8,128)S(1)} reduce(f32[32,1,4224]{2,1,0:T(1,128)S(1)} %all-to-all-done, f32[]{:T(128)} %constant.75), dimensions={1}, to_apply=%all_to_all.13.reduce_sub_computation | reduce | bytes 1081348 | tf_op jit(solution)/shard_map/all_to_all | solution.py:113
  34.8 0.1 reshape.284
  34.9 0.1 slice.75
  35.0 0.1 copy.93
  35.1 0.1 copy.94
  35.2 0.1 sub.153
  35.3 1.0 %fusion.28 = f32[2,168,1024]{2,1,0:T(8,128)S(1)} fusion(s32[2,1024]{1,0:T(2,128)S(1)} %sub.153, bf16[56,512]{1,0:T(8,128)(2,1)S(1)} %get-tuple-element.30, bf16[56,512]{1,0:T(8,128)(2,1)S(1)} %get-tuple-element.29, bf16[56,512]{1,0:T(8,128)(2,1)S(1)} %get-tuple-element.28), kind=kOutput, calls=%fused_computation.40 | convolution fusion | flops 353886208 | bytes 1556480 | tf_op jit(solution)/shard_map/fg,pgs->pfs/dot_general | solution.py:134
  36.2 0.1 slice_add_fusion.2
  36.3 0.0 copy-start.6
  36.4 1.8 %fusion.44 = f32[2,4,64,1024]{3,2,1,0:T(8,128)S(1)} fusion(f32[1024,128,1,1]{1,0,3,2:T(8,128)S(1)} %bitcast.88, f32[64,128]{1,0:T(8,128)S(1)} %copy.95, f32[2,4,128]{2,1,0:T(4,128)S(1)} %mul.357), kind=kOutput, calls=%fused_computation.73 | convolution fusion | flops 805371904 | bytes 2658304 | tf_op jit(solution)/shard_map/dot_general | solution.py:143
  38.2 0.0 copy-done.6
  38.3 0.3 fusion.40
  38.5 0.4 fusion.41
  39.0 11.8 %fusion.18 = f32[2,16,1024]{2,1,0:T(8,128)S(1)} fusion(f32[2,64,1024]{2,1,0:T(8,128)S(1)} %get-tuple-element.14, f32[2,16,1024]{2,1,0:T(8,128)S(1)} %get-tuple-element.22, f32[2,16,1024]{2,1,0:T(8,128)S(1)} %get-tuple-element.23, f32[2,64,1024]{2,1,0:T(8,128)S(1)} %get-tuple-element.12, f32[2,16,1024]{2,1,0:T(8,128)S(1)} %get-tuple-element.24, ...), kind=kLoop, calls=%fused_computation.26 | loop fusion | flops 90144768 | bytes 3276800 | tf_op jit(solution)/shard_map/reduce_sum | solution.py:63
  50.8 0.9 %fusion.30 = f32[48,512]{1,0:T(8,128)S(1)} fusion(s32[2,1024]{1,0:T(2,128)S(1)} %sub.153, bf16[2,16,1024]{2,1,0:T(8,128)(2,1)S(1)} %get-tuple-element.26, bf16[2,16,1024]{2,1,0:T(8,128)(2,1)S(1)} %get-tuple-element.27, bf16[2,16,1024]{2,1,0:T(8,128)(2,1)S(1)} %get-tuple-element.25), kind=kOutput, calls=%fused_computation.42 | convolution fusion | flops 102301696 | bytes 303104 | tf_op jit(solution)/shard_map/pks,pgs->kg/dot_general | solution.py:149
  51.7 0.5 fusion.27
  52.3 0.2 copy.100
  52.5 0.2 all_to_all.16
  52.7 9.4 %all_to_all.19 = f32[32,1,512]{2,1,0:T(1,128)S(1)} all-to-all(f32[32,1,512]{2,1,0:T(1,128)S(1)} %all_to_all.16), channel_id=1, replica_groups=mesh['grp'=4,'dev'=8] {'grp','dev'}, dimensions={0} | all-to-all | bytes 131072 | tf_op jit(solution)/shard_map/all_to_all | solution.py:160
  62.1 0.6 %copy.115 = f32[16384]{0:T(1024)} copy(f32[16384]{0:T(1024)S(1)} %bitcast.93) | data formatting | bytes 131072
  (26 shorter events, 0.4 us)
Async XLA Ops:
  0.0 2.7 %copy-start.2 = (f32[8192]{0:T(1024)S(1)}, f32[8192]{0:T(1024)}, u32[]{:S(2)}) copy-start(f32[8192]{0:T(1024)} %param.10) | copy-start | bytes 98308
  2.5 1.2 %copy-start.4 = (s32[512,2]{0,1:T(2,128)S(1)}, s32[512,2]{0,1:T(2,128)}, u32[]{:S(2)}) copy-start(s32[512,2]{0,1:T(2,128)} %param.11) | copy-start | bytes 12292
  7.6 9.4 %copy-start = (f32[3,8192]{1,0:T(4,128)S(1)}, f32[3,8192]{1,0:T(4,128)}, u32[]{:S(2)}) copy-start(f32[3,8192]{1,0:T(4,128)} %param.14) | copy-start | bytes 294916
  8.1 9.2 %copy-start.1 = (f32[3,512]{1,0:T(4,128)S(1)}, f32[3,512]{1,0:T(4,128)}, u32[]{:S(2)}) copy-start(f32[3,512]{1,0:T(4,128)} %param.13) | copy-start | bytes 18436
  9.5 8.3 %copy-start.3 = (f32[64,16]{0,1:T(8,128)S(1)}, f32[64,16]{0,1:T(8,128)}, u32[]{:S(2)}) copy-start(f32[64,16]{0,1:T(8,128)} %param.16) | copy-start | bytes 12292
  9.5 24.0 %all-to-all-start = ((f32[32,1,4224]{2,1,0:T(1,128)}), f32[32,1,4224]{2,1,0:T(1,128)S(1)}, u32[]{:S(2)}, u32[]{:S(2)}) async-start(f32[32,1,4224]{2,1,0:T(1,128)} %copy.91), calls=%async_computation | async-start | bytes 1081344 | tf_op jit(solution)/shard_map/all_to_all | solution.py:113
  17.0 1.3 %copy-start.5 = (s32[512,1]{0,1:T(1,128)S(1)}, s32[512,1]{0,1:T(1,128)}, u32[]{:S(2)}) copy-start(s32[512,1]{0,1:T(1,128)} %param.15) | copy-start | bytes 6148
  36.3 1.9 %copy-start.6 = (f32[64]{0:T(128)S(1)}, f32[64]{0:T(128)}, u32[]{:S(2)}) copy-start(f32[64]{0:T(128)} %param.17) | copy-start | bytes 772

commit v7 on v6

--- a/solution.py
+++ b/solution.py
@@ -90,12 +90,12 @@
          density.reshape(panels, nodes)],
         axis=1,
     )
-    coarse_pairs = jnp.broadcast_to(coarse[:, None, :], (panels, fanout, width)).reshape(pairs, width)
-    ids1 = crevice_centre.reshape(pairs) + 1
+    coarse_parts = jnp.concatenate([split3(coarse, 1)] * fanout, axis=0)
+    ids1 = jnp.concatenate([crevice_centre[:, t] for t in range(fanout)]) + 1
     id_parts = jnp.stack([ids1 // 16, ids1 % 16], axis=1).astype(BF)
-    rhs = jnp.concatenate([split3(coarse_pairs, 1), id_parts], axis=1)
+    rhs = jnp.concatenate([coarse_parts, id_parts], axis=1)
 
-    destination = crevice_routes.reshape(-1)
+    destination = jnp.concatenate([crevice_routes[:, t] for t in range(fanout)])
     slot_index = destination * capacity + route_rank(destination, devices)
     place = (jnp.arange(slots, dtype=jnp.int32)[:, None] == slot_index[None, :]).astype(BF)
     placed = jnp.dot(place, rhs, preferred_element_type=F32)

time: 63.1 us -> 61.7 us (0.978)
  other arithmetic: 15.4 us -> 14.6 us
    slice x0 -> x2, local copies, waits for them, and re-layouts: none -> 1.54 us  [the longest x1 0.77 us: per_device(): ids1 = jnp.concatenate([crevice_centre[:, t] for t in range(fanout)]) + 1]
    add x1 -> x0, other arithmetic: 0.7 us -> none  [per_device(): ids1 = crevice_centre.reshape(pairs) + 1]
    concatenate x2 -> x0, local copies, waits for them, and re-layouts: 0.69 us -> none  [the longest x1 0.57 us: per_device(): rhs = jnp.concatenate([split3(coarse_pairs, 1), id_parts], axis=1)]
where the time goes in v7:
time: 61.7 us; the launch traced here: 61.3 us
  waiting for transfers between devices  14.8 us (24%)
  other arithmetic  14.6 us (24%)
  blocking collectives  9.41 us (15%)
  local copies, waits for them, and re-layouts  7.78 us (13%)
  starting transfers between devices  7.48 us (12%)
  matrix products  6.8 us (11%)
    all_to_all x1, waiting for transfers between devices, per_device(): lax.all_to_all(outgoing, ('grp', 'dev'), split_axis=0, concat_axis=0, til...  14.8 us
    reduce_sum x1, other arithmetic, expansion_terms(): return jnp.sum(scale[:, :, None] * t_next, axis=1)  11.8 us
    all_to_all x1, blocking collectives, per_device(): lax.all_to_all(sending, ('grp', 'dev'), split_axis=0, concat_axis=0, tile...  9.41 us
    all_to_all x1, starting transfers between devices, per_device(): lax.all_to_all(outgoing, ('grp', 'dev'), split_axis=0, concat_axis=0, til...  7.48 us
    dot_general x1, matrix products, per_device(): placed = jnp.dot(place, rhs, preferred_element_type=F32)  1.87 us
    dot_general x1, matrix products, per_device(): lax.dot_general(refine_w, coarse_in, (((1,), (1,)), ((), ())), precision=HI)  1.8 us
    all_to_all x1, local copies, waits for them, and re-layouts, per_device(): lax.all_to_all(outgoing, ('grp', 'dev'), split_axis=0, concat_axis=0, til...  1.36 us
    all_to_all x1, other arithmetic, per_device(): lax.all_to_all(outgoing, ('grp', 'dev'), split_axis=0, concat_axis=0, til...  1.28 us
  transfers between devices with their start and end apart: 1, of which 1 were waited for; matrix products, arithmetic and copies ran while one was open for 3% of the time, Pallas kernels for 0%

profile of v7, /device:TPU:0, one launch (start us, length us, event | category | flops | bytes accessed | tf_op | source)
XLA Modules:
  0.0 61.3 jit_solution(5870794253964058509)
XLA Ops:
  0.0 0.0 copy-start.2
  0.0 0.8 %fusion.94 = (s32[512,1]{0,1:T(1,128)S(1)}, s32[512,1]{0,1:T(1,128)S(1)}) fusion(s32[512,2]{0,1:T(2,128)} %param.11), kind=kLoop, calls=%fused_computation.167 | loop fusion | bytes 8192 | tf_op jit(solution)/shard_map/slice | solution.py:98
  0.8 0.5 fusion.31
  1.3 0.8 %fusion.93 = (s32[512,1]{0,1:T(1,128)S(1)}, s32[512,1]{0,1:T(1,128)S(1)}) fusion(s32[512,2]{0,1:T(2,128)} %param.12), kind=kLoop, calls=%fused_computation.166 | loop fusion | bytes 8192 | tf_op jit(solution)/shard_map/slice | solution.py:94
  2.2 1.2 %reshape.307 = f32[3,512,16]{2,1,0:T(8,128)S(1)} reshape(f32[3,8192]{1,0:T(4,128)} %param.9) | data formatting | bytes 196608 | tf_op jit(solution)/shard_map/reshape | solution.py:89
  3.4 0.2 copy.65
  3.6 0.0 copy-done.2
  3.6 0.1 reshape.309
  3.7 0.1 copy.66
  3.9 1.9 %fusion.20 = f32[2048,194]{0,1:T(8,128)S(1)} fusion(s32[1024]{0:T(1024)S(1)} %convert_add_fusion.1, bf16[1024,1]{0,1:T(2,128)(2,1)S(1)} %fusion.85, bf16[1024,1]{0,1:T(2,128)(2,1)S(1)} %get-tuple-element.9, bf16[512,64]{0,1:T(8,128)(2,1)S(1)} %get-tuple-element.27, bf16[512,64]{0,1:T(8,128)(2,1)S(1)} %get-tuple-element.26, ...), kind=kOutput, calls=%fused_computation.29 | convolution fusion | flops 818970624 | bytes 1794048 | tf_op jit(solution)/shard_map/dot_general | solution.py:101
  5.7 0.1 slice_add_fusion
  5.9 0.3 copy.67
  6.2 0.0 copy-start
  6.2 0.4 reshape.310
  6.6 0.1 add.196
  6.6 0.0 copy-start.1
  6.7 0.1 concatenate.65
  6.7 1.4 %copy.68 = f32[32,1,4224]{2,1,0:T(1,128)} copy(f32[32,1,4224]{2,0,1:T(8,128)S(1)} %bitcast.86) | data formatting | bytes 1081344 | tf_op jit(solution)/shard_map/all_to_all | solution.py:113
  8.1 0.0 copy-start.3
  8.1 7.5 %all-to-all-start = ((f32[32,1,4224]{2,1,0:T(1,128)}), f32[32,1,4224]{2,1,0:T(1,128)S(1)}, u32[]{:S(2)}, u32[]{:S(2)}) async-start(f32[32,1,4224]{2,1,0:T(1,128)} %copy.68), calls=%async_computation | async-start | bytes 1081344 | tf_op jit(solution)/shard_map/all_to_all | solution.py:113
  15.6 0.0 copy-done
  15.6 0.0 copy-start.4
  15.6 0.3 reshape.313
  15.9 0.0 copy-done.1
  15.9 0.3 subtract_bitcast_fusion
  16.2 0.2 copy.75
  16.4 0.0 copy-done.3
  16.4 0.1 copy.72
  16.5 0.1 broadcast_multiply_fusion
  16.6 0.1 mul.356
  16.7 0.1 mul.357
  16.8 0.1 pad.11.clone
  16.9 0.0 copy-done.4
  16.9 0.3 fusion.32
  17.2 0.1 reduce-precision_convert_fusion.5
  17.3 14.8 %all-to-all-done = f32[32,1,4224]{2,1,0:T(1,128)S(1)} async-done(((f32[32,1,4224]{2,1,0:T(1,128)}), f32[32,1,4224]{2,1,0:T(1,128)S(1)}, u32[]{:S(2)}, u32[]{:S(2)}) %all-to-all-start) | async-done | bytes 540704 | tf_op jit(solution)/shard_map/all_to_all | solution.py:113
  32.1 1.3 %reduce.1 = f32[32,4224]{1,0:T(8,128)S(1)} reduce(f32[32,1,4224]{2,1,0:T(1,128)S(1)} %all-to-all-done, f32[]{:T(128)} %constant.75), dimensions={1}, to_apply=%all_to_all.13.reduce_sub_computation | reduce | bytes 1081348 | tf_op jit(solution)/shard_map/all_to_all | solution.py:113
  33.4 0.1 reshape.311
  33.5 0.1 slice.91
  33.6 0.1 copy.70
  33.6 0.1 copy.71
  33.7 0.1 sub.153
  33.8 1.0 %fusion.28 = f32[2,168,1024]{2,1,0:T(8,128)S(1)} fusion(s32[2,1024]{1,0:T(2,128)S(1)} %sub.153, bf16[56,512]{1,0:T(8,128)(2,1)S(1)} %get-tuple-element.30, bf16[56,512]{1,0:T(8,128)(2,1)S(1)} %get-tuple-element.29, bf16[56,512]{1,0:T(8,128)(2,1)S(1)} %get-tuple-element.28), kind=kOutput, calls=%fused_computation.40 | convolution fusion | flops 353886208 | bytes 1556480 | tf_op jit(solution)/shard_map/fg,pgs->pfs/dot_general | solution.py:134
  34.8 0.1 slice_add_fusion.2
  34.9 0.0 copy-start.5
  35.0 1.8 %fusion.58 = f32[2,4,64,1024]{3,2,1,0:T(8,128)S(1)} fusion(f32[1024,128,1,1]{1,0,3,2:T(8,128)S(1)} %bitcast.87, f32[64,128]{1,0:T(8,128)S(1)} %copy.72, f32[2,4,128]{2,1,0:T(4,128)S(1)} %mul.357), kind=kOutput, calls=%fused_computation.83 | convolution fusion | flops 805371904 | bytes 2658304 | tf_op jit(solution)/shard_map/dot_general | solution.py:143
  36.8 0.0 copy-done.5
  36.8 0.3 fusion.39
  37.1 0.4 fusion.40
  37.6 11.8 %fusion.18 = f32[2,16,1024]{2,1,0:T(8,128)S(1)} fusion(f32[2,64,1024]{2,1,0:T(8,128)S(1)} %get-tuple-element.14, f32[2,16,1024]{2,1,0:T(8,128)S(1)} %get-tuple-element.19, f32[2,16,1024]{2,1,0:T(8,128)S(1)} %get-tuple-element.20, f32[2,64,1024]{2,1,0:T(8,128)S(1)} %get-tuple-element.12, f32[2,16,1024]{2,1,0:T(8,128)S(1)} %get-tuple-element.21, ...), kind=kLoop, calls=%fused_computation.26 | loop fusion | flops 90144768 | bytes 3276800 | tf_op jit(solution)/shard_map/reduce_sum | solution.py:63
  49.4 0.9 %fusion.30 = f32[48,512]{1,0:T(8,128)S(1)} fusion(s32[2,1024]{1,0:T(2,128)S(1)} %sub.153, bf16[2,16,1024]{2,1,0:T(8,128)(2,1)S(1)} %get-tuple-element.23, bf16[2,16,1024]{2,1,0:T(8,128)(2,1)S(1)} %get-tuple-element.24, bf16[2,16,1024]{2,1,0:T(8,128)(2,1)S(1)} %get-tuple-element.22), kind=kOutput, calls=%fused_computation.42 | convolution fusion | flops 102301696 | bytes 303104 | tf_op jit(solution)/shard_map/pks,pgs->kg/dot_general | solution.py:149
  50.3 0.5 fusion.27
  50.8 0.2 copy.77
  51.0 0.2 all_to_all.16
  51.3 9.4 %all_to_all.19 = f32[32,1,512]{2,1,0:T(1,128)S(1)} all-to-all(f32[32,1,512]{2,1,0:T(1,128)S(1)} %all_to_all.16), channel_id=1, replica_groups=mesh['grp'=4,'dev'=8] {'grp','dev'}, dimensions={0} | all-to-all | bytes 131072 | tf_op jit(solution)/shard_map/all_to_all | solution.py:160
  60.7 0.6 %copy.92 = f32[16384]{0:T(1024)} copy(f32[16384]{0:T(1024)S(1)} %bitcast.92) | data formatting | bytes 131072
  (24 shorter events, 0.4 us)
Async XLA Ops:
  0.0 3.6 %copy-start.2 = (f32[8192]{0:T(1024)S(1)}, f32[8192]{0:T(1024)}, u32[]{:S(2)}) copy-start(f32[8192]{0:T(1024)} %param.10) | copy-start | bytes 98308
  6.2 9.4 %copy-start = (f32[3,8192]{1,0:T(4,128)S(1)}, f32[3,8192]{1,0:T(4,128)}, u32[]{:S(2)}) copy-start(f32[3,8192]{1,0:T(4,128)} %param.14) | copy-start | bytes 294916
  6.6 9.2 %copy-start.1 = (f32[3,512]{1,0:T(4,128)S(1)}, f32[3,512]{1,0:T(4,128)}, u32[]{:S(2)}) copy-start(f32[3,512]{1,0:T(4,128)} %param.13) | copy-start | bytes 18436
  8.1 8.3 %copy-start.3 = (f32[64,16]{0,1:T(8,128)S(1)}, f32[64,16]{0,1:T(8,128)}, u32[]{:S(2)}) copy-start(f32[64,16]{0,1:T(8,128)} %param.16) | copy-start | bytes 12292
  8.1 24.0 %all-to-all-start = ((f32[32,1,4224]{2,1,0:T(1,128)}), f32[32,1,4224]{2,1,0:T(1,128)S(1)}, u32[]{:S(2)}, u32[]{:S(2)}) async-start(f32[32,1,4224]{2,1,0:T(1,128)} %copy.68), calls=%async_computation | async-start | bytes 1081344 | tf_op jit(solution)/shard_map/all_to_all | solution.py:113
  15.6 1.3 %copy-start.4 = (s32[512,1]{0,1:T(1,128)S(1)}, s32[512,1]{0,1:T(1,128)}, u32[]{:S(2)}) copy-start(s32[512,1]{0,1:T(1,128)} %param.15) | copy-start | bytes 6148
  34.9 1.9 %copy-start.5 = (f32[64]{0:T(128)S(1)}, f32[64]{0:T(128)}, u32[]{:S(2)}) copy-start(f32[64]{0:T(128)} %param.17) | copy-start | bytes 772

commit v8 on v7

--- a/solution.py
+++ b/solution.py
@@ -23,6 +23,16 @@
     mid = lax.reduce_precision(rest, exponent_bits=8, mantissa_bits=7)
     lo = rest - mid
     return jnp.concatenate([hi, mid, lo], axis=axis).astype(BF)
+
+
+def split2(x, axis):
+    hi = lax.reduce_precision(x, exponent_bits=8, mantissa_bits=7)
+    return jnp.concatenate([hi, x - hi], axis=axis).astype(BF)
+
+
+def join2(y, axis):
+    a, b = jnp.split(y, 2, axis=axis)
+    return a + b
 
 
 def join3(y, axis):
@@ -131,7 +141,7 @@
         ],
         axis=0,
     )
-    gathered = join3(jnp.einsum("fg,pgs->pfs", split3(centre_data, 0), pick, preferred_element_type=F32), 1)
+    gathered = join2(jnp.einsum("fg,pgs->pfs", split2(centre_data, 0), pick, preferred_element_type=F32), 1)
     slot_centre = gathered[:, :3]
     slot_targets = gathered[:, 3:data_rows].reshape(2, 3, nodes, slots // 2)
 
@@ -140,13 +150,13 @@
     refine_w = (
         eye_p[:, None, None, :, None, None] * eye_c[None, :, None, None, :, None] * upsample[None, None, :, None, None, :]
     ).reshape(2 * 4 * fine_count, 2 * width)
-    upper = lax.dot_general(refine_w, coarse_in, (((1,), (1,)), ((), ())), precision=HI)
+    upper = lax.dot_general(refine_w, coarse_in, (((1,), (1,)), ((), ())), precision=lax.Precision.HIGH)
     upper = upper.reshape(2, 4, fine_count, slots // 2)
     strength = upper[:, 3] * fine_weights[None, :, None]
     terms = expansion_terms(upper[:, :3], strength, slot_centre, slot_targets)
     terms = jnp.where(valid[:, None, :], terms, 0.0)
 
-    potential = join3(jnp.einsum("pks,pgs->kg", split3(terms, 1), pick, preferred_element_type=F32), 0)
+    potential = join2(jnp.einsum("pks,pgs->kg", split2(terms, 1), pick, preferred_element_type=F32), 0)
 
     home = centre_home.reshape(-1)
     back_index = home * capacity_back + route_rank(home, devices)

time: 61.7 us -> 60.7 us (0.984)
  matrix products: 6.8 us -> 5.88 us
    dot_general x3, matrix products: 3.62 us -> 2.7 us  [the longest x1 0.99 us: per_device(): lax.dot_general(refine_w, coarse_in, (((1,), (1,)), ((), ())), precision=...]
where the time goes in v8:
time: 60.7 us; the launch traced here: 60.3 us
  waiting for transfers between devices  14.9 us (25%)
  other arithmetic  14.6 us (24%)
  blocking collectives  9.41 us (16%)
  local copies, waits for them, and re-layouts  7.77 us (13%)
  starting transfers between devices  7.48 us (12%)
  matrix products  5.88 us (10%)
    all_to_all x1, waiting for transfers between devices, per_device(): lax.all_to_all(outgoing, ('grp', 'dev'), split_axis=0, concat_axis=0, til...  14.9 us
    reduce_sum x1, other arithmetic, expansion_terms(): return jnp.sum(scale[:, :, None] * t_next, axis=1)  11.8 us
    all_to_all x1, blocking collectives, per_device(): lax.all_to_all(sending, ('grp', 'dev'), split_axis=0, concat_axis=0, tile...  9.41 us
    all_to_all x1, starting transfers between devices, per_device(): lax.all_to_all(outgoing, ('grp', 'dev'), split_axis=0, concat_axis=0, til...  7.48 us
    dot_general x1, matrix products, per_device(): placed = jnp.dot(place, rhs, preferred_element_type=F32)  1.87 us
    all_to_all x1, local copies, waits for them, and re-layouts, per_device(): lax.all_to_all(outgoing, ('grp', 'dev'), split_axis=0, concat_axis=0, til...  1.35 us
    all_to_all x1, other arithmetic, per_device(): lax.all_to_all(outgoing, ('grp', 'dev'), split_axis=0, concat_axis=0, til...  1.28 us
  transfers between devices with their start and end apart: 1, of which 1 were waited for; matrix products, arithmetic and copies ran while one was open for 3% of the time, Pallas kernels for 0%

profile of v8, /device:TPU:0, one launch (start us, length us, event | category | flops | bytes accessed | tf_op | source)
XLA Modules:
  0.0 60.3 jit_solution(10324235238061984116)
XLA Ops:
  0.0 0.0 copy-start.2
  0.0 0.8 %fusion.90 = (s32[512,1]{0,1:T(1,128)S(1)}, s32[512,1]{0,1:T(1,128)S(1)}) fusion(s32[512,2]{0,1:T(2,128)} %param.11), kind=kLoop, calls=%fused_computation.157 | loop fusion | bytes 8192 | tf_op jit(solution)/shard_map/slice | solution.py:108
  0.8 0.5 fusion.30
  1.3 0.8 %fusion.89 = (s32[512,1]{0,1:T(1,128)S(1)}, s32[512,1]{0,1:T(1,128)S(1)}) fusion(s32[512,2]{0,1:T(2,128)} %param.12), kind=kLoop, calls=%fused_computation.156 | loop fusion | bytes 8192 | tf_op jit(solution)/shard_map/slice | solution.py:104
  2.2 1.2 %reshape.307 = f32[3,512,16]{2,1,0:T(8,128)S(1)} reshape(f32[3,8192]{1,0:T(4,128)} %param.9) | data formatting | bytes 196608 | tf_op jit(solution)/shard_map/reshape | solution.py:99
  3.4 0.2 copy.65
  3.6 0.0 copy-done.2
  3.6 0.1 reshape.309
  3.7 0.1 copy.66
  3.9 1.9 %fusion.20 = f32[2048,194]{0,1:T(8,128)S(1)} fusion(s32[1024]{0:T(1024)S(1)} %convert_add_fusion.1, bf16[1024,1]{0,1:T(2,128)(2,1)S(1)} %fusion.81, bf16[1024,1]{0,1:T(2,128)(2,1)S(1)} %get-tuple-element.7, bf16[512,64]{0,1:T(8,128)(2,1)S(1)} %get-tuple-element.24, bf16[512,64]{0,1:T(8,128)(2,1)S(1)} %get-tuple-element.23, ...), kind=kOutput, calls=%fused_computation.29 | convolution fusion | flops 818970624 | bytes 1794048 | tf_op jit(solution)/shard_map/dot_general | solution.py:111
  5.7 0.1 slice_add_fusion
  5.9 0.3 copy.67
  6.2 0.0 copy-start
  6.2 0.4 reshape.310
  6.6 0.1 add.190
  6.6 0.0 copy-start.1
  6.7 0.1 concatenate.65
  6.7 1.4 %copy.68 = f32[32,1,4224]{2,1,0:T(1,128)} copy(f32[32,1,4224]{2,0,1:T(8,128)S(1)} %bitcast.86) | data formatting | bytes 1081344 | tf_op jit(solution)/shard_map/all_to_all | solution.py:123
  8.1 0.0 copy-start.3
  8.1 7.5 %all-to-all-start = ((f32[32,1,4224]{2,1,0:T(1,128)}), f32[32,1,4224]{2,1,0:T(1,128)S(1)}, u32[]{:S(2)}, u32[]{:S(2)}) async-start(f32[32,1,4224]{2,1,0:T(1,128)} %copy.68), calls=%async_computation | async-start | bytes 1081344 | tf_op jit(solution)/shard_map/all_to_all | solution.py:123
  15.6 0.0 copy-done
  15.6 0.0 copy-start.4
  15.6 0.3 reshape.313
  15.9 0.0 copy-done.1
  15.9 0.3 subtract_bitcast_fusion
  16.2 0.2 copy.75
  16.4 0.0 copy-done.3
  16.4 0.1 copy.72
  16.5 0.1 broadcast_multiply_fusion
  16.6 0.1 mul.356
  16.7 0.1 mul.357
  16.8 0.1 pad.9.clone
  16.9 0.0 copy-done.4
  16.9 0.3 fusion.32
  17.1 0.1 reduce-precision_convert_fusion.3
  17.2 14.9 %all-to-all-done = f32[32,1,4224]{2,1,0:T(1,128)S(1)} async-done(((f32[32,1,4224]{2,1,0:T(1,128)}), f32[32,1,4224]{2,1,0:T(1,128)S(1)}, u32[]{:S(2)}, u32[]{:S(2)}) %all-to-all-start) | async-done | bytes 540704 | tf_op jit(solution)/shard_map/all_to_all | solution.py:123
  32.1 1.3 %reduce.1 = f32[32,4224]{1,0:T(8,128)S(1)} reduce(f32[32,1,4224]{2,1,0:T(1,128)S(1)} %all-to-all-done, f32[]{:T(128)} %constant.75), dimensions={1}, to_apply=%all_to_all.13.reduce_sub_computation | reduce | bytes 1081348 | tf_op jit(solution)/shard_map/all_to_all | solution.py:123
  33.4 0.1 reshape.311
  33.5 0.1 slice.91
  33.6 0.1 copy.70
  33.6 0.1 copy.71
  33.7 0.1 sub.147
  33.8 0.9 %fusion.28 = f32[2,112,1024]{2,1,0:T(8,128)S(1)} fusion(s32[2,1024]{1,0:T(2,128)S(1)} %sub.147, bf16[56,512]{1,0:T(8,128)(2,1)S(1)} %get-tuple-element.26, bf16[56,512]{1,0:T(8,128)(2,1)S(1)} %get-tuple-element.25), kind=kOutput, calls=%fused_computation.40 | convolution fusion | flops 236158976 | bytes 1040384 | tf_op jit(solution)/shard_map/fg,pgs->pfs/dot_general | solution.py:144
  34.7 0.1 slice_add_fusion.2
  34.8 0.0 copy-start.5
  34.9 1.0 %fusion.58 = f32[2,4,64,1024]{3,2,1,0:T(8,128)S(1)} fusion(f32[1024,128,1,1]{1,0,3,2:T(8,128)S(1)} %bitcast.87, f32[64,128]{1,0:T(8,128)S(1)} %copy.72, f32[2,4,128]{2,1,0:T(4,128)S(1)} %mul.357), kind=kOutput, calls=%fused_computation.82 | convolution fusion | flops 402718720 | bytes 2658304 | tf_op jit(solution)/shard_map/dot_general | solution.py:153
  35.9 0.0 copy-done.5
  35.9 0.3 fusion.39
  36.2 0.4 fusion.40
  36.7 11.8 %fusion.18 = f32[2,16,1024]{2,1,0:T(8,128)S(1)} fusion(f32[2,64,1024]{2,1,0:T(8,128)S(1)} %get-tuple-element.12, f32[2,16,1024]{2,1,0:T(8,128)S(1)} %get-tuple-element.17, f32[2,16,1024]{2,1,0:T(8,128)S(1)} %get-tuple-element.18, f32[2,64,1024]{2,1,0:T(8,128)S(1)} %get-tuple-element.10, f32[2,16,1024]{2,1,0:T(8,128)S(1)} %get-tuple-element.19, ...), kind=kLoop, calls=%fused_computation.26 | loop fusion | flops 90144768 | bytes 3276800 | tf_op jit(solution)/shard_map/reduce_sum | solution.py:73
  48.5 0.8 %fusion.31 = f32[32,512]{1,0:T(8,128)S(1)} fusion(s32[2,1024]{1,0:T(2,128)S(1)} %sub.147, bf16[2,16,1024]{2,1,0:T(8,128)(2,1)S(1)} %get-tuple-element.21, bf16[2,16,1024]{2,1,0:T(8,128)(2,1)S(1)} %get-tuple-element.20), kind=kOutput, calls=%fused_computation.43 | convolution fusion | flops 68419584 | bytes 204800 | tf_op jit(solution)/shard_map/pks,pgs->kg/dot_general | solution.py:159
  49.3 0.5 fusion.27
  49.9 0.2 copy.77
  50.1 0.2 all_to_all.16
  50.3 9.4 %all_to_all.19 = f32[32,1,512]{2,1,0:T(1,128)S(1)} all-to-all(f32[32,1,512]{2,1,0:T(1,128)S(1)} %all_to_all.16), channel_id=1, replica_groups=mesh['grp'=4,'dev'=8] {'grp','dev'}, dimensions={0} | all-to-all | bytes 131072 | tf_op jit(solution)/shard_map/all_to_all | solution.py:170
  59.7 0.6 %copy.92 = f32[16384]{0:T(1024)} copy(f32[16384]{0:T(1024)S(1)} %bitcast.92) | data formatting | bytes 131072
  (23 shorter events, 0.4 us)
Async XLA Ops:
  0.0 3.6 %copy-start.2 = (f32[8192]{0:T(1024)S(1)}, f32[8192]{0:T(1024)}, u32[]{:S(2)}) copy-start(f32[8192]{0:T(1024)} %param.10) | copy-start | bytes 98308
  6.2 9.4 %copy-start = (f32[3,8192]{1,0:T(4,128)S(1)}, f32[3,8192]{1,0:T(4,128)}, u32[]{:S(2)}) copy-start(f32[3,8192]{1,0:T(4,128)} %param.14) | copy-start | bytes 294916
  6.6 9.2 %copy-start.1 = (f32[3,512]{1,0:T(4,128)S(1)}, f32[3,512]{1,0:T(4,128)}, u32[]{:S(2)}) copy-start(f32[3,512]{1,0:T(4,128)} %param.13) | copy-start | bytes 18436
  8.1 8.3 %copy-start.3 = (f32[64,16]{0,1:T(8,128)S(1)}, f32[64,16]{0,1:T(8,128)}, u32[]{:S(2)}) copy-start(f32[64,16]{0,1:T(8,128)} %param.16) | copy-start | bytes 12292
  8.1 24.0 %all-to-all-start = ((f32[32,1,4224]{2,1,0:T(1,128)}), f32[32,1,4224]{2,1,0:T(1,128)S(1)}, u32[]{:S(2)}, u32[]{:S(2)}) async-start(f32[32,1,4224]{2,1,0:T(1,128)} %copy.68), calls=%async_computation | async-start | bytes 1081344 | tf_op jit(solution)/shard_map/all_to_all | solution.py:123
  15.6 1.3 %copy-start.4 = (s32[512,1]{0,1:T(1,128)S(1)}, s32[512,1]{0,1:T(1,128)}, u32[]{:S(2)}) copy-start(s32[512,1]{0,1:T(1,128)} %param.15) | copy-start | bytes 6148
  34.8 1.1 %copy-start.5 = (f32[64]{0:T(128)S(1)}, f32[64]{0:T(128)}, u32[]{:S(2)}) copy-start(f32[64]{0:T(128)} %param.17) | copy-start | bytes 772

commit v9 on v8

--- a/solution.py
+++ b/solution.py
@@ -130,14 +130,18 @@
     valid = ids >= 0
     pick = (jnp.arange(centre_count, dtype=jnp.int32)[None, :, None] == ids[:, None, :]).astype(BF)
 
+    home = centre_home.reshape(-1)
+    back_index = home * capacity_back + route_rank(home, devices)
     rel = targets.reshape(3, centre_count, nodes) - centres[:, :, None]
     data_rows = 3 + 3 * nodes
-    padded_rows = -(-data_rows // 8) * 8
+    padded_rows = -(-(data_rows + 2) // 8) * 8
     centre_data = jnp.concatenate(
         [
             centres,
             rel.transpose(0, 2, 1).reshape(3 * nodes, centre_count),
-            jnp.zeros((padded_rows - data_rows, centre_count), F32),
+            (back_index // 32).astype(F32)[None],
+            (back_index % 32).astype(F32)[None],
+            jnp.zeros((padded_rows - data_rows - 2, centre_count), F32),
         ],
         axis=0,
     )
@@ -156,15 +160,12 @@
     terms = expansion_terms(upper[:, :3], strength, slot_centre, slot_targets)
     terms = jnp.where(valid[:, None, :], terms, 0.0)
 
-    potential = join2(jnp.einsum("pks,pgs->kg", split2(terms, 1), pick, preferred_element_type=F32), 0)
-
-    home = centre_home.reshape(-1)
-    back_index = home * capacity_back + route_rank(home, devices)
-    back_place = (
-        jnp.arange(devices * capacity_back, dtype=jnp.int32)[:, None] == back_index[None, :]
+    back_slot = 32.0 * gathered[:, data_rows] + gathered[:, data_rows + 1]
+    to_back = (
+        (jnp.arange(devices * capacity_back, dtype=F32)[:, None, None] == back_slot[None]) & valid[None]
     ).astype(BF)
     sending = join3(
-        lax.dot_general(back_place, split3(potential, 0), (((1,), (1,)), ((), ())), preferred_element_type=F32), 1
+        lax.dot_general(to_back, split3(terms, 1), (((1, 2), (0, 2)), ((), ())), preferred_element_type=F32), 1
     )
     sending = sending.reshape(devices, capacity_back * nodes)
     returned = lax.all_to_all(sending, ("grp", "dev"), split_axis=0, concat_axis=0, tiled=True)

time: 60.7 us -> 62 us (1.021)
  local copies, waits for them, and re-layouts: 7.77 us -> 8.67 us
    reshape x2, local copies, waits for them, and re-layouts: 0.23 us -> 0.98 us  [per_device(): density.reshape(panels, nodes)]
    dot_general x2 -> x1, matrix products: 1.32 us -> 1.9 us  [per_device(): lax.dot_general(to_back, split3(terms, 1), (((1, 2), (0, 2)), ((), ())),...]
where the time goes in v9:
time: 62 us; the launch traced here: 61.7 us
  waiting for transfers between devices  14.7 us (24%)
  other arithmetic  14.6 us (24%)
  blocking collectives  9.41 us (15%)
  local copies, waits for them, and re-layouts  8.67 us (14%)
  starting transfers between devices  7.48 us (12%)
  matrix products  6.46 us (10%)
    all_to_all x1, waiting for transfers between devices, per_device(): lax.all_to_all(outgoing, ('grp', 'dev'), split_axis=0, concat_axis=0, til...  14.7 us
    reduce_sum x1, other arithmetic, expansion_terms(): return jnp.sum(scale[:, :, None] * t_next, axis=1)  11.8 us
    all_to_all x1, blocking collectives, per_device(): lax.all_to_all(sending, ('grp', 'dev'), split_axis=0, concat_axis=0, tile...  9.41 us
    all_to_all x1, starting transfers between devices, per_device(): lax.all_to_all(outgoing, ('grp', 'dev'), split_axis=0, concat_axis=0, til...  7.48 us
    dot_general x1, matrix products, per_device(): lax.dot_general(to_back, split3(terms, 1), (((1, 2), (0, 2)), ((), ())),...  1.9 us
    dot_general x1, matrix products, per_device(): placed = jnp.dot(place, rhs, preferred_element_type=F32)  1.87 us
    all_to_all x1, local copies, waits for them, and re-layouts, per_device(): lax.all_to_all(outgoing, ('grp', 'dev'), split_axis=0, concat_axis=0, til...  1.35 us
    all_to_all x1, other arithmetic, per_device(): lax.all_to_all(outgoing, ('grp', 'dev'), split_axis=0, concat_axis=0, til...  1.28 us
  transfers between devices with their start and end apart: 1, of which 1 were waited for; matrix products, arithmetic and copies ran while one was open for 3% of the time, Pallas kernels for 0%

profile of v9, /device:TPU:0, one launch (start us, length us, event | category | flops | bytes accessed | tf_op | source)
XLA Modules:
  0.0 61.7 jit_solution(4811903877784108378)
XLA Ops:
  0.0 0.8 %fusion.90 = (s32[512,1]{0,1:T(1,128)S(1)}, s32[512,1]{0,1:T(1,128)S(1)}) fusion(s32[512,2]{0,1:T(2,128)} %param.11), kind=kLoop, calls=%fused_computation.158 | loop fusion | bytes 8192 | tf_op jit(solution)/shard_map/slice | solution.py:108
  0.8 0.5 fusion.35
  1.3 0.8 %fusion.89 = (s32[512,1]{0,1:T(1,128)S(1)}, s32[512,1]{0,1:T(1,128)S(1)}) fusion(s32[512,2]{0,1:T(2,128)} %param.12), kind=kLoop, calls=%fused_computation.157 | loop fusion | bytes 8192 | tf_op jit(solution)/shard_map/slice | solution.py:104
  2.2 0.9 %reshape.417 = f32[512,16]{1,0:T(8,128)S(1)} reshape(f32[8192]{0:T(1024)} %param.10) | data formatting | bytes 65536 | tf_op jit(solution)/shard_map/reshape | solution.py:100
  3.0 0.1 copy.66
  3.1 1.2 %reshape.415 = f32[3,512,16]{2,1,0:T(8,128)S(1)} reshape(f32[3,8192]{1,0:T(4,128)} %param.9) | data formatting | bytes 196608 | tf_op jit(solution)/shard_map/reshape | solution.py:99
  4.3 0.2 copy.65
  4.6 1.9 %fusion.21 = f32[2048,194]{0,1:T(8,128)S(1)} fusion(s32[1024]{0:T(1024)S(1)} %convert_add_fusion.1, bf16[1024,1]{0,1:T(2,128)(2,1)S(1)} %fusion.80, bf16[1024,1]{0,1:T(2,128)(2,1)S(1)} %get-tuple-element.9, bf16[512,64]{0,1:T(8,128)(2,1)S(1)} %get-tuple-element.28, bf16[512,64]{0,1:T(8,128)(2,1)S(1)} %get-tuple-element.27, ...), kind=kOutput, calls=%fused_computation.31 | convolution fusion | flops 818970624 | bytes 1794048 | tf_op jit(solution)/shard_map/dot_general | solution.py:111
  6.5 0.1 slice_add_fusion
  6.6 0.3 copy.67
  7.0 0.0 copy-start
  7.0 0.4 reshape.418
  7.3 0.1 add.228
  7.4 0.0 copy-start.3
  7.4 0.0 copy-start.1
  7.4 0.1 concatenate.61
  7.5 1.4 %copy.68 = f32[32,1,4224]{2,1,0:T(1,128)} copy(f32[32,1,4224]{2,0,1:T(8,128)S(1)} %bitcast.95) | data formatting | bytes 1081344 | tf_op jit(solution)/shard_map/all_to_all | solution.py:123
  8.8 7.5 %all-to-all-start = ((f32[32,1,4224]{2,1,0:T(1,128)}), f32[32,1,4224]{2,1,0:T(1,128)S(1)}, u32[]{:S(2)}, u32[]{:S(2)}) async-start(f32[32,1,4224]{2,1,0:T(1,128)} %copy.68), calls=%async_computation | async-start | bytes 1081344 | tf_op jit(solution)/shard_map/all_to_all | solution.py:123
  16.3 0.0 copy-done
  16.3 0.0 copy-start.2
  16.4 0.3 reshape.420
  16.6 0.0 copy-done.3
  16.7 0.3 fusion.36
  16.9 0.0 copy-done.1
  16.9 0.3 subtract_bitcast_fusion
  17.2 0.2 copy.72
  17.5 0.0 copy-done.2
  17.5 0.1 copy.73
  17.6 0.1 broadcast_multiply_fusion
  17.6 0.1 mul.383
  17.7 0.1 mul.384
  17.9 0.2 concatenate.62
  18.1 14.7 %all-to-all-done = f32[32,1,4224]{2,1,0:T(1,128)S(1)} async-done(((f32[32,1,4224]{2,1,0:T(1,128)}), f32[32,1,4224]{2,1,0:T(1,128)S(1)}, u32[]{:S(2)}, u32[]{:S(2)}) %all-to-all-start) | async-done | bytes 540704 | tf_op jit(solution)/shard_map/all_to_all | solution.py:123
  32.9 1.3 %reduce.1 = f32[32,4224]{1,0:T(8,128)S(1)} reduce(f32[32,1,4224]{2,1,0:T(1,128)S(1)} %all-to-all-done, f32[]{:T(128)} %constant.101), dimensions={1}, to_apply=%all_to_all.13.reduce_sub_computation | reduce | bytes 1081348 | tf_op jit(solution)/shard_map/all_to_all | solution.py:123
  34.1 0.1 reshape.419
  34.2 0.1 slice.101
  34.3 0.1 copy.70
  34.4 0.1 copy.71
  34.5 0.1 sub.150
  34.6 0.9 %fusion.30 = f32[2,112,1024]{2,1,0:T(8,128)S(1)} fusion(s32[2,1024]{1,0:T(2,128)S(1)} %sub.150, bf16[56,512]{1,0:T(8,128)(2,1)S(1)} %get-tuple-element.30, bf16[56,512]{1,0:T(8,128)(2,1)S(1)} %get-tuple-element.29), kind=kOutput, calls=%fused_computation.41 | convolution fusion | flops 236158976 | bytes 1040384 | tf_op jit(solution)/shard_map/fg,pgs->pfs/dot_general | solution.py:148
  35.5 0.1 slice_add_fusion.2
  35.5 0.0 copy-start.4
  35.7 1.0 %fusion.61 = f32[2,4,64,1024]{3,2,1,0:T(8,128)S(1)} fusion(f32[1024,128,1,1]{1,0,3,2:T(8,128)S(1)} %bitcast.96, f32[64,128]{1,0:T(8,128)S(1)} %copy.73, f32[2,4,128]{2,1,0:T(4,128)S(1)} %mul.384), kind=kOutput, calls=%fused_computation.82 | convolution fusion | flops 402718720 | bytes 2658304 | tf_op jit(solution)/shard_map/dot_general | solution.py:157
  36.7 0.0 copy-done.4
  36.7 0.3 fusion.42
  37.0 0.4 fusion.43
  37.4 11.8 %fusion.18 = f32[2,16,1024]{2,1,0:T(8,128)S(1)} fusion(f32[2,64,1024]{2,1,0:T(8,128)S(1)} %get-tuple-element.14, f32[2,16,1024]{2,1,0:T(8,128)S(1)} %get-tuple-element.20, f32[2,16,1024]{2,1,0:T(8,128)S(1)} %get-tuple-element.21, f32[2,64,1024]{2,1,0:T(8,128)S(1)} %get-tuple-element.12, f32[2,16,1024]{2,1,0:T(8,128)S(1)} %get-tuple-element.22, ...), kind=kLoop, calls=%fused_computation.26 | loop fusion | flops 90144768 | bytes 3276800 | tf_op jit(solution)/shard_map/reduce_sum | solution.py:73
  49.3 1.9 %fusion.31 = f32[1024,48]{0,1:T(8,128)S(1)} fusion(f32[2,1024]{1,0:T(2,128)S(1)} %get-tuple-element.38, pred[2,1024]{1,0:T(4,128)(4,1)S(1)} %broadcast_compare_fusion, bf16[2,16,1024]{2,1,0:T(8,128)(2,1)S(1)} %get-tuple-element.24, bf16[2,16,1024]{2,1,0:T(8,128)(2,1)S(1)} %get-tuple-element.25, bf16[2,16,1024]{2,1,0:T(8,128)(2,1)S(1)} %get-tuple-element.23), kind=kOutput, calls=%fused_computation.42 | convolution fusion | flops 206110720 | bytes 403456 | tf_op jit(solution)/shard_map/dot_general | solution.py:168
  51.2 0.2 copy.77
  51.4 0.2 all_to_all.16
  51.6 9.4 %all_to_all.19 = f32[32,1,512]{2,1,0:T(1,128)S(1)} all-to-all(f32[32,1,512]{2,1,0:T(1,128)S(1)} %all_to_all.16), channel_id=1, replica_groups=mesh['grp'=4,'dev'=8] {'grp','dev'}, dimensions={0} | all-to-all | bytes 131072 | tf_op jit(solution)/shard_map/all_to_all | solution.py:171
  61.0 0.6 %copy.93 = f32[16384]{0:T(1024)} copy(f32[16384]{0:T(1024)S(1)} %bitcast.101) | data formatting | bytes 131072
  (25 shorter events, 0.4 us)
Async XLA Ops:
  7.0 9.4 %copy-start = (f32[3,8192]{1,0:T(4,128)S(1)}, f32[3,8192]{1,0:T(4,128)}, u32[]{:S(2)}) copy-start(f32[3,8192]{1,0:T(4,128)} %param.14) | copy-start | bytes 294916
  7.4 9.2 %copy-start.3 = (s32[512,1]{0,1:T(1,128)S(1)}, s32[512,1]{0,1:T(1,128)}, u32[]{:S(2)}) copy-start(s32[512,1]{0,1:T(1,128)} %param.15) | copy-start | bytes 6148
  7.4 9.5 %copy-start.1 = (f32[3,512]{1,0:T(4,128)S(1)}, f32[3,512]{1,0:T(4,128)}, u32[]{:S(2)}) copy-start(f32[3,512]{1,0:T(4,128)} %param.13) | copy-start | bytes 18436
  8.8 24.0 %all-to-all-start = ((f32[32,1,4224]{2,1,0:T(1,128)}), f32[32,1,4224]{2,1,0:T(1,128)S(1)}, u32[]{:S(2)}, u32[]{:S(2)}) async-start(f32[32,1,4224]{2,1,0:T(1,128)} %copy.68), calls=%async_computation | async-start | bytes 1081344 | tf_op jit(solution)/shard_map/all_to_all | solution.py:123
  16.3 1.1 %copy-start.2 = (f32[64,16]{0,1:T(8,128)S(1)}, f32[64,16]{0,1:T(8,128)}, u32[]{:S(2)}) copy-start(f32[64,16]{0,1:T(8,128)} %param.16) | copy-start | bytes 12292
  35.5 1.1 %copy-start.4 = (f32[64]{0:T(128)S(1)}, f32[64]{0:T(128)}, u32[]{:S(2)}) copy-start(f32[64]{0:T(128)} %param.17) | copy-start | bytes 772

commit v10 on v8

--- a/solution.py
+++ b/solution.py
@@ -101,11 +101,11 @@
         axis=1,
     )
     coarse_parts = jnp.concatenate([split3(coarse, 1)] * fanout, axis=0)
-    ids1 = jnp.concatenate([crevice_centre[:, t] for t in range(fanout)]) + 1
+    ids1 = crevice_centre.T.reshape(pairs) + 1
     id_parts = jnp.stack([ids1 // 16, ids1 % 16], axis=1).astype(BF)
     rhs = jnp.concatenate([coarse_parts, id_parts], axis=1)
 
-    destination = jnp.concatenate([crevice_routes[:, t] for t in range(fanout)])
+    destination = crevice_routes.T.reshape(pairs)
     slot_index = destination * capacity + route_rank(destination, devices)
     place = (jnp.arange(slots, dtype=jnp.int32)[:, None] == slot_index[None, :]).astype(BF)
     placed = jnp.dot(place, rhs, preferred_element_type=F32)

time: 60.7 us -> 59.9 us (0.987)
  local copies, waits for them, and re-layouts: 7.77 us -> 7.03 us
    slice x2 -> x0, local copies, waits for them, and re-layouts: 1.54 us -> none  [the longest x1 0.77 us: per_device(): ids1 = jnp.concatenate([crevice_centre[:, t] for t in range(fanout)]) + 1]
    reshape x2, local copies, waits for them, and re-layouts: 0.23 us -> 0.98 us  [per_device(): density.reshape(panels, nodes)]
where the time goes in v10:
time: 59.9 us; the launch traced here: 59.6 us
  waiting for transfers between devices  14.9 us (25%)
  other arithmetic  14.6 us (24%)
  blocking collectives  9.41 us (16%)
  starting transfers between devices  7.48 us (12%)
  local copies, waits for them, and re-layouts  7.03 us (12%)
  matrix products  5.89 us (10%)
    all_to_all x1, waiting for transfers between devices, per_device(): lax.all_to_all(outgoing, ('grp', 'dev'), split_axis=0, concat_axis=0, til...  14.9 us
    reduce_sum x1, other arithmetic, expansion_terms(): return jnp.sum(scale[:, :, None] * t_next, axis=1)  11.8 us
    all_to_all x1, blocking collectives, per_device(): lax.all_to_all(sending, ('grp', 'dev'), split_axis=0, concat_axis=0, tile...  9.41 us
    all_to_all x1, starting transfers between devices, per_device(): lax.all_to_all(outgoing, ('grp', 'dev'), split_axis=0, concat_axis=0, til...  7.48 us
    dot_general x1, matrix products, per_device(): placed = jnp.dot(place, rhs, preferred_element_type=F32)  1.86 us
    all_to_all x1, local copies, waits for them, and re-layouts, per_device(): lax.all_to_all(outgoing, ('grp', 'dev'), split_axis=0, concat_axis=0, til...  1.36 us
    all_to_all x1, other arithmetic, per_device(): lax.all_to_all(outgoing, ('grp', 'dev'), split_axis=0, concat_axis=0, til...  1.28 us
    reshape x1, local copies, waits for them, and re-layouts, per_device(): panel_nodes.reshape(3, panels, nodes).transpose(1, 0, 2)  1.21 us
  transfers between devices with their start and end apart: 1, of which 1 were waited for; matrix products, arithmetic and copies ran while one was open for 3% of the time, Pallas kernels for 0%

profile of v10, /device:TPU:0, one launch (start us, length us, event | category | flops | bytes accessed | tf_op | source)
XLA Modules:
  0.0 59.6 jit_solution(13368584183962024951)
XLA Ops:
  0.0 0.0 copy-start.3
  0.0 0.0 copy-start.4
  0.0 1.2 %reshape.275 = f32[3,512,16]{2,1,0:T(8,128)S(1)} reshape(f32[3,8192]{1,0:T(4,128)} %param.9) | data formatting | bytes 196608 | tf_op jit(solution)/shard_map/reshape | solution.py:99
  1.2 0.2 copy.65
  1.5 0.9 %reshape.277 = f32[512,16]{1,0:T(8,128)S(1)} reshape(f32[8192]{0:T(1024)} %param.10) | data formatting | bytes 65536 | tf_op jit(solution)/shard_map/reshape | solution.py:100
  2.4 0.1 copy.66
  2.4 0.0 copy-done.3
  2.5 0.5 fusion.30
  3.0 0.0 copy-done.4
  3.1 1.9 %fusion.20 = f32[2048,194]{0,1:T(8,128)S(1)} fusion(s32[1024]{0:T(1024)S(1)} %convert_add_fusion.1, bf16[1024,1]{0,1:T(2,128)(2,1)S(1)} %fusion.81, bf16[1024,1]{0,1:T(2,128)(2,1)S(1)} %get-tuple-element.7, bf16[512,64]{0,1:T(8,128)(2,1)S(1)} %get-tuple-element.24, bf16[512,64]{0,1:T(8,128)(2,1)S(1)} %get-tuple-element.23, ...), kind=kOutput, calls=%fused_computation.29 | convolution fusion | flops 818970624 | bytes 1794048 | tf_op jit(solution)/shard_map/dot_general | solution.py:111
  5.0 0.1 slice_add_fusion
  5.1 0.3 copy.67
  5.5 0.0 copy-start
  5.5 0.4 reshape.278
  5.9 0.1 add.201
  5.9 0.0 copy-start.1
  5.9 0.1 concatenate.36
  6.0 1.4 %copy.68 = f32[32,1,4224]{2,1,0:T(1,128)} copy(f32[32,1,4224]{2,0,1:T(8,128)S(1)} %bitcast.93) | data formatting | bytes 1081344 | tf_op jit(solution)/shard_map/all_to_all | solution.py:123
  7.4 0.0 copy-start.2
  7.4 7.5 %all-to-all-start = ((f32[32,1,4224]{2,1,0:T(1,128)}), f32[32,1,4224]{2,1,0:T(1,128)S(1)}, u32[]{:S(2)}, u32[]{:S(2)}) async-start(f32[32,1,4224]{2,1,0:T(1,128)} %copy.68), calls=%async_computation | async-start | bytes 1081344 | tf_op jit(solution)/shard_map/all_to_all | solution.py:123
  14.9 0.0 copy-done
  14.9 0.0 copy-start.5
  14.9 0.3 reshape.281
  15.2 0.0 copy-done.1
  15.2 0.3 subtract_bitcast_fusion
  15.5 0.2 copy.75
  15.7 0.0 copy-done.2
  15.7 0.1 copy.72
  15.8 0.1 broadcast_multiply_fusion
  15.9 0.1 mul.356
  16.0 0.1 mul.357
  16.1 0.1 pad.9.clone
  16.1 0.0 copy-done.5
  16.1 0.3 fusion.32
  16.4 0.1 reduce-precision_convert_fusion.3
  16.5 14.9 %all-to-all-done = f32[32,1,4224]{2,1,0:T(1,128)S(1)} async-done(((f32[32,1,4224]{2,1,0:T(1,128)}), f32[32,1,4224]{2,1,0:T(1,128)S(1)}, u32[]{:S(2)}, u32[]{:S(2)}) %all-to-all-start) | async-done | bytes 540704 | tf_op jit(solution)/shard_map/all_to_all | solution.py:123
  31.4 1.3 %reduce.1 = f32[32,4224]{1,0:T(8,128)S(1)} reduce(f32[32,1,4224]{2,1,0:T(1,128)S(1)} %all-to-all-done, f32[]{:T(128)} %constant.75), dimensions={1}, to_apply=%all_to_all.13.reduce_sub_computation | reduce | bytes 1081348 | tf_op jit(solution)/shard_map/all_to_all | solution.py:123
  32.7 0.1 reshape.279
  32.8 0.1 slice.75
  32.8 0.1 copy.70
  32.9 0.1 copy.71
  33.0 0.1 sub.147
  33.1 0.9 %fusion.28 = f32[2,112,1024]{2,1,0:T(8,128)S(1)} fusion(s32[2,1024]{1,0:T(2,128)S(1)} %sub.147, bf16[56,512]{1,0:T(8,128)(2,1)S(1)} %get-tuple-element.26, bf16[56,512]{1,0:T(8,128)(2,1)S(1)} %get-tuple-element.25), kind=kOutput, calls=%fused_computation.40 | convolution fusion | flops 236158976 | bytes 1040384 | tf_op jit(solution)/shard_map/fg,pgs->pfs/dot_general | solution.py:144
  34.0 0.1 slice_add_fusion.2
  34.1 0.0 copy-start.6
  34.2 1.0 %fusion.58 = f32[2,4,64,1024]{3,2,1,0:T(8,128)S(1)} fusion(f32[1024,128,1,1]{1,0,3,2:T(8,128)S(1)} %bitcast.94, f32[64,128]{1,0:T(8,128)S(1)} %copy.72, f32[2,4,128]{2,1,0:T(4,128)S(1)} %mul.357), kind=kOutput, calls=%fused_computation.82 | convolution fusion | flops 402718720 | bytes 2658304 | tf_op jit(solution)/shard_map/dot_general | solution.py:153
  35.2 0.0 copy-done.6
  35.2 0.3 fusion.39
  35.5 0.4 fusion.40
  35.9 11.8 %fusion.18 = f32[2,16,1024]{2,1,0:T(8,128)S(1)} fusion(f32[2,64,1024]{2,1,0:T(8,128)S(1)} %get-tuple-element.12, f32[2,16,1024]{2,1,0:T(8,128)S(1)} %get-tuple-element.17, f32[2,16,1024]{2,1,0:T(8,128)S(1)} %get-tuple-element.18, f32[2,64,1024]{2,1,0:T(8,128)S(1)} %get-tuple-element.10, f32[2,16,1024]{2,1,0:T(8,128)S(1)} %get-tuple-element.19, ...), kind=kLoop, calls=%fused_computation.26 | loop fusion | flops 90144768 | bytes 3276800 | tf_op jit(solution)/shard_map/reduce_sum | solution.py:73
  47.8 0.8 %fusion.31 = f32[32,512]{1,0:T(8,128)S(1)} fusion(s32[2,1024]{1,0:T(2,128)S(1)} %sub.147, bf16[2,16,1024]{2,1,0:T(8,128)(2,1)S(1)} %get-tuple-element.21, bf16[2,16,1024]{2,1,0:T(8,128)(2,1)S(1)} %get-tuple-element.20), kind=kOutput, calls=%fused_computation.43 | convolution fusion | flops 68419584 | bytes 204800 | tf_op jit(solution)/shard_map/pks,pgs->kg/dot_general | solution.py:159
  48.6 0.5 fusion.27
  49.1 0.2 copy.77
  49.3 0.2 all_to_all.16
  49.6 9.4 %all_to_all.19 = f32[32,1,512]{2,1,0:T(1,128)S(1)} all-to-all(f32[32,1,512]{2,1,0:T(1,128)S(1)} %all_to_all.16), channel_id=1, replica_groups=mesh['grp'=4,'dev'=8] {'grp','dev'}, dimensions={0} | all-to-all | bytes 131072 | tf_op jit(solution)/shard_map/all_to_all | solution.py:170
  59.0 0.6 %copy.94 = f32[16384]{0:T(1024)} copy(f32[16384]{0:T(1024)S(1)} %bitcast.99) | data formatting | bytes 131072
  (25 shorter events, 0.4 us)
Async XLA Ops:
  0.0 2.4 %copy-start.3 = (s32[512,2]{0,1:T(2,128)S(1)}, s32[512,2]{0,1:T(2,128)}, u32[]{:S(2)}) copy-start(s32[512,2]{0,1:T(2,128)} %param.11) | copy-start | bytes 12292
  0.0 3.0 %copy-start.4 = (s32[512,2]{0,1:T(2,128)S(1)}, s32[512,2]{0,1:T(2,128)}, u32[]{:S(2)}) copy-start(s32[512,2]{0,1:T(2,128)} %param.12) | copy-start | bytes 12292
  5.5 9.4 %copy-start = (f32[3,8192]{1,0:T(4,128)S(1)}, f32[3,8192]{1,0:T(4,128)}, u32[]{:S(2)}) copy-start(f32[3,8192]{1,0:T(4,128)} %param.14) | copy-start | bytes 294916
  5.9 9.2 %copy-start.1 = (f32[3,512]{1,0:T(4,128)S(1)}, f32[3,512]{1,0:T(4,128)}, u32[]{:S(2)}) copy-start(f32[3,512]{1,0:T(4,128)} %param.13) | copy-start | bytes 18436
  7.4 8.3 %copy-start.2 = (f32[64,16]{0,1:T(8,128)S(1)}, f32[64,16]{0,1:T(8,128)}, u32[]{:S(2)}) copy-start(f32[64,16]{0,1:T(8,128)} %param.16) | copy-start | bytes 12292
  7.4 24.0 %all-to-all-start = ((f32[32,1,4224]{2,1,0:T(1,128)}), f32[32,1,4224]{2,1,0:T(1,128)S(1)}, u32[]{:S(2)}, u32[]{:S(2)}) async-start(f32[32,1,4224]{2,1,0:T(1,128)} %copy.68), calls=%async_computation | async-start | bytes 1081344 | tf_op jit(solution)/shard_map/all_to_all | solution.py:123
  14.9 1.3 %copy-start.5 = (s32[512,1]{0,1:T(1,128)S(1)}, s32[512,1]{0,1:T(1,128)}, u32[]{:S(2)}) copy-start(s32[512,1]{0,1:T(1,128)} %param.15) | copy-start | bytes 6148
  34.1 1.1 %copy-start.6 = (f32[64]{0:T(128)S(1)}, f32[64]{0:T(128)}, u32[]{:S(2)}) copy-start(f32[64]{0:T(128)} %param.17) | copy-start | bytes 772

commit v11 on v10

--- a/solution.py
+++ b/solution.py
@@ -95,10 +95,11 @@
     slots = devices * capacity
     width = 4 * nodes
 
-    coarse = jnp.concatenate(
-        [panel_nodes.reshape(3, panels, nodes).transpose(1, 0, 2).reshape(panels, 3 * nodes),
-         density.reshape(panels, nodes)],
-        axis=1,
+    coarse = (
+        lax.optimization_barrier(jnp.concatenate([panel_nodes, density[None]], axis=0))
+        .reshape(4, panels, nodes)
+        .transpose(1, 0, 2)
+        .reshape(panels, width)
     )
     coarse_parts = jnp.concatenate([split3(coarse, 1)] * fanout, axis=0)
     ids1 = crevice_centre.T.reshape(pairs) + 1

time: 59.9 us -> 59.1 us (0.987)
  local copies, waits for them, and re-layouts: 7.03 us -> 5.28 us
  other arithmetic: 14.6 us -> 15.6 us
    reshape x3 -> x1, local copies, waits for them, and re-layouts: 2.19 us -> 0.37 us  [per_device(): coarse = lax.optimization_barrier(jnp.concatenate([panel_nodes, density[N...]
    concatenate x0 -> x1, other arithmetic: none -> 1 us  [per_device(): jnp.concatenate([panel_nodes, density[None]], axis=0)]
where the time goes in v11:
time: 59.1 us; the launch traced here: 58.9 us
  other arithmetic  15.6 us (26%)
  waiting for transfers between devices  14.9 us (25%)
  blocking collectives  9.41 us (16%)
  starting transfers between devices  7.48 us (13%)
  matrix products  5.88 us (10%)
  local copies, waits for them, and re-layouts  5.28 us (9%)
    all_to_all x1, waiting for transfers between devices, per_device(): lax.all_to_all(outgoing, ('grp', 'dev'), split_axis=0, concat_axis=0, til...  14.9 us
    reduce_sum x1, other arithmetic, expansion_terms(): return jnp.sum(scale[:, :, None] * t_next, axis=1)  11.8 us
    all_to_all x1, blocking collectives, per_device(): lax.all_to_all(sending, ('grp', 'dev'), split_axis=0, concat_axis=0, tile...  9.41 us
    all_to_all x1, starting transfers between devices, per_device(): lax.all_to_all(outgoing, ('grp', 'dev'), split_axis=0, concat_axis=0, til...  7.48 us
    dot_general x1, matrix products, per_device(): placed = jnp.dot(place, rhs, preferred_element_type=F32)  1.87 us
    all_to_all x1, local copies, waits for them, and re-layouts, per_device(): lax.all_to_all(outgoing, ('grp', 'dev'), split_axis=0, concat_axis=0, til...  1.36 us
    all_to_all x1, other arithmetic, per_device(): lax.all_to_all(outgoing, ('grp', 'dev'), split_axis=0, concat_axis=0, til...  1.28 us
  transfers between devices with their start and end apart: 1, of which 1 were waited for; matrix products, arithmetic and copies ran while one was open for 3% of the time, Pallas kernels for 0%

profile of v11, /device:TPU:0, one launch (start us, length us, event | category | flops | bytes accessed | tf_op | source)
XLA Modules:
  0.0 58.9 jit_solution(2471170848045550062)
XLA Ops:
  0.0 0.0 copy-start.3
  0.0 1.0 %pad_maximum_fusion = f32[4,8192]{1,0:T(4,128)S(1)} fusion(f32[1,8192]{1,0:T(1,128)} %bitcast.110, f32[3,8192]{1,0:T(4,128)} %param.9), kind=kLoop, calls=%fused_computation.94 | loop fusion | flops 32768 | bytes 262144 | tf_op jit(solution)/shard_map/concatenate | solution.py:99
  1.0 0.0 copy-start.4
  1.0 0.4 reshape.272
  1.4 0.3 copy.61
  1.7 0.0 copy-done.3
  1.8 0.5 fusion.30
  2.3 0.0 copy-done.4
  2.4 1.9 %fusion.20 = f32[2048,194]{0,1:T(8,128)S(1)} fusion(s32[1024]{0:T(1024)S(1)} %convert_add_fusion.1, bf16[1024,1]{0,1:T(2,128)(2,1)S(1)} %fusion.81, bf16[1024,1]{0,1:T(2,128)(2,1)S(1)} %get-tuple-element.7, bf16[512,64]{0,1:T(8,128)(2,1)S(1)} %get-tuple-element.23, bf16[512,64]{0,1:T(8,128)(2,1)S(1)} %get-tuple-element.24, ...), kind=kOutput, calls=%fused_computation.29 | convolution fusion | flops 818970624 | bytes 1794048 | tf_op jit(solution)/shard_map/dot_general | solution.py:112
  4.3 0.1 slice_add_fusion
  4.4 0.3 copy.62
  4.8 0.0 copy-start
  4.8 0.4 reshape.274
  5.1 0.1 add.201
  5.2 0.0 copy-start.1
  5.2 0.1 concatenate.36
  5.3 1.4 %copy.63 = f32[32,1,4224]{2,1,0:T(1,128)} copy(f32[32,1,4224]{2,0,1:T(8,128)S(1)} %bitcast.100) | data formatting | bytes 1081344 | tf_op jit(solution)/shard_map/all_to_all | solution.py:124
  6.6 0.0 copy-start.2
  6.6 7.5 %all-to-all-start = ((f32[32,1,4224]{2,1,0:T(1,128)}), f32[32,1,4224]{2,1,0:T(1,128)S(1)}, u32[]{:S(2)}, u32[]{:S(2)}) async-start(f32[32,1,4224]{2,1,0:T(1,128)} %copy.63), calls=%async_computation | async-start | bytes 1081344 | tf_op jit(solution)/shard_map/all_to_all | solution.py:124
  14.1 0.0 copy-done
  14.1 0.0 copy-start.5
  14.1 0.3 reshape.277
  14.4 0.0 copy-done.1
  14.4 0.3 subtract_bitcast_fusion
  14.7 0.2 copy.70
  14.9 0.0 copy-done.2
  15.0 0.1 copy.67
  15.1 0.1 broadcast_multiply_fusion
  15.1 0.1 mul.356
  15.2 0.1 mul.357
  15.3 0.1 pad.9.clone
  15.4 0.0 copy-done.5
  15.4 0.3 fusion.32
  15.7 0.1 reduce-precision_convert_fusion.3
  15.8 14.9 %all-to-all-done = f32[32,1,4224]{2,1,0:T(1,128)S(1)} async-done(((f32[32,1,4224]{2,1,0:T(1,128)}), f32[32,1,4224]{2,1,0:T(1,128)S(1)}, u32[]{:S(2)}, u32[]{:S(2)}) %all-to-all-start) | async-done | bytes 540704 | tf_op jit(solution)/shard_map/all_to_all | solution.py:124
  30.6 1.3 %reduce.1 = f32[32,4224]{1,0:T(8,128)S(1)} reduce(f32[32,1,4224]{2,1,0:T(1,128)S(1)} %all-to-all-done, f32[]{:T(128)} %constant.75), dimensions={1}, to_apply=%all_to_all.13.reduce_sub_computation | reduce | bytes 1081348 | tf_op jit(solution)/shard_map/all_to_all | solution.py:124
  31.9 0.1 reshape.275
  32.0 0.1 slice.75
  32.1 0.1 copy.65
  32.2 0.1 copy.66
  32.3 0.1 sub.147
  32.4 0.9 %fusion.28 = f32[2,112,1024]{2,1,0:T(8,128)S(1)} fusion(s32[2,1024]{1,0:T(2,128)S(1)} %sub.147, bf16[56,512]{1,0:T(8,128)(2,1)S(1)} %get-tuple-element.26, bf16[56,512]{1,0:T(8,128)(2,1)S(1)} %get-tuple-element.25), kind=kOutput, calls=%fused_computation.40 | convolution fusion | flops 236158976 | bytes 1040384 | tf_op jit(solution)/shard_map/fg,pgs->pfs/dot_general | solution.py:145
  33.3 0.1 slice_add_fusion.2
  33.3 0.0 copy-start.6
  33.5 1.0 %fusion.58 = f32[2,4,64,1024]{3,2,1,0:T(8,128)S(1)} fusion(f32[1024,128,1,1]{1,0,3,2:T(8,128)S(1)} %bitcast.101, f32[64,128]{1,0:T(8,128)S(1)} %copy.67, f32[2,4,128]{2,1,0:T(4,128)S(1)} %mul.357), kind=kOutput, calls=%fused_computation.82 | convolution fusion | flops 402718720 | bytes 2658304 | tf_op jit(solution)/shard_map/dot_general | solution.py:154
  34.5 0.0 copy-done.6
  34.5 0.3 fusion.39
  34.8 0.4 fusion.40
  35.2 11.8 %fusion.18 = f32[2,16,1024]{2,1,0:T(8,128)S(1)} fusion(f32[2,64,1024]{2,1,0:T(8,128)S(1)} %get-tuple-element.12, f32[2,16,1024]{2,1,0:T(8,128)S(1)} %get-tuple-element.17, f32[2,16,1024]{2,1,0:T(8,128)S(1)} %get-tuple-element.18, f32[2,64,1024]{2,1,0:T(8,128)S(1)} %get-tuple-element.10, f32[2,16,1024]{2,1,0:T(8,128)S(1)} %get-tuple-element.19, ...), kind=kLoop, calls=%fused_computation.26 | loop fusion | flops 90144768 | bytes 3276800 | tf_op jit(solution)/shard_map/reduce_sum | solution.py:73
  47.0 0.8 %fusion.31 = f32[32,512]{1,0:T(8,128)S(1)} fusion(s32[2,1024]{1,0:T(2,128)S(1)} %sub.147, bf16[2,16,1024]{2,1,0:T(8,128)(2,1)S(1)} %get-tuple-element.21, bf16[2,16,1024]{2,1,0:T(8,128)(2,1)S(1)} %get-tuple-element.20), kind=kOutput, calls=%fused_computation.43 | convolution fusion | flops 68419584 | bytes 204800 | tf_op jit(solution)/shard_map/pks,pgs->kg/dot_general | solution.py:160
  47.9 0.5 fusion.27
  48.4 0.2 copy.72
  48.6 0.2 all_to_all.16
  48.8 9.4 %all_to_all.19 = f32[32,1,512]{2,1,0:T(1,128)S(1)} all-to-all(f32[32,1,512]{2,1,0:T(1,128)S(1)} %all_to_all.16), channel_id=1, replica_groups=mesh['grp'=4,'dev'=8] {'grp','dev'}, dimensions={0} | all-to-all | bytes 131072 | tf_op jit(solution)/shard_map/all_to_all | solution.py:171
  58.3 0.6 %copy.89 = f32[16384]{0:T(1024)} copy(f32[16384]{0:T(1024)S(1)} %bitcast.105) | data formatting | bytes 131072
  (25 shorter events, 0.4 us)
Async XLA Ops:
  0.0 1.7 %copy-start.3 = (s32[512,2]{0,1:T(2,128)S(1)}, s32[512,2]{0,1:T(2,128)}, u32[]{:S(2)}) copy-start(s32[512,2]{0,1:T(2,128)} %param.11) | copy-start | bytes 12292
  1.0 1.3 %copy-start.4 = (s32[512,2]{0,1:T(2,128)S(1)}, s32[512,2]{0,1:T(2,128)}, u32[]{:S(2)}) copy-start(s32[512,2]{0,1:T(2,128)} %param.12) | copy-start | bytes 12292
  4.8 9.4 %copy-start = (f32[3,8192]{1,0:T(4,128)S(1)}, f32[3,8192]{1,0:T(4,128)}, u32[]{:S(2)}) copy-start(f32[3,8192]{1,0:T(4,128)} %param.14) | copy-start | bytes 294916
  5.2 9.2 %copy-start.1 = (f32[3,512]{1,0:T(4,128)S(1)}, f32[3,512]{1,0:T(4,128)}, u32[]{:S(2)}) copy-start(f32[3,512]{1,0:T(4,128)} %param.13) | copy-start | bytes 18436
  6.6 8.3 %copy-start.2 = (f32[64,16]{0,1:T(8,128)S(1)}, f32[64,16]{0,1:T(8,128)}, u32[]{:S(2)}) copy-start(f32[64,16]{0,1:T(8,128)} %param.16) | copy-start | bytes 12292
  6.6 24.0 %all-to-all-start = ((f32[32,1,4224]{2,1,0:T(1,128)}), f32[32,1,4224]{2,1,0:T(1,128)S(1)}, u32[]{:S(2)}, u32[]{:S(2)}) async-start(f32[32,1,4224]{2,1,0:T(1,128)} %copy.63), calls=%async_computation | async-start | bytes 1081344 | tf_op jit(solution)/shard_map/all_to_all | solution.py:124
  14.1 1.3 %copy-start.5 = (s32[512,1]{0,1:T(1,128)S(1)}, s32[512,1]{0,1:T(1,128)}, u32[]{:S(2)}) copy-start(s32[512,1]{0,1:T(1,128)} %param.15) | copy-start | bytes 6148
  33.3 1.1 %copy-start.6 = (f32[64]{0:T(128)S(1)}, f32[64]{0:T(128)}, u32[]{:S(2)}) copy-start(f32[64]{0:T(128)} %param.17) | copy-start | bytes 772

commit v12 on v11

--- a/solution.py
+++ b/solution.py
@@ -112,13 +112,10 @@
     placed = jnp.dot(place, rhs, preferred_element_type=F32)
     payload = join3(placed[:, : 3 * width], 1)
     slot_ids = 16.0 * placed[:, 3 * width] + placed[:, 3 * width + 1]
-    outgoing = jnp.concatenate(
-        [
-            payload.reshape(devices, capacity * width),
-            slot_ids.reshape(devices, capacity),
-            jnp.zeros((devices, 2 * width - capacity), F32),
-        ],
-        axis=1,
+    outgoing = (
+        jnp.zeros((devices, capacity * width + 2 * width), F32)
+        .at[:, : capacity * width].set(payload.reshape(devices, capacity * width))
+        .at[:, capacity * width : capacity * width + capacity].set(slot_ids.reshape(devices, capacity))
     )
 
     incoming = lax.all_to_all(outgoing, ("grp", "dev"), split_axis=0, concat_axis=0, tiled=True)

time: 59.1 us -> 62 us (1.049)
  other arithmetic: 15.6 us -> 18.2 us
    another operation x6 -> x9, other arithmetic: 0.21 us -> 2.3 us
    scatter x0 -> x2, local copies, waits for them, and re-layouts: none -> 1.54 us  [per_device(): outgoing = jnp.zeros((devices, capacity * width + 2 * width), F32).at[:,...]
    all_to_all x1 -> x2, local copies, waits for them, and re-layouts: 1.36 us -> 0.11 us  [per_device(): lax.all_to_all(outgoing, ('grp', 'dev'), split_axis=0, concat_axis=0, til...]
    all_to_all x1 -> x2, other arithmetic: 1.28 us -> 2 us  [per_device(): lax.all_to_all(outgoing, ('grp', 'dev'), split_axis=0, concat_axis=0, til...]
    another operation x0 -> x2, local copies, waits for them, and re-layouts: none -> 0.69 us
where the time goes in v12:
time: 62 us; the launch traced here: 61.7 us
  other arithmetic  18.2 us (29%)
  waiting for transfers between devices  14.9 us (24%)
  blocking collectives  9.41 us (15%)
  starting transfers between devices  7.48 us (12%)
  matrix products  5.87 us (9%)
  local copies, waits for them, and re-layouts  5.42 us (9%)
    all_to_all x1, waiting for transfers between devices, per_device(): lax.all_to_all(outgoing, ('grp', 'dev'), split_axis=0, concat_axis=0, til...  14.9 us
    reduce_sum x1, other arithmetic, expansion_terms(): return jnp.sum(scale[:, :, None] * t_next, axis=1)  11.8 us
    all_to_all x1, blocking collectives, per_device(): lax.all_to_all(sending, ('grp', 'dev'), split_axis=0, concat_axis=0, tile...  9.41 us
    all_to_all x1, starting transfers between devices, per_device(): lax.all_to_all(outgoing, ('grp', 'dev'), split_axis=0, concat_axis=0, til...  7.48 us
    another operation x9, other arithmetic  2.3 us
    all_to_all x2, other arithmetic, per_device(): lax.all_to_all(outgoing, ('grp', 'dev'), split_axis=0, concat_axis=0, til...  2 us
    dot_general x1, matrix products, per_device(): placed = jnp.dot(place, rhs, preferred_element_type=F32)  1.87 us
    scatter x2, local copies, waits for them, and re-layouts, per_device(): outgoing = jnp.zeros((devices, capacity * width + 2 * width), F32).at[:,...  1.54 us
  transfers between devices with their start and end apart: 1, of which 1 were waited for; matrix products, arithmetic and copies ran while one was open for 3% of the time, Pallas kernels for 0%

profile of v12, /device:TPU:0, one launch (start us, length us, event | category | flops | bytes accessed | tf_op | source)
XLA Modules:
  0.0 61.7 jit_solution(12232859902821357577)
XLA Ops:
  0.0 0.0 copy-start.3
  0.0 0.6 %compare_reduce_fusion.1 = pred[]{:T(512)} fusion(), kind=kLoop, calls=%fused_computation.154 | loop fusion | flops 5 | bytes 1 | tf_op jit(solution)/shard_map/reduce.2
  0.6 0.7 %compare_reduce_fusion = pred[]{:T(512)} fusion(), kind=kLoop, calls=%fused_computation.153 | loop fusion | flops 7 | bytes 1 | tf_op jit(solution)/shard_map/reduce.3
  1.4 1.0 %pad_maximum_fusion = f32[4,8192]{1,0:T(4,128)S(1)} fusion(f32[1,8192]{1,0:T(1,128)} %bitcast.110, f32[3,8192]{1,0:T(4,128)} %param.13), kind=kLoop, calls=%fused_computation.96 | loop fusion | flops 32768 | bytes 262144 | tf_op jit(solution)/shard_map/concatenate | solution.py:99
  2.3 0.0 copy-start.4
  2.4 0.4 reshape.338
  2.7 0.3 copy.61
  3.1 0.0 copy-done.3
  3.1 0.5 fusion.30
  3.7 0.0 copy-done.4
  3.7 1.9 %fusion.20 = f32[2048,194]{0,1:T(8,128)S(1)} fusion(s32[1024]{0:T(1024)S(1)} %convert_add_fusion.1, bf16[1024,1]{0,1:T(2,128)(2,1)S(1)} %fusion.82, bf16[1024,1]{0,1:T(2,128)(2,1)S(1)} %get-tuple-element.31, bf16[512,64]{0,1:T(8,128)(2,1)S(1)} %get-tuple-element.47, bf16[512,64]{0,1:T(8,128)(2,1)S(1)} %get-tuple-element.48, ...), kind=kOutput, calls=%fused_computation.29 | convolution fusion | flops 818970624 | bytes 1794048 | tf_op jit(solution)/shard_map/dot_general | solution.py:112
  5.6 0.7 %fusion.40 = f32[2048,64]{0,1:T(8,128)S(1)} fusion(f32[2048,194]{0,1:T(8,128)S(1)} %fusion.20, pred[]{:T(512)} %compare_reduce_fusion.1), kind=kLoop, calls=%fused_computation.61 | loop fusion | flops 393216 | bytes 2097153 | tf_op jit(solution)/shard_map/select.43
  6.4 0.3 copy.62
  6.7 0.0 copy-start
  6.7 0.4 reshape.340
  7.1 0.0 copy-start.1
  7.1 0.7 %fusion.81 = f32[2048]{0:T(1024)S(1)} fusion(pred[]{:T(512)} %compare_reduce_fusion, f32[2048,194]{0,1:T(8,128)S(1)} %fusion.20), kind=kLoop, calls=%fused_computation.137 | loop fusion | flops 6144 | bytes 24577 | tf_op jit(solution)/shard_map/all_to_all | solution.py:121
  7.9 0.1 all_to_all.18
  7.9 0.2 scatter.9
  8.1 1.3 %copy.63 = f32[32,1,4224]{2,1,0:T(1,128)} copy(f32[32,1,4224]{2,0,1:T(8,128)S(1)} %scatter.9) | data formatting | bytes 1081344 | tf_op jit(solution)/shard_map/scatter | solution.py:118
  9.5 0.0 copy-start.2
  9.5 7.5 %all-to-all-start = ((f32[32,1,4224]{2,1,0:T(1,128)}), f32[32,1,4224]{2,1,0:T(1,128)S(1)}, u32[]{:S(2)}, u32[]{:S(2)}) async-start(f32[32,1,4224]{2,1,0:T(1,128)} %copy.63), calls=%async_computation | async-start | bytes 1081344 | tf_op jit(solution)/shard_map/all_to_all | solution.py:121
  17.0 0.0 copy-done
  17.0 0.0 copy-start.5
  17.0 0.3 reshape.343
  17.3 0.0 copy-done.1
  17.3 0.3 subtract_bitcast_fusion
  17.6 0.2 copy.70
  17.8 0.0 copy-done.2
  17.8 0.1 copy.67
  17.9 0.1 broadcast_multiply_fusion
  18.0 0.1 mul.359
  18.1 0.1 mul.360
  18.2 0.1 pad.14.clone
  18.2 0.0 copy-done.5
  18.2 0.3 fusion.32
  18.5 0.1 reduce-precision_convert_fusion.3
  18.6 14.9 %all-to-all-done = f32[32,1,4224]{2,1,0:T(1,128)S(1)} async-done(((f32[32,1,4224]{2,1,0:T(1,128)}), f32[32,1,4224]{2,1,0:T(1,128)S(1)}, u32[]{:S(2)}, u32[]{:S(2)}) %all-to-all-start) | async-done | bytes 540704 | tf_op jit(solution)/shard_map/all_to_all | solution.py:121
  33.5 1.3 %reduce.15 = f32[32,4224]{1,0:T(8,128)S(1)} reduce(f32[32,1,4224]{2,1,0:T(1,128)S(1)} %all-to-all-done, f32[]{:T(128)} %constant.134), dimensions={1}, to_apply=%all_to_all.19.reduce_sub_computation | reduce | bytes 1081348 | tf_op jit(solution)/shard_map/all_to_all | solution.py:121
  34.8 0.1 reshape.341
  34.9 0.1 slice.108
  35.0 0.1 copy.65
  35.0 0.1 copy.66
  35.1 0.1 sub.147
  35.2 0.9 %fusion.28 = f32[2,112,1024]{2,1,0:T(8,128)S(1)} fusion(s32[2,1024]{1,0:T(2,128)S(1)} %sub.147, bf16[56,512]{1,0:T(8,128)(2,1)S(1)} %get-tuple-element.50, bf16[56,512]{1,0:T(8,128)(2,1)S(1)} %get-tuple-element.49), kind=kOutput, calls=%fused_computation.40 | convolution fusion | flops 236158976 | bytes 1040384 | tf_op jit(solution)/shard_map/fg,pgs->pfs/dot_general | solution.py:142
  36.1 0.1 slice_add_fusion.2
  36.2 0.0 copy-start.6
  36.3 1.0 %fusion.59 = f32[2,4,64,1024]{3,2,1,0:T(8,128)S(1)} fusion(f32[1024,128,1,1]{1,0,3,2:T(8,128)S(1)} %bitcast.101, f32[64,128]{1,0:T(8,128)S(1)} %copy.67, f32[2,4,128]{2,1,0:T(4,128)S(1)} %mul.360), kind=kOutput, calls=%fused_computation.84 | convolution fusion | flops 402718720 | bytes 2658304 | tf_op jit(solution)/shard_map/dot_general | solution.py:151
  37.3 0.0 copy-done.6
  37.3 0.3 fusion.39
  37.6 0.4 fusion.41
  38.1 11.8 %fusion.18 = f32[2,16,1024]{2,1,0:T(8,128)S(1)} fusion(f32[2,64,1024]{2,1,0:T(8,128)S(1)} %get-tuple-element.36, f32[2,16,1024]{2,1,0:T(8,128)S(1)} %get-tuple-element.41, f32[2,16,1024]{2,1,0:T(8,128)S(1)} %get-tuple-element.42, f32[2,64,1024]{2,1,0:T(8,128)S(1)} %get-tuple-element.34, f32[2,16,1024]{2,1,0:T(8,128)S(1)} %get-tuple-element.43, ...), kind=kLoop, calls=%fused_computation.26 | loop fusion | flops 90144768 | bytes 3276800 | tf_op jit(solution)/shard_map/reduce_sum | solution.py:73
  49.9 0.8 %fusion.31 = f32[32,512]{1,0:T(8,128)S(1)} fusion(s32[2,1024]{1,0:T(2,128)S(1)} %sub.147, bf16[2,16,1024]{2,1,0:T(8,128)(2,1)S(1)} %get-tuple-element.45, bf16[2,16,1024]{2,1,0:T(8,128)(2,1)S(1)} %get-tuple-element.44), kind=kOutput, calls=%fused_computation.43 | convolution fusion | flops 68419584 | bytes 204800 | tf_op jit(solution)/shard_map/pks,pgs->kg/dot_general | solution.py:157
  50.7 0.5 fusion.27
  51.2 0.2 copy.72
  51.4 0.2 all_to_all.22
  51.7 9.4 %all_to_all.28 = f32[32,1,512]{2,1,0:T(1,128)S(1)} all-to-all(f32[32,1,512]{2,1,0:T(1,128)S(1)} %all_to_all.22), channel_id=1, replica_groups=mesh['grp'=4,'dev'=8] {'grp','dev'}, dimensions={0} | all-to-all | bytes 131072 | tf_op jit(solution)/shard_map/all_to_all | solution.py:168
  61.1 0.6 %copy.90 = f32[16384]{0:T(1024)} copy(f32[16384]{0:T(1024)S(1)} %bitcast.105) | data formatting | bytes 131072
  (24 shorter events, 0.4 us)
Async XLA Ops:
  0.0 3.1 %copy-start.3 = (s32[512,2]{0,1:T(2,128)S(1)}, s32[512,2]{0,1:T(2,128)}, u32[]{:S(2)}) copy-start(s32[512,2]{0,1:T(2,128)} %param.15) | copy-start | bytes 12292
  2.3 1.3 %copy-start.4 = (s32[512,2]{0,1:T(2,128)S(1)}, s32[512,2]{0,1:T(2,128)}, u32[]{:S(2)}) copy-start(s32[512,2]{0,1:T(2,128)} %param.16) | copy-start | bytes 12292
  6.7 10.3 %copy-start = (f32[3,8192]{1,0:T(4,128)S(1)}, f32[3,8192]{1,0:T(4,128)}, u32[]{:S(2)}) copy-start(f32[3,8192]{1,0:T(4,128)} %param.18) | copy-start | bytes 294916
  7.1 10.2 %copy-start.1 = (f32[3,512]{1,0:T(4,128)S(1)}, f32[3,512]{1,0:T(4,128)}, u32[]{:S(2)}) copy-start(f32[3,512]{1,0:T(4,128)} %param.17) | copy-start | bytes 18436
  9.5 8.3 %copy-start.2 = (f32[64,16]{0,1:T(8,128)S(1)}, f32[64,16]{0,1:T(8,128)}, u32[]{:S(2)}) copy-start(f32[64,16]{0,1:T(8,128)} %param.20) | copy-start | bytes 12292
  9.5 24.0 %all-to-all-start = ((f32[32,1,4224]{2,1,0:T(1,128)}), f32[32,1,4224]{2,1,0:T(1,128)S(1)}, u32[]{:S(2)}, u32[]{:S(2)}) async-start(f32[32,1,4224]{2,1,0:T(1,128)} %copy.63), calls=%async_computation | async-start | bytes 1081344 | tf_op jit(solution)/shard_map/all_to_all | solution.py:121
  17.0 1.3 %copy-start.5 = (s32[512,1]{0,1:T(1,128)S(1)}, s32[512,1]{0,1:T(1,128)}, u32[]{:S(2)}) copy-start(s32[512,1]{0,1:T(1,128)} %param.19) | copy-start | bytes 6148
  36.2 1.1 %copy-start.6 = (f32[64]{0:T(128)S(1)}, f32[64]{0:T(128)}, u32[]{:S(2)}) copy-start(f32[64]{0:T(128)} %param.21) | copy-start | bytes 772

commit v13 on v11

--- a/solution.py
+++ b/solution.py
@@ -1,3 +1,5 @@
+import functools
+
 import jax
 import jax.numpy as jnp
 from jax import lax
@@ -101,17 +103,24 @@
         .transpose(1, 0, 2)
         .reshape(panels, width)
     )
-    coarse_parts = jnp.concatenate([split3(coarse, 1)] * fanout, axis=0)
-    ids1 = crevice_centre.T.reshape(pairs) + 1
-    id_parts = jnp.stack([ids1 // 16, ids1 % 16], axis=1).astype(BF)
-    rhs = jnp.concatenate([coarse_parts, id_parts], axis=1)
-
+    ids1 = crevice_centre.T + 1
     destination = crevice_routes.T.reshape(pairs)
     slot_index = destination * capacity + route_rank(destination, devices)
-    place = (jnp.arange(slots, dtype=jnp.int32)[:, None] == slot_index[None, :]).astype(BF)
+    slot_t = slot_index.reshape(fanout, panels)
+    extra = [ids1[t] // 16 for t in range(fanout)] + [ids1[t] % 16 for t in range(fanout)]
+    extra += [slot_t[t] // 64 for t in range(fanout)] + [slot_t[t] % 64 for t in range(fanout)]
+    rhs = jnp.concatenate([split3(coarse, 1), jnp.stack(extra, axis=1).astype(BF)], axis=1)
+    slot_iota = jnp.arange(slots, dtype=jnp.int32)[:, None]
+    place = functools.reduce(jnp.logical_or, [slot_iota == slot_t[t][None, :] for t in range(fanout)]).astype(BF)
     placed = jnp.dot(place, rhs, preferred_element_type=F32)
     payload = join3(placed[:, : 3 * width], 1)
-    slot_ids = 16.0 * placed[:, 3 * width] + placed[:, 3 * width + 1]
+    col = 3 * width
+    slot_here = jnp.arange(slots, dtype=F32)
+    slot_ids = jnp.zeros((slots,), F32)
+    for t in range(fanout):
+        id_t = 16.0 * placed[:, col + t] + placed[:, col + fanout + t]
+        slot_of_t = 64.0 * placed[:, col + 2 * fanout + t] + placed[:, col + 3 * fanout + t]
+        slot_ids = jnp.where(slot_of_t == slot_here, id_t, slot_ids)
     outgoing = jnp.concatenate(
         [
             payload.reshape(devices, capacity * width),

time: 59.1 us -> 60.3 us (1.020)
  local copies, waits for them, and re-layouts: 5.28 us -> 6.23 us
  other arithmetic: 15.6 us -> 16.4 us
  matrix products: 5.88 us -> 5.18 us
    add x1 -> x2, other arithmetic: 0.03 us -> 0.81 us  [the longest x1 0.69 us: per_device(): ids1 = crevice_centre.T + 1]
    dot_general x1, matrix products: 1.87 us -> 1.16 us  [per_device(): placed = jnp.dot(place, rhs, preferred_element_type=F32)]
    unnamed x19 -> x14, local copies, waits for them, and re-layouts: 0.7 us -> 1.37 us
where the time goes in v13:
time: 60.3 us; the launch traced here: 60 us
  other arithmetic  16.4 us (27%)
  waiting for transfers between devices  15 us (25%)
  blocking collectives  9.41 us (16%)
  starting transfers between devices  7.3 us (12%)
  local copies, waits for them, and re-layouts  6.23 us (10%)
  matrix products  5.18 us (9%)
    all_to_all x1, waiting for transfers between devices, per_device(): lax.all_to_all(outgoing, ('grp', 'dev'), split_axis=0, concat_axis=0, til...  15 us
    reduce_sum x1, other arithmetic, expansion_terms(): return jnp.sum(scale[:, :, None] * t_next, axis=1)  11.8 us
    all_to_all x1, blocking collectives, per_device(): lax.all_to_all(sending, ('grp', 'dev'), split_axis=0, concat_axis=0, tile...  9.41 us
    all_to_all x1, starting transfers between devices, per_device(): lax.all_to_all(outgoing, ('grp', 'dev'), split_axis=0, concat_axis=0, til...  7.3 us
    unnamed x14, local copies, waits for them, and re-layouts  1.37 us
    all_to_all x1, local copies, waits for them, and re-layouts, per_device(): lax.all_to_all(outgoing, ('grp', 'dev'), split_axis=0, concat_axis=0, til...  1.35 us
    all_to_all x1, other arithmetic, per_device(): lax.all_to_all(outgoing, ('grp', 'dev'), split_axis=0, concat_axis=0, til...  1.28 us
  transfers between devices with their start and end apart: 1, of which 1 were waited for; matrix products, arithmetic and copies ran while one was open for 3% of the time, Pallas kernels for 0%

profile of v13, /device:TPU:0, one launch (start us, length us, event | category | flops | bytes accessed | tf_op | source)
XLA Modules:
  0.0 60.0 jit_solution(14581714444856305815)
XLA Ops:
  0.0 0.7 %add_bitcast_fusion.1 = s32[2,512]{1,0:T(2,128)S(1)} fusion(s32[512,2]{0,1:T(2,128)} %param.12), kind=kLoop, calls=%fused_computation.148 | loop fusion | flops 1024 | bytes 8192 | tf_op jit(solution)/shard_map/add | solution.py:106
  0.8 0.7 %copy.80 = s32[1,4,2,128]{3,1,2,0:T(4,128)S(1)} copy(s32[1,4,2,128]{3,2,1,0:T(2,128)} %bitcast.124) | data formatting | bytes 8192
  1.5 0.5 fusion.33
  2.1 1.0 %pad_maximum_fusion = f32[4,8192]{1,0:T(4,128)S(1)} fusion(f32[1,8192]{1,0:T(1,128)} %bitcast.121, f32[3,8192]{1,0:T(4,128)} %param.9), kind=kLoop, calls=%fused_computation.82 | loop fusion | flops 32768 | bytes 262144 | tf_op jit(solution)/shard_map/concatenate | solution.py:101
  3.1 0.4 reshape.410
  3.5 0.3 copy.59
  3.8 0.1 concatenate.28
  3.9 1.2 %fusion.23 = f32[2048,200]{0,1:T(8,128)S(1)} fusion(bf16[512,200]{0,1:T(8,128)(2,1)S(1)} %concatenate.28, s32[512]{0:T(512)S(1)} %get-tuple-element.41, s32[512]{0:T(512)S(1)} %get-tuple-element.36), kind=kOutput, calls=%fused_computation.35 | convolution fusion | flops 422576128 | bytes 1847296 | tf_op jit(solution)/shard_map/dot_general | solution.py:115
  5.0 0.1 fusion.71
  5.2 0.1 slice_add_fusion
  5.2 0.1 add.234
  5.3 0.1 add.236
  5.4 0.1 add.238
  5.5 0.1 add.240
  5.5 0.3 copy.60
  5.9 0.0 copy-start
  5.9 0.4 reshape.412
  6.3 0.0 copy-start.1
  6.3 0.1 concatenate.29
  6.4 1.3 %copy.61 = f32[32,1,4224]{2,1,0:T(1,128)} copy(f32[32,1,4224]{2,0,1:T(8,128)S(1)} %bitcast.111) | data formatting | bytes 1081344 | tf_op jit(solution)/shard_map/all_to_all | solution.py:133
  7.7 0.0 copy-start.2
  7.7 7.3 %all-to-all-start = ((f32[32,1,4224]{2,1,0:T(1,128)}), f32[32,1,4224]{2,1,0:T(1,128)S(1)}, u32[]{:S(2)}, u32[]{:S(2)}) async-start(f32[32,1,4224]{2,1,0:T(1,128)} %copy.61), calls=%async_computation | async-start | bytes 1081344 | tf_op jit(solution)/shard_map/all_to_all | solution.py:133
  15.0 0.0 copy-done
  15.0 0.0 copy-start.3
  15.0 0.3 reshape.415
  15.3 0.0 copy-done.1
  15.3 0.3 subtract_bitcast_fusion
  15.6 0.2 copy.68
  15.8 0.0 copy-done.2
  15.9 0.1 copy.65
  16.0 0.1 broadcast_multiply_fusion
  16.0 0.1 mul.366
  16.1 0.1 mul.367
  16.2 0.1 pad.9.clone
  16.3 0.0 copy-done.3
  16.3 0.3 fusion.35
  16.6 0.1 reduce-precision_convert_fusion.3
  16.7 15.0 %all-to-all-done = f32[32,1,4224]{2,1,0:T(1,128)S(1)} async-done(((f32[32,1,4224]{2,1,0:T(1,128)}), f32[32,1,4224]{2,1,0:T(1,128)S(1)}, u32[]{:S(2)}, u32[]{:S(2)}) %all-to-all-start) | async-done | bytes 540704 | tf_op jit(solution)/shard_map/all_to_all | solution.py:133
  31.7 1.3 %reduce.4 = f32[32,4224]{1,0:T(8,128)S(1)} reduce(f32[32,1,4224]{2,1,0:T(1,128)S(1)} %all-to-all-done, f32[]{:T(128)} %constant.126), dimensions={1}, to_apply=%all_to_all.13.reduce_sub_computation | reduce | bytes 1081348 | tf_op jit(solution)/shard_map/all_to_all | solution.py:133
  33.0 0.1 reshape.413
  33.1 0.1 slice.131
  33.2 0.1 copy.63
  33.3 0.1 copy.64
  33.3 0.1 sub.162
  33.4 0.9 %fusion.31 = f32[2,112,1024]{2,1,0:T(8,128)S(1)} fusion(s32[2,1024]{1,0:T(2,128)S(1)} %sub.162, bf16[56,512]{1,0:T(8,128)(2,1)S(1)} %get-tuple-element.32, bf16[56,512]{1,0:T(8,128)(2,1)S(1)} %get-tuple-element.31), kind=kOutput, calls=%fused_computation.43 | convolution fusion | flops 236158976 | bytes 1040384 | tf_op jit(solution)/shard_map/fg,pgs->pfs/dot_general | solution.py:154
  34.3 0.1 slice_add_fusion.2
  34.4 0.0 copy-start.4
  34.5 1.0 %fusion.46 = f32[2,4,64,1024]{3,2,1,0:T(8,128)S(1)} fusion(f32[1024,128,1,1]{1,0,3,2:T(8,128)S(1)} %bitcast.112, f32[64,128]{1,0:T(8,128)S(1)} %copy.65, f32[2,4,128]{2,1,0:T(4,128)S(1)} %mul.367), kind=kOutput, calls=%fused_computation.70 | convolution fusion | flops 402718720 | bytes 2658304 | tf_op jit(solution)/shard_map/dot_general | solution.py:163
  35.5 0.0 copy-done.4
  35.5 0.3 fusion.42
  35.8 0.4 fusion.43
  36.3 11.8 %fusion.18 = f32[2,16,1024]{2,1,0:T(8,128)S(1)} fusion(f32[2,64,1024]{2,1,0:T(8,128)S(1)} %get-tuple-element.18, f32[2,16,1024]{2,1,0:T(8,128)S(1)} %get-tuple-element.23, f32[2,16,1024]{2,1,0:T(8,128)S(1)} %get-tuple-element.24, f32[2,64,1024]{2,1,0:T(8,128)S(1)} %get-tuple-element.16, f32[2,16,1024]{2,1,0:T(8,128)S(1)} %get-tuple-element.25, ...), kind=kLoop, calls=%fused_computation.26 | loop fusion | flops 90144768 | bytes 3276800 | tf_op jit(solution)/shard_map/reduce_sum | solution.py:75
  48.1 0.8 %fusion.34 = f32[32,512]{1,0:T(8,128)S(1)} fusion(s32[2,1024]{1,0:T(2,128)S(1)} %sub.162, bf16[2,16,1024]{2,1,0:T(8,128)(2,1)S(1)} %get-tuple-element.27, bf16[2,16,1024]{2,1,0:T(8,128)(2,1)S(1)} %get-tuple-element.26), kind=kOutput, calls=%fused_computation.46 | convolution fusion | flops 68419584 | bytes 204800 | tf_op jit(solution)/shard_map/pks,pgs->kg/dot_general | solution.py:169
  49.0 0.5 fusion.30
  49.5 0.2 copy.70
  49.7 0.2 all_to_all.16
  49.9 9.4 %all_to_all.19 = f32[32,1,512]{2,1,0:T(1,128)S(1)} all-to-all(f32[32,1,512]{2,1,0:T(1,128)S(1)} %all_to_all.16), channel_id=1, replica_groups=mesh['grp'=4,'dev'=8] {'grp','dev'}, dimensions={0} | all-to-all | bytes 131072 | tf_op jit(solution)/shard_map/all_to_all | solution.py:180
  59.3 0.6 %copy.86 = f32[16384]{0:T(1024)} copy(f32[16384]{0:T(1024)S(1)} %bitcast.116) | data formatting | bytes 131072
  (28 shorter events, 0.4 us)
Async XLA Ops:
  5.9 9.2 %copy-start = (f32[3,8192]{1,0:T(4,128)S(1)}, f32[3,8192]{1,0:T(4,128)}, u32[]{:S(2)}) copy-start(f32[3,8192]{1,0:T(4,128)} %param.14) | copy-start | bytes 294916
  6.3 9.1 %copy-start.1 = (f32[3,512]{1,0:T(4,128)S(1)}, f32[3,512]{1,0:T(4,128)}, u32[]{:S(2)}) copy-start(f32[3,512]{1,0:T(4,128)} %param.13) | copy-start | bytes 18436
  7.7 8.1 %copy-start.2 = (f32[64,16]{0,1:T(8,128)S(1)}, f32[64,16]{0,1:T(8,128)}, u32[]{:S(2)}) copy-start(f32[64,16]{0,1:T(8,128)} %param.16) | copy-start | bytes 12292
  7.7 24.0 %all-to-all-start = ((f32[32,1,4224]{2,1,0:T(1,128)}), f32[32,1,4224]{2,1,0:T(1,128)S(1)}, u32[]{:S(2)}, u32[]{:S(2)}) async-start(f32[32,1,4224]{2,1,0:T(1,128)} %copy.61), calls=%async_computation | async-start | bytes 1081344 | tf_op jit(solution)/shard_map/all_to_all | solution.py:133
  15.0 1.3 %copy-start.3 = (s32[512,1]{0,1:T(1,128)S(1)}, s32[512,1]{0,1:T(1,128)}, u32[]{:S(2)}) copy-start(s32[512,1]{0,1:T(1,128)} %param.15) | copy-start | bytes 6148
  34.4 1.1 %copy-start.4 = (f32[64]{0:T(128)S(1)}, f32[64]{0:T(128)}, u32[]{:S(2)}) copy-start(f32[64]{0:T(128)} %param.17) | copy-start | bytes 772

commit v14 on v13

--- a/solution.py
+++ b/solution.py
@@ -103,7 +103,7 @@
         .transpose(1, 0, 2)
         .reshape(panels, width)
     )
-    ids1 = crevice_centre.T + 1
+    ids1 = (crevice_centre.T.reshape(pairs) + 1).reshape(fanout, panels)
     destination = crevice_routes.T.reshape(pairs)
     slot_index = destination * capacity + route_rank(destination, devices)
     slot_t = slot_index.reshape(fanout, panels)

time: 60.3 us -> 59.6 us (0.988)
  other arithmetic: 16.4 us -> 15.7 us
    add x1, other arithmetic: 0.69 us -> 0.01 us  [per_device(): ids1 = (crevice_centre.T.reshape(pairs) + 1).reshape(fanout, panels)]
    unnamed x14 -> x16, local copies, waits for them, and re-layouts: 1.37 us -> 1.37 us
where the time goes in v14:
time: 59.6 us; the launch traced here: 59.3 us
  other arithmetic  15.7 us (26%)
  waiting for transfers between devices  15 us (25%)
  blocking collectives  9.41 us (16%)
  starting transfers between devices  7.3 us (12%)
  local copies, waits for them, and re-layouts  6.26 us (11%)
  matrix products  5.17 us (9%)
    all_to_all x1, waiting for transfers between devices, per_device(): lax.all_to_all(outgoing, ('grp', 'dev'), split_axis=0, concat_axis=0, til...  15 us
    reduce_sum x1, other arithmetic, expansion_terms(): return jnp.sum(scale[:, :, None] * t_next, axis=1)  11.8 us
    all_to_all x1, blocking collectives, per_device(): lax.all_to_all(sending, ('grp', 'dev'), split_axis=0, concat_axis=0, tile...  9.41 us
    all_to_all x1, starting transfers between devices, per_device(): lax.all_to_all(outgoing, ('grp', 'dev'), split_axis=0, concat_axis=0, til...  7.3 us
    unnamed x16, local copies, waits for them, and re-layouts  1.37 us
    all_to_all x1, local copies, waits for them, and re-layouts, per_device(): lax.all_to_all(outgoing, ('grp', 'dev'), split_axis=0, concat_axis=0, til...  1.35 us
    all_to_all x1, other arithmetic, per_device(): lax.all_to_all(outgoing, ('grp', 'dev'), split_axis=0, concat_axis=0, til...  1.28 us
  transfers between devices with their start and end apart: 1, of which 1 were waited for; matrix products, arithmetic and copies ran while one was open for 3% of the time, Pallas kernels for 0%

profile of v14, /device:TPU:0, one launch (start us, length us, event | category | flops | bytes accessed | tf_op | source)
XLA Modules:
  0.0 59.3 jit_solution(15684539252235744072)
XLA Ops:
  0.0 0.7 %copy.80 = s32[1,4,2,128]{3,1,2,0:T(4,128)S(1)} copy(s32[1,4,2,128]{3,2,1,0:T(2,128)} %bitcast.114) | data formatting | bytes 8192
  0.7 0.0 copy-start.3
  0.7 0.5 fusion.33
  1.3 1.0 %pad_maximum_fusion = f32[4,8192]{1,0:T(4,128)S(1)} fusion(f32[1,8192]{1,0:T(1,128)} %bitcast.109, f32[3,8192]{1,0:T(4,128)} %param.9), kind=kLoop, calls=%fused_computation.82 | loop fusion | flops 32768 | bytes 262144 | tf_op jit(solution)/shard_map/concatenate | solution.py:101
  2.3 0.4 reshape.216
  2.7 0.3 copy.59
  3.0 0.0 copy-done.3
  3.2 0.1 concatenate.28
  3.2 1.2 %fusion.23 = f32[2048,200]{0,1:T(8,128)S(1)} fusion(bf16[512,200]{0,1:T(8,128)(2,1)S(1)} %concatenate.28, s32[512]{0:T(512)S(1)} %get-tuple-element.37, s32[512]{0:T(512)S(1)} %get-tuple-element.32), kind=kOutput, calls=%fused_computation.35 | convolution fusion | flops 422576128 | bytes 1847296 | tf_op jit(solution)/shard_map/dot_general | solution.py:115
  4.4 0.1 fusion.71
  4.5 0.1 slice_add_fusion
  4.6 0.1 add.207
  4.7 0.1 add.209
  4.7 0.1 add.211
  4.8 0.1 add.213
  4.9 0.3 copy.60
  5.2 0.0 copy-start
  5.2 0.4 reshape.218
  5.6 0.0 copy-start.1
  5.6 0.1 concatenate.29
  5.7 1.3 %copy.61 = f32[32,1,4224]{2,1,0:T(1,128)} copy(f32[32,1,4224]{2,0,1:T(8,128)S(1)} %bitcast.99) | data formatting | bytes 1081344 | tf_op jit(solution)/shard_map/all_to_all | solution.py:133
  7.1 0.0 copy-start.2
  7.1 7.3 %all-to-all-start = ((f32[32,1,4224]{2,1,0:T(1,128)}), f32[32,1,4224]{2,1,0:T(1,128)S(1)}, u32[]{:S(2)}, u32[]{:S(2)}) async-start(f32[32,1,4224]{2,1,0:T(1,128)} %copy.61), calls=%async_computation | async-start | bytes 1081344 | tf_op jit(solution)/shard_map/all_to_all | solution.py:133
  14.4 0.0 copy-done
  14.4 0.0 copy-start.4
  14.4 0.3 reshape.221
  14.7 0.0 copy-done.1
  14.7 0.3 subtract_bitcast_fusion
  15.0 0.2 copy.68
  15.2 0.0 copy-done.2
  15.2 0.1 copy.65
  15.3 0.1 broadcast_multiply_fusion
  15.4 0.1 mul.366
  15.5 0.1 mul.367
  15.6 0.1 pad.9.clone
  15.6 0.0 copy-done.4
  15.7 0.3 fusion.35
  15.9 0.1 reduce-precision_convert_fusion.3
  16.0 15.0 %all-to-all-done = f32[32,1,4224]{2,1,0:T(1,128)S(1)} async-done(((f32[32,1,4224]{2,1,0:T(1,128)}), f32[32,1,4224]{2,1,0:T(1,128)S(1)}, u32[]{:S(2)}, u32[]{:S(2)}) %all-to-all-start) | async-done | bytes 540704 | tf_op jit(solution)/shard_map/all_to_all | solution.py:133
  31.1 1.3 %reduce.4 = f32[32,4224]{1,0:T(8,128)S(1)} reduce(f32[32,1,4224]{2,1,0:T(1,128)S(1)} %all-to-all-done, f32[]{:T(128)} %constant.126), dimensions={1}, to_apply=%all_to_all.13.reduce_sub_computation | reduce | bytes 1081348 | tf_op jit(solution)/shard_map/all_to_all | solution.py:133
  32.4 0.1 reshape.219
  32.5 0.1 slice.141
  32.5 0.1 copy.63
  32.6 0.1 copy.64
  32.7 0.1 sub.162
  32.8 0.9 %fusion.31 = f32[2,112,1024]{2,1,0:T(8,128)S(1)} fusion(s32[2,1024]{1,0:T(2,128)S(1)} %sub.162, bf16[56,512]{1,0:T(8,128)(2,1)S(1)} %get-tuple-element.28, bf16[56,512]{1,0:T(8,128)(2,1)S(1)} %get-tuple-element.27), kind=kOutput, calls=%fused_computation.43 | convolution fusion | flops 236158976 | bytes 1040384 | tf_op jit(solution)/shard_map/fg,pgs->pfs/dot_general | solution.py:154
  33.7 0.1 slice_add_fusion.2
  33.7 0.0 copy-start.5
  33.9 1.0 %fusion.46 = f32[2,4,64,1024]{3,2,1,0:T(8,128)S(1)} fusion(f32[1024,128,1,1]{1,0,3,2:T(8,128)S(1)} %bitcast.100, f32[64,128]{1,0:T(8,128)S(1)} %copy.65, f32[2,4,128]{2,1,0:T(4,128)S(1)} %mul.367), kind=kOutput, calls=%fused_computation.70 | convolution fusion | flops 402718720 | bytes 2658304 | tf_op jit(solution)/shard_map/dot_general | solution.py:163
  34.9 0.0 copy-done.5
  34.9 0.3 fusion.42
  35.2 0.4 fusion.43
  35.6 11.8 %fusion.18 = f32[2,16,1024]{2,1,0:T(8,128)S(1)} fusion(f32[2,64,1024]{2,1,0:T(8,128)S(1)} %get-tuple-element.14, f32[2,16,1024]{2,1,0:T(8,128)S(1)} %get-tuple-element.19, f32[2,16,1024]{2,1,0:T(8,128)S(1)} %get-tuple-element.20, f32[2,64,1024]{2,1,0:T(8,128)S(1)} %get-tuple-element.12, f32[2,16,1024]{2,1,0:T(8,128)S(1)} %get-tuple-element.21, ...), kind=kLoop, calls=%fused_computation.26 | loop fusion | flops 90144768 | bytes 3276800 | tf_op jit(solution)/shard_map/reduce_sum | solution.py:75
  47.5 0.8 %fusion.34 = f32[32,512]{1,0:T(8,128)S(1)} fusion(s32[2,1024]{1,0:T(2,128)S(1)} %sub.162, bf16[2,16,1024]{2,1,0:T(8,128)(2,1)S(1)} %get-tuple-element.23, bf16[2,16,1024]{2,1,0:T(8,128)(2,1)S(1)} %get-tuple-element.22), kind=kOutput, calls=%fused_computation.46 | convolution fusion | flops 68419584 | bytes 204800 | tf_op jit(solution)/shard_map/pks,pgs->kg/dot_general | solution.py:169
  48.3 0.5 fusion.30
  48.8 0.2 copy.70
  49.0 0.2 all_to_all.16
  49.3 9.4 %all_to_all.19 = f32[32,1,512]{2,1,0:T(1,128)S(1)} all-to-all(f32[32,1,512]{2,1,0:T(1,128)S(1)} %all_to_all.16), channel_id=1, replica_groups=mesh['grp'=4,'dev'=8] {'grp','dev'}, dimensions={0} | all-to-all | bytes 131072 | tf_op jit(solution)/shard_map/all_to_all | solution.py:180
  58.7 0.6 %copy.86 = f32[16384]{0:T(1024)} copy(f32[16384]{0:T(1024)S(1)} %bitcast.104) | data formatting | bytes 131072
  (33 shorter events, 0.4 us)
Async XLA Ops:
  0.7 2.3 %copy-start.3 = (s32[512,2]{0,1:T(2,128)S(1)}, s32[512,2]{0,1:T(2,128)}, u32[]{:S(2)}) copy-start(s32[512,2]{0,1:T(2,128)} %param.12) | copy-start | bytes 12292
  5.2 9.2 %copy-start = (f32[3,8192]{1,0:T(4,128)S(1)}, f32[3,8192]{1,0:T(4,128)}, u32[]{:S(2)}) copy-start(f32[3,8192]{1,0:T(4,128)} %param.14) | copy-start | bytes 294916
  5.6 9.1 %copy-start.1 = (f32[3,512]{1,0:T(4,128)S(1)}, f32[3,512]{1,0:T(4,128)}, u32[]{:S(2)}) copy-start(f32[3,512]{1,0:T(4,128)} %param.13) | copy-start | bytes 18436
  7.1 8.1 %copy-start.2 = (f32[64,16]{0,1:T(8,128)S(1)}, f32[64,16]{0,1:T(8,128)}, u32[]{:S(2)}) copy-start(f32[64,16]{0,1:T(8,128)} %param.16) | copy-start | bytes 12292
  7.1 24.0 %all-to-all-start = ((f32[32,1,4224]{2,1,0:T(1,128)}), f32[32,1,4224]{2,1,0:T(1,128)S(1)}, u32[]{:S(2)}, u32[]{:S(2)}) async-start(f32[32,1,4224]{2,1,0:T(1,128)} %copy.61), calls=%async_computation | async-start | bytes 1081344 | tf_op jit(solution)/shard_map/all_to_all | solution.py:133
  14.4 1.3 %copy-start.4 = (s32[512,1]{0,1:T(1,128)S(1)}, s32[512,1]{0,1:T(1,128)}, u32[]{:S(2)}) copy-start(s32[512,1]{0,1:T(1,128)} %param.15) | copy-start | bytes 6148
  33.7 1.1 %copy-start.5 = (f32[64]{0:T(128)S(1)}, f32[64]{0:T(128)}, u32[]{:S(2)}) copy-start(f32[64]{0:T(128)} %param.17) | copy-start | bytes 772

commit v15 on v11

--- a/solution.py
+++ b/solution.py
@@ -11,10 +11,16 @@
 
 def route_rank(destination, count):
     rows = destination.shape[0]
+    block = 128 if rows % 128 == 0 else rows
     onehot = (destination[:, None] == jnp.arange(count, dtype=jnp.int32)[None, :]).astype(BF)
-    lower = (jnp.arange(rows)[:, None] > jnp.arange(rows)[None, :]).astype(BF)
-    before = jnp.dot(lower, onehot, preferred_element_type=F32)
-    return jnp.sum(before * onehot.astype(F32), axis=1).astype(jnp.int32)
+    onehot = onehot.reshape(rows // block, block, count)
+    lower = (jnp.arange(block)[:, None] > jnp.arange(block)[None, :]).astype(BF)
+    within = jnp.einsum("ij,bjc->bic", lower, onehot, preferred_element_type=F32)
+    totals = jnp.sum(onehot.astype(F32), axis=1)
+    earlier = (jnp.arange(rows // block)[:, None] > jnp.arange(rows // block)[None, :]).astype(F32)
+    offsets = jnp.dot(earlier, totals, precision=HI)
+    before = within + offsets[:, None, :]
+    return jnp.sum(before * onehot.astype(F32), axis=2).reshape(rows).astype(jnp.int32)
 
 
 def split3(x, axis):

time: 59.1 us -> 59.1 us (level)
  no operation moved by 1% of the time
where the time goes in v15:
time: 59.1 us; the launch traced here: 58.8 us
  other arithmetic  15.8 us (27%)
  waiting for transfers between devices  14.7 us (25%)
  blocking collectives  9.41 us (16%)
  starting transfers between devices  7.48 us (13%)
  matrix products  5.7 us (10%)
  local copies, waits for them, and re-layouts  5.3 us (9%)
    all_to_all x1, waiting for transfers between devices, per_device(): lax.all_to_all(outgoing, ('grp', 'dev'), split_axis=0, concat_axis=0, til...  14.7 us
    reduce_sum x1, other arithmetic, expansion_terms(): return jnp.sum(scale[:, :, None] * t_next, axis=1)  11.8 us
    all_to_all x1, blocking collectives, per_device(): lax.all_to_all(sending, ('grp', 'dev'), split_axis=0, concat_axis=0, tile...  9.41 us
    all_to_all x1, starting transfers between devices, per_device(): lax.all_to_all(outgoing, ('grp', 'dev'), split_axis=0, concat_axis=0, til...  7.48 us
    dot_general x1, matrix products, per_device(): placed = jnp.dot(place, rhs, preferred_element_type=F32)  1.87 us
    all_to_all x1, local copies, waits for them, and re-layouts, per_device(): lax.all_to_all(outgoing, ('grp', 'dev'), split_axis=0, concat_axis=0, til...  1.35 us
    all_to_all x1, other arithmetic, per_device(): lax.all_to_all(outgoing, ('grp', 'dev'), split_axis=0, concat_axis=0, til...  1.28 us
  transfers between devices with their start and end apart: 1, of which 1 were waited for; matrix products, arithmetic and copies ran while one was open for 3% of the time, Pallas kernels for 0%

profile of v15, /device:TPU:0, one launch (start us, length us, event | category | flops | bytes accessed | tf_op | source)
XLA Modules:
  0.0 58.8 jit_solution(2587036908760274666)
XLA Ops:
  0.0 0.0 copy-start.2
  0.0 0.0 copy-start.5
  0.0 1.0 %pad_maximum_fusion = f32[4,8192]{1,0:T(4,128)S(1)} fusion(f32[1,8192]{1,0:T(1,128)} %bitcast.135, f32[3,8192]{1,0:T(4,128)} %param.9), kind=kLoop, calls=%fused_computation.96 | loop fusion | flops 32768 | bytes 262144 | tf_op jit(solution)/shard_map/concatenate | solution.py:105
  1.0 0.4 reshape.314
  1.4 0.3 copy.61
  1.7 0.0 copy-done.2
  1.8 0.1 convert_reduce_fusion
  1.9 0.1 fusion.87
  2.0 0.2 fusion.30
  2.2 0.0 copy-done.5
  2.3 1.9 %fusion.20 = f32[2048,194]{0,1:T(8,128)S(1)} fusion(s32[1024]{0:T(1024)S(1)} %bitcast_add_fusion, bf16[1024,1]{0,1:T(2,128)(2,1)S(1)} %fusion.86, bf16[1024,1]{0,1:T(2,128)(2,1)S(1)} %get-tuple-element.7, bf16[512,64]{0,1:T(8,128)(2,1)S(1)} %get-tuple-element.23, bf16[512,64]{0,1:T(8,128)(2,1)S(1)} %get-tuple-element.24, ...), kind=kOutput, calls=%fused_computation.29 | convolution fusion | flops 818970624 | bytes 1794048 | tf_op jit(solution)/shard_map/dot_general | solution.py:118
  4.2 0.1 slice_add_fusion
  4.3 0.3 copy.62
  4.7 0.0 copy-start
  4.7 0.4 reshape.316
  5.1 0.1 add.229
  5.1 0.0 copy-start.1
  5.1 0.1 concatenate.36
  5.2 0.0 copy-start.4
  5.2 1.3 %copy.63 = f32[32,1,4224]{2,1,0:T(1,128)} copy(f32[32,1,4224]{2,0,1:T(8,128)S(1)} %bitcast.125) | data formatting | bytes 1081344 | tf_op jit(solution)/shard_map/all_to_all | solution.py:130
  6.6 0.0 copy-start.3
  6.6 7.5 %all-to-all-start = ((f32[32,1,4224]{2,1,0:T(1,128)}), f32[32,1,4224]{2,1,0:T(1,128)S(1)}, u32[]{:S(2)}, u32[]{:S(2)}) async-start(f32[32,1,4224]{2,1,0:T(1,128)} %copy.63), calls=%async_computation | async-start | bytes 1081344 | tf_op jit(solution)/shard_map/all_to_all | solution.py:130
  14.1 0.0 copy-done
  14.1 0.3 reshape.319
  14.4 0.0 copy-done.1
  14.4 0.3 subtract_bitcast_fusion
  14.7 0.1 broadcast_multiply_fusion
  14.7 0.0 copy-done.4
  14.7 0.1 convert_reduce_fusion.1
  14.8 0.2 copy.70
  15.1 0.0 copy-done.3
  15.1 0.1 copy.67
  15.1 0.1 mul.364
  15.2 0.1 mul.365
  15.3 0.1 pad.9.clone
  15.4 0.1 fusion.89
  15.5 0.2 fusion.34
  15.8 0.1 reduce-precision_convert_fusion.3
  15.8 14.7 %all-to-all-done = f32[32,1,4224]{2,1,0:T(1,128)S(1)} async-done(((f32[32,1,4224]{2,1,0:T(1,128)}), f32[32,1,4224]{2,1,0:T(1,128)S(1)}, u32[]{:S(2)}, u32[]{:S(2)}) %all-to-all-start) | async-done | bytes 540704 | tf_op jit(solution)/shard_map/all_to_all | solution.py:130
  30.6 1.3 %reduce.1 = f32[32,4224]{1,0:T(8,128)S(1)} reduce(f32[32,1,4224]{2,1,0:T(1,128)S(1)} %all-to-all-done, f32[]{:T(128)} %constant.75), dimensions={1}, to_apply=%all_to_all.13.reduce_sub_computation | reduce | bytes 1081348 | tf_op jit(solution)/shard_map/all_to_all | solution.py:130
  31.8 0.1 reshape.317
  32.0 0.1 slice.75
  32.0 0.1 copy.65
  32.1 0.1 copy.66
  32.2 0.1 sub.147
  32.3 0.9 %fusion.27 = f32[2,112,1024]{2,1,0:T(8,128)S(1)} fusion(s32[2,1024]{1,0:T(2,128)S(1)} %sub.147, bf16[56,512]{1,0:T(8,128)(2,1)S(1)} %get-tuple-element.26, bf16[56,512]{1,0:T(8,128)(2,1)S(1)} %get-tuple-element.25), kind=kOutput, calls=%fused_computation.38 | convolution fusion | flops 236158976 | bytes 1040384 | tf_op jit(solution)/shard_map/fg,pgs->pfs/dot_general | solution.py:151
  33.2 0.1 slice_add_fusion.2
  33.2 0.0 copy-start.6
  33.4 1.0 %fusion.60 = f32[2,4,64,1024]{3,2,1,0:T(8,128)S(1)} fusion(f32[1024,128,1,1]{1,0,3,2:T(8,128)S(1)} %bitcast.126, f32[64,128]{1,0:T(8,128)S(1)} %copy.67, f32[2,4,128]{2,1,0:T(4,128)S(1)} %mul.365), kind=kOutput, calls=%fused_computation.83 | convolution fusion | flops 402718720 | bytes 2658304 | tf_op jit(solution)/shard_map/dot_general | solution.py:160
  34.4 0.0 copy-done.6
  34.4 0.3 fusion.41
  34.7 0.4 fusion.42
  35.1 11.8 %fusion.18 = f32[2,16,1024]{2,1,0:T(8,128)S(1)} fusion(f32[2,64,1024]{2,1,0:T(8,128)S(1)} %get-tuple-element.12, f32[2,16,1024]{2,1,0:T(8,128)S(1)} %get-tuple-element.17, f32[2,16,1024]{2,1,0:T(8,128)S(1)} %get-tuple-element.18, f32[2,64,1024]{2,1,0:T(8,128)S(1)} %get-tuple-element.10, f32[2,16,1024]{2,1,0:T(8,128)S(1)} %get-tuple-element.19, ...), kind=kLoop, calls=%fused_computation.26 | loop fusion | flops 90144768 | bytes 3276800 | tf_op jit(solution)/shard_map/reduce_sum | solution.py:79
  47.0 0.8 %fusion.31 = f32[32,512]{1,0:T(8,128)S(1)} fusion(s32[2,1024]{1,0:T(2,128)S(1)} %sub.147, bf16[2,16,1024]{2,1,0:T(8,128)(2,1)S(1)} %get-tuple-element.21, bf16[2,16,1024]{2,1,0:T(8,128)(2,1)S(1)} %get-tuple-element.20), kind=kOutput, calls=%fused_computation.43 | convolution fusion | flops 68419584 | bytes 204800 | tf_op jit(solution)/shard_map/pks,pgs->kg/dot_general | solution.py:166
  47.8 0.5 fusion.26
  48.3 0.2 copy.72
  48.5 0.2 all_to_all.16
  48.8 9.4 %all_to_all.19 = f32[32,1,512]{2,1,0:T(1,128)S(1)} all-to-all(f32[32,1,512]{2,1,0:T(1,128)S(1)} %all_to_all.16), channel_id=1, replica_groups=mesh['grp'=4,'dev'=8] {'grp','dev'}, dimensions={0} | all-to-all | bytes 131072 | tf_op jit(solution)/shard_map/all_to_all | solution.py:177
  58.2 0.6 %copy.89 = f32[16384]{0:T(1024)} copy(f32[16384]{0:T(1024)S(1)} %bitcast.130) | data formatting | bytes 131072
  (28 shorter events, 0.4 us)
Async XLA Ops:
  0.0 1.7 %copy-start.2 = (s32[512,2]{0,1:T(2,128)S(1)}, s32[512,2]{0,1:T(2,128)}, u32[]{:S(2)}) copy-start(s32[512,2]{0,1:T(2,128)} %param.11) | copy-start | bytes 12292
  0.0 2.2 %copy-start.5 = (s32[512,2]{0,1:T(2,128)S(1)}, s32[512,2]{0,1:T(2,128)}, u32[]{:S(2)}) copy-start(s32[512,2]{0,1:T(2,128)} %param.12) | copy-start | bytes 12292
  4.7 9.4 %copy-start = (f32[3,8192]{1,0:T(4,128)S(1)}, f32[3,8192]{1,0:T(4,128)}, u32[]{:S(2)}) copy-start(f32[3,8192]{1,0:T(4,128)} %param.14) | copy-start | bytes 294916
  5.1 9.2 %copy-start.1 = (f32[3,512]{1,0:T(4,128)S(1)}, f32[3,512]{1,0:T(4,128)}, u32[]{:S(2)}) copy-start(f32[3,512]{1,0:T(4,128)} %param.13) | copy-start | bytes 18436
  5.2 9.5 %copy-start.4 = (s32[512,1]{0,1:T(1,128)S(1)}, s32[512,1]{0,1:T(1,128)}, u32[]{:S(2)}) copy-start(s32[512,1]{0,1:T(1,128)} %param.15) | copy-start | bytes 6148
  6.6 8.5 %copy-start.3 = (f32[64,16]{0,1:T(8,128)S(1)}, f32[64,16]{0,1:T(8,128)}, u32[]{:S(2)}) copy-start(f32[64,16]{0,1:T(8,128)} %param.16) | copy-start | bytes 12292
  6.6 24.0 %all-to-all-start = ((f32[32,1,4224]{2,1,0:T(1,128)}), f32[32,1,4224]{2,1,0:T(1,128)S(1)}, u32[]{:S(2)}, u32[]{:S(2)}) async-start(f32[32,1,4224]{2,1,0:T(1,128)} %copy.63), calls=%async_computation | async-start | bytes 1081344 | tf_op jit(solution)/shard_map/all_to_all | solution.py:130
  33.2 1.1 %copy-start.6 = (f32[64]{0:T(128)S(1)}, f32[64]{0:T(128)}, u32[]{:S(2)}) copy-start(f32[64]{0:T(128)} %param.17) | copy-start | bytes 772
